TPU v7x, 32 devices: a whole 2x2x4 slice. The times are simulated.
32 devices in a mesh: batch: 4 (over z), seq: 8 (over y, x, core).
Axes of the slice: x: 2, y: 2, z: 4, core: 2. Of those that a mesh axis runs over, the one named last changes fastest.
Arguments:
- block_input: bfloat16 [16384, 768], P(('batch', 'seq')), may hold values from -6 to 6
- history: bfloat16 [8, 16384, 768], P(None, ('batch', 'seq')), may hold values from -6 to 6
- cotangent: bfloat16 [16384, 768], P(('batch', 'seq')), may hold values from -6 to 6
- qkv_weight: bfloat16 [768, 2304], P('batch', 'seq'), may hold values from -0.21875 to 0.21875
- proj_weight: bfloat16 [768, 768], P('batch', 'seq'), may hold values from -1.25 to 1.25
- up_weight: bfloat16 [768, 3072], P('batch', 'seq'), may hold values from -0.21875 to 0.21875
- down_weight: bfloat16 [3072, 768], P('batch', 'seq'), may hold values from -0.109375 to 0.109375
- norm1_gain: float32 [768], replicated, may hold values from 0.5 to 1.5
- norm1_bias: float32 [768], replicated, may hold values from -1.2 to 1.2
- norm2_gain: float32 [768], replicated, may hold values from 0.5 to 1.5
- norm2_bias: float32 [768], replicated, may hold values from -1.2 to 1.2
- dwa_weights: float32 [9], replicated, may hold values from 0.3 to 1
- pair_order: int32 [4, 24], P('batch'), may hold values from 0 to 23, each once within a row
- long_group: int32 [4, 2], P('batch'), may hold values from 0 to 2
Outputs:
- block_output: bfloat16 [16384, 768], P(('batch', 'seq'))
- input_grad: bfloat16 [16384, 768], P(('batch', 'seq'))
- history_grad: bfloat16 [8, 16384, 768], P(None, ('batch', 'seq'))
- row_lse: float32 [4, 24, 2048], P('batch', 'seq')
- qkv_grad: float32 [768, 2304], P('batch', 'seq')
- proj_grad: float32 [768, 768], P('batch', 'seq')
- up_grad: float32 [768, 3072], P('batch', 'seq')
- down_grad: float32 [3072, 768], P('batch', 'seq')
- norm1_gain_grad: float32 [768], replicated
- norm1_bias_grad: float32 [768], replicated
- norm2_gain_grad: float32 [768], replicated
- norm2_bias_grad: float32 [768], replicated
- dwa_grad: float32 [9], replicated
Inputs may be any that keep to these rules, and one draw needn't show every extreme that they name: `pair_order`: each row lists each of its group's 24 pairs once. `long_group`: an entry v: that slot holds 2^v sequences of 2048 // 2^v tokens.
All inputs are finite; a program needn't handle non-finite values.
Results may differ from a plain program's by a relative error of at most 0.017.
Values may be sent and summed in bfloat16 or wider, within the bound.
No kernel may reach another device: no remote copies, remote signals or barrier semaphores. Data moves between devices by JAX's collectives and lax.ppermute only.
A program may use at most 192 MiB of HBM per device.

v0:
```python
import jax
import jax.numpy as jnp
from jax import lax
from jax.sharding import PartitionSpec as P

D = 768
HEADS = 12
HD = 64
SLOT = 2048
HIST = 8


NORM_EPS = 1e-05
MASKED = -1e30


def norm_rows(values, gain, shift):
    row_mean = jnp.mean(values, axis=-1, keepdims=True)
    centred = values - row_mean
    variance = jnp.mean(centred * centred, axis=-1, keepdims=True)
    inv_std = lax.rsqrt(variance + NORM_EPS)
    normed = centred * inv_std
    return (normed * gain + shift, normed, inv_std)


def norm_back(grad_in, normed, inv_std, gain):
    scaled = grad_in * gain
    centred = (
        scaled
        - jnp.mean(scaled, axis=-1, keepdims=True)
        - normed * jnp.mean(scaled * normed, axis=-1, keepdims=True)
    )
    return (centred * inv_std, jnp.sum(grad_in * normed, axis=0), jnp.sum(grad_in, axis=0))


def rotate(values, cosine, sine_tab):
    half_size = values.shape[-1] // 2
    front = values[..., :half_size]
    behind = values[..., half_size:]
    cos_part = cosine[..., None, :]
    sin_part = sine_tab[..., None, :]
    return jnp.concatenate(
        [front * cos_part - behind * sin_part, behind * cos_part + front * sin_part], axis=-1
    )


def unrotate(values, cosine, sine_tab):
    half_size = values.shape[-1] // 2
    front = values[..., :half_size]
    behind = values[..., half_size:]
    cos_part = cosine[..., None, :]
    sin_part = sine_tab[..., None, :]
    return jnp.concatenate(
        [front * cos_part + behind * sin_part, behind * cos_part - front * sin_part], axis=-1
    )


def to_pairs(stacked, order_row, n_seq, per_dev):
    slot_count, piece_len, part_count, head_count, head_size = stacked.shape
    reordered = jnp.transpose(stacked, (0, 3, 2, 1, 4)).reshape(
        slot_count * head_count, part_count, piece_len * head_size
    )
    return jnp.take(reordered, order_row, axis=0).reshape(
        n_seq, per_dev, part_count, piece_len * head_size
    )


def pairs_whole(incoming, head_size):
    n_seq, per_dev, part_count, flat_len = incoming.shape
    piece_len = flat_len // head_size
    reordered = jnp.transpose(
        incoming.reshape(n_seq, per_dev, part_count, piece_len, head_size), (1, 2, 0, 3, 4)
    )
    return reordered.reshape(per_dev, part_count, n_seq * piece_len, head_size)


def pairs_split(whole_seq, n_seq):
    per_dev, part_count, seq_len, head_size = whole_seq.shape
    return jnp.transpose(
        whole_seq.reshape(per_dev, part_count, n_seq, seq_len // n_seq * head_size), (2, 0, 1, 3)
    )


def tokens_back(incoming, inverse, slot_count, head_size):
    n_seq, per_dev, part_count, flat_len = incoming.shape
    piece_len = flat_len // head_size
    ordered = jnp.take(incoming.reshape(n_seq * per_dev, part_count, flat_len), inverse, axis=0)
    head_count = n_seq * per_dev // slot_count
    return jnp.transpose(
        ordered.reshape(slot_count, head_count, part_count, piece_len, head_size), (0, 3, 2, 1, 4)
    )


def local(
    block_input,
    history,
    cotangent,
    qkv_weight,
    proj_weight,
    up_weight,
    down_weight,
    norm1_gain,
    norm1_bias,
    norm2_gain,
    norm2_bias,
    dwa_weights,
    pair_order,
    long_group,
):
    n_seq = lax.axis_size("seq")
    row_count = block_input.shape[0]
    piece_len = SLOT // n_seq
    slot_count = row_count // piece_len
    pair_count = slot_count * HEADS
    per_dev = pair_count // n_seq
    block_rows = min(512, SLOT)
    block_count = SLOT // block_rows
    score_scale = HD ** (-0.5)
    slot_flags = long_group[0]
    seg_len = SLOT // jnp.left_shift(jnp.ones_like(slot_flags), slot_flags)
    position = jnp.arange(SLOT, dtype=jnp.int32)
    segment_all = position[None, :] // seg_len[:, None]
    doc_place = (position[None, :] % seg_len[:, None]).astype(jnp.float32)
    frequency = jnp.power(10000.0, jnp.arange(HD // 2, dtype=jnp.float32) * (-2.0 / HD))
    angles = doc_place[..., None] * frequency
    my_index = lax.axis_index("seq")
    my_start = my_index * piece_len
    cosine = lax.dynamic_slice_in_dim(jnp.cos(angles), my_start, piece_len, 1)
    sine_tab = lax.dynamic_slice_in_dim(jnp.sin(angles), my_start, piece_len, 1)
    order_row = pair_order[0]
    inverse = (
        jnp.zeros((pair_count,), jnp.int32)
        .at[order_row]
        .set(jnp.arange(pair_count, dtype=jnp.int32))
    )
    held_pairs = lax.dynamic_slice_in_dim(order_row, my_index * per_dev, per_dev, 0)
    pair_segment = jnp.take(segment_all, held_pairs // HEADS, axis=0)
    row_parts = (
        lax.all_gather(qkv_weight, "batch", axis=0, tiled=True),
        lax.all_gather(proj_weight, "batch", axis=0, tiled=True),
        lax.all_gather(up_weight, "batch", axis=0, tiled=True),
        lax.all_gather(down_weight, "batch", axis=0, tiled=True),
    )
    w_qkv, w_proj, w_up, w_down = (
        lax.all_gather(row_parts[0], "seq", axis=1, tiled=True),
        lax.all_gather(row_parts[1], "seq", axis=1, tiled=True),
        lax.all_gather(row_parts[2], "seq", axis=1, tiled=True),
        lax.all_gather(row_parts[3], "seq", axis=1, tiled=True),
    )
    inputs32 = block_input.astype(jnp.float32)
    norm1_out, normed1, inv_std1 = norm_rows(inputs32, norm1_gain, norm1_bias)
    norm1_low = norm1_out.astype(jnp.bfloat16)
    qkv_out = jnp.dot(norm1_low, w_qkv, preferred_element_type=jnp.float32)
    queries = rotate(qkv_out[:, :D].reshape(slot_count, piece_len, HEADS, HD), cosine, sine_tab)
    keys_rot = rotate(
        qkv_out[:, D : 2 * D].reshape(slot_count, piece_len, HEADS, HD), cosine, sine_tab
    )
    values_in = qkv_out[:, 2 * D :].reshape(slot_count, piece_len, HEADS, HD)
    stacked = jnp.stack([queries, keys_rot, values_in], axis=2).astype(jnp.bfloat16)
    incoming = lax.all_to_all(
        to_pairs(stacked, order_row, n_seq, per_dev), "seq", split_axis=0, concat_axis=0, tiled=True
    )
    sequences = pairs_whole(incoming, HD)
    query_pairs = sequences[:, 0]
    key_pairs = sequences[:, 1]
    value_pairs = sequences[:, 2]

    def masked_scores(start_row, query_block):
        raw_scores = jnp.einsum(
            "pqd,pkd->pqk", query_block, key_pairs, preferred_element_type=jnp.float32
        )
        query_place = start_row + jnp.arange(block_rows, dtype=jnp.int32)
        query_seg = lax.dynamic_slice_in_dim(pair_segment, start_row, block_rows, 1)
        allowed = (position[None, None, :] <= query_place[None, :, None]) & (
            pair_segment[:, None, :] == query_seg[:, :, None]
        )
        return jnp.where(allowed, raw_scores * score_scale, MASKED)

    def forward_block(start_row):
        query_block = lax.dynamic_slice_in_dim(query_pairs, start_row, block_rows, 1)
        scores = masked_scores(start_row, query_block)
        row_top = jnp.max(scores, axis=-1, keepdims=True)
        weights_exp = jnp.exp(scores - row_top)
        row_total = jnp.sum(weights_exp, axis=-1, keepdims=True)
        probability = (weights_exp / row_total).astype(jnp.bfloat16)
        attn_block = jnp.einsum(
            "pqk,pkd->pqd", probability, value_pairs, preferred_element_type=jnp.float32
        ).astype(jnp.bfloat16)
        return (attn_block, row_top[..., 0] + jnp.log(row_total[..., 0]))

    starts = jnp.arange(block_count, dtype=jnp.int32) * block_rows
    attn_blocks, totals = lax.map(forward_block, starts)
    attended_pairs = jnp.transpose(attn_blocks, (1, 0, 2, 3)).reshape(per_dev, 1, SLOT, HD)
    log_total = jnp.transpose(totals, (1, 0, 2)).reshape(per_dev, SLOT)
    returned = lax.all_to_all(
        pairs_split(attended_pairs, n_seq), "seq", split_axis=0, concat_axis=0, tiled=True
    )
    attended = tokens_back(returned, inverse, slot_count, HD).reshape(row_count, D)
    middle = inputs32 + jnp.dot(attended, w_proj, preferred_element_type=jnp.float32)
    norm2_out, normed2, inv_std2 = norm_rows(middle, norm2_gain, norm2_bias)
    norm2_low = norm2_out.astype(jnp.bfloat16)
    hidden_up = jnp.dot(norm2_low, w_up, preferred_element_type=jnp.float32)
    gelu_out, gelu_pull = jax.vjp(lambda hidden: jax.nn.gelu(hidden, approximate=True), hidden_up)
    gelu_low = gelu_out.astype(jnp.bfloat16)
    block_out = middle + jnp.dot(gelu_low, w_down, preferred_element_type=jnp.float32)
    dwa_out = dwa_weights[HIST] * block_out
    for layer_idx in range(HIST):
        dwa_out = dwa_out + dwa_weights[layer_idx] * history[layer_idx].astype(jnp.float32)
    block_output = dwa_out.astype(jnp.bfloat16)
    grad_out = cotangent.astype(jnp.float32)
    history_grad = (dwa_weights[:HIST, None, None] * grad_out[None]).astype(jnp.bfloat16)
    dwa_terms = [
        jnp.sum(history[layer_idx].astype(jnp.float32) * grad_out) for layer_idx in range(HIST)
    ]
    dwa_terms.append(jnp.sum(block_out * grad_out))
    dwa_local = jnp.stack(dwa_terms)
    again_parts = (
        lax.all_gather(qkv_weight, "batch", axis=0, tiled=True),
        lax.all_gather(proj_weight, "batch", axis=0, tiled=True),
        lax.all_gather(up_weight, "batch", axis=0, tiled=True),
        lax.all_gather(down_weight, "batch", axis=0, tiled=True),
    )
    w_qkv, w_proj, w_up, w_down = (
        lax.all_gather(again_parts[0], "seq", axis=1, tiled=True),
        lax.all_gather(again_parts[1], "seq", axis=1, tiled=True),
        lax.all_gather(again_parts[2], "seq", axis=1, tiled=True),
        lax.all_gather(again_parts[3], "seq", axis=1, tiled=True),
    )
    dy_full = dwa_weights[HIST] * grad_out
    dmlp_low = dy_full.astype(jnp.bfloat16)
    down_local = jnp.einsum("nf,nd->fd", gelu_low, dmlp_low, preferred_element_type=jnp.float32)
    dgelu = jnp.einsum("nd,fd->nf", dmlp_low, w_down, preferred_element_type=jnp.float32)
    dup_low = gelu_pull(dgelu)[0].astype(jnp.bfloat16)
    up_local = jnp.einsum("nd,nf->df", norm2_low, dup_low, preferred_element_type=jnp.float32)
    dnorm2 = jnp.einsum("nf,df->nd", dup_low, w_up, preferred_element_type=jnp.float32)
    dmid_norm, gain2_local, bias2_local = norm_back(dnorm2, normed2, inv_std2, norm2_gain)
    dmiddle = dy_full + dmid_norm
    dmiddle_low = dmiddle.astype(jnp.bfloat16)
    proj_local = jnp.einsum("nd,ne->de", attended, dmiddle_low, preferred_element_type=jnp.float32)
    dattended = jnp.einsum(
        "ne,de->nd", dmiddle_low, w_proj, preferred_element_type=jnp.float32
    ).astype(jnp.bfloat16)
    dattn_tokens = dattended.reshape(slot_count, piece_len, 1, HEADS, HD)
    dattn_in = lax.all_to_all(
        to_pairs(dattn_tokens, order_row, n_seq, per_dev),
        "seq",
        split_axis=0,
        concat_axis=0,
        tiled=True,
    )
    dout_pairs = pairs_whole(dattn_in, HD)[:, 0]

    def backward_block(sums_carry, start_row):
        dkeys_sum, dvalues_sum = sums_carry
        query_block = lax.dynamic_slice_in_dim(query_pairs, start_row, block_rows, 1)
        dout_block = lax.dynamic_slice_in_dim(dout_pairs, start_row, block_rows, 1)
        total_block = lax.dynamic_slice_in_dim(log_total, start_row, block_rows, 1)
        probability = jnp.exp(masked_scores(start_row, query_block) - total_block[..., None])
        prob_low = probability.astype(jnp.bfloat16)
        dprob_full = jnp.einsum(
            "pqd,pkd->pqk", dout_block, value_pairs, preferred_element_type=jnp.float32
        )
        row_delta = jnp.sum(probability * dprob_full, axis=-1, keepdims=True)
        dscore = (probability * (dprob_full - row_delta) * score_scale).astype(jnp.bfloat16)
        dquery_block = jnp.einsum(
            "pqk,pkd->pqd", dscore, key_pairs, preferred_element_type=jnp.float32
        )
        dkeys_sum = dkeys_sum + jnp.einsum(
            "pqk,pqd->pkd", dscore, query_block, preferred_element_type=jnp.float32
        )
        dvalues_sum = dvalues_sum + jnp.einsum(
            "pqk,pqd->pkd", prob_low, dout_block, preferred_element_type=jnp.float32
        )
        return ((dkeys_sum, dvalues_sum), dquery_block)

    zero_pairs = jnp.zeros((per_dev, SLOT, HD), jnp.float32)
    (dkeys_sum, dvalues_sum), dquery_blocks = lax.scan(
        backward_block, (zero_pairs, zero_pairs), starts
    )
    dquery = jnp.transpose(dquery_blocks, (1, 0, 2, 3)).reshape(per_dev, SLOT, HD)
    dpairs = jnp.stack([dquery, dkeys_sum, dvalues_sum], axis=1).astype(jnp.bfloat16)
    dreturned = lax.all_to_all(
        pairs_split(dpairs, n_seq), "seq", split_axis=0, concat_axis=0, tiled=True
    )
    dtokens = tokens_back(dreturned, inverse, slot_count, HD)
    dq_rows = unrotate(dtokens[:, :, 0].astype(jnp.float32), cosine, sine_tab).reshape(row_count, D)
    dk_rows = unrotate(dtokens[:, :, 1].astype(jnp.float32), cosine, sine_tab).reshape(row_count, D)
    dv_rows = dtokens[:, :, 2].astype(jnp.float32).reshape(row_count, D)
    dqkv_low = jnp.concatenate([dq_rows, dk_rows, dv_rows], axis=-1).astype(jnp.bfloat16)
    qkv_local = jnp.einsum("nd,nf->df", norm1_low, dqkv_low, preferred_element_type=jnp.float32)
    dnorm1 = jnp.einsum("nf,df->nd", dqkv_low, w_qkv, preferred_element_type=jnp.float32)
    dinput_norm, gain1_local, bias1_local = norm_back(dnorm1, normed1, inv_std1, norm1_gain)
    input_grad = (dmiddle + dinput_norm).astype(jnp.bfloat16)
    col_sums = (
        lax.psum_scatter(
            qkv_local.astype(jnp.bfloat16), "seq", scatter_dimension=1, tiled=True
        ).astype(jnp.float32),
        lax.psum_scatter(
            proj_local.astype(jnp.bfloat16), "seq", scatter_dimension=1, tiled=True
        ).astype(jnp.float32),
        lax.psum_scatter(
            up_local.astype(jnp.bfloat16), "seq", scatter_dimension=1, tiled=True
        ).astype(jnp.float32),
        lax.psum_scatter(
            down_local.astype(jnp.bfloat16), "seq", scatter_dimension=1, tiled=True
        ).astype(jnp.float32),
    )
    qkv_grad, proj_grad, up_grad, down_grad = (
        lax.psum_scatter(
            col_sums[0].astype(jnp.bfloat16), "batch", scatter_dimension=0, tiled=True
        ).astype(jnp.float32),
        lax.psum_scatter(
            col_sums[1].astype(jnp.bfloat16), "batch", scatter_dimension=0, tiled=True
        ).astype(jnp.float32),
        lax.psum_scatter(
            col_sums[2].astype(jnp.bfloat16), "batch", scatter_dimension=0, tiled=True
        ).astype(jnp.float32),
        lax.psum_scatter(
            col_sums[3].astype(jnp.bfloat16), "batch", scatter_dimension=0, tiled=True
        ).astype(jnp.float32),
    )
    gain1_grad, bias1_grad, gain2_grad, bias2_grad, dwa_grad = lax.psum(
        (gain1_local, bias1_local, gain2_local, bias2_local, dwa_local), ("batch", "seq")
    )
    row_lse = log_total.reshape(1, per_dev, SLOT)
    return (
        block_output,
        input_grad,
        history_grad,
        row_lse,
        qkv_grad,
        proj_grad,
        up_grad,
        down_grad,
        gain1_grad,
        bias1_grad,
        gain2_grad,
        bias2_grad,
        dwa_grad,
    )


def solution(mesh):
    placed = (
        P(("batch", "seq"), None),
        P(None, ("batch", "seq"), None),
        P(("batch", "seq"), None),
        P("batch", "seq"),
        P("batch", "seq"),
        P("batch", "seq"),
        P("batch", "seq"),
        P(),
        P(),
        P(),
        P(),
        P(),
        P("batch", None),
        P("batch", None),
    )
    return jax.shard_map(
        local,
        mesh=mesh,
        in_specs=placed,
        out_specs=(
            P(("batch", "seq"), None),
            P(("batch", "seq"), None),
            P(None, ("batch", "seq"), None),
            P("batch", "seq", None),
            P("batch", "seq"),
            P("batch", "seq"),
            P("batch", "seq"),
            P("batch", "seq"),
            P(),
            P(),
            P(),
            P(),
            P(),
        ),
        check_vma=False,
    )
```

profile of v0, /device:TPU:0, one launch (start us, length us, event | category | flops | bytes accessed | tf_op | source)
XLA Modules:
  0.0 866.0 jit_solution(16337869639670817424)
XLA Ops:
  7.3 18.6 %all_gather.32 = bf16[768,288]{1,0:T(8,128)(2,1)S(1)} all-gather(bf16[192,288]{1,0:T(8,128)(2,1)} %param.25), channel_id=1, replica_groups=mesh['batch'=4,'seq'=8] {'batch'}, dimensions={0}, use_global_device_ids=true | all-gather | bytes 552960 | tf_op jit(solution)/shard_map/all_gather | solution.py:139
  27.0 13.8 %all_gather.34 = bf16[768,96]{1,0:T(8,128)(2,1)S(1)} all-gather(bf16[192,96]{1,0:T(8,128)(2,1)} %param.26), channel_id=1, replica_groups=mesh['batch'=4,'seq'=8] {'batch'}, dimensions={0}, use_global_device_ids=true | all-gather | bytes 184320 | tf_op jit(solution)/shard_map/all_gather | solution.py:140
  41.7 17.0 %all_gather.36 = bf16[768,384]{1,0:T(8,128)(2,1)} all-gather(bf16[192,384]{1,0:T(8,128)(2,1)S(1)} %copy-done.18), channel_id=1, replica_groups=mesh['batch'=4,'seq'=8] {'batch'}, dimensions={0}, use_global_device_ids=true | all-gather | bytes 737280 | tf_op jit(solution)/shard_map/all_gather | solution.py:141
  91.5 8.2 reshape.607
  99.6 6.8 gather_fusion.1
  116.0 17.4 %all_gather.38 = bf16[3072,96]{0,1:T(8,128)(2,1)} all-gather(bf16[768,96]{0,1:T(8,128)(2,1)S(1)} %copy-done.19), channel_id=1, replica_groups=mesh['batch'=4,'seq'=8] {'batch'}, dimensions={0}, use_global_device_ids=true | all-gather | bytes 737280 | tf_op jit(solution)/shard_map/all_gather | solution.py:142
  134.1 27.9 %all-to-all-done = bf16[8,3,3,16384]{3,1,2,0:T(4,128)(2,1)S(1)} async-done(((bf16[8,3,3,16384]{3,1,2,0:T(4,128)(2,1)}), bf16[8,3,3,16384]{3,1,2,0:T(4,128)(2,1)S(1)}, u32[]{:S(2)}, u32[]{:S(2)}) %all-to-all-start) | async-done | bytes 2359328 | tf_op jit(solution)/shard_map/all_to_all | solution.py:160
  165.2 7.4 reshape.515
  182.1 80.8 %while.28 = (s32[]{:T(128)}, bf16[4,3,512,64]{2,3,1,0:T(8,128)(2,1)}, f32[4,3,512]{2,1,0:T(4,128)S(1)}, s32[4]{0:T(128)S(1)}, s32[3,2048]{1,0:T(4,128)S(1)}, /*i...) while((s32[]{:T(128)}, ...), condition=%wide.region_5.7_spmd.clone, body=%wide.region_2.6_spmd.clone.sunk | while | flops 863075328 | bytes 44073140 | solution.py:192
  273.7 13.8 %all-to-all-done.1 = bf16[8,3,1,16384]{3,1,2,0:T(4,128)(2,1)S(1)} async-done(((bf16[8,3,1,16384]{3,1,2,0:T(4,128)(2,1)}), bf16[8,3,1,16384]{3,1,2,0:T(4,128)(2,1)S(1)}, u32[]{:S(2)}, u32[]{:S(2)}) %all-to-all-start.1) | async-done | bytes 786464 | tf_op jit(solution)/shard_map/all_to_all | solution.py:195
  298.1 7.1 fusion.111
  305.2 10.1 %fusion.58 = bf16[512,3072]{1,0:T(8,128)(2,1)S(1)} fusion(f32[512,3072]{1,0:T(8,128)} %fusion.111, bf16[3072,768]{0,1:T(8,128)(2,1)} %all-gather.11.cloned.1.call-done, bf16[512,768]{1,0:T(8,128)(2,1)S(1)} %copy-done.9, f32[]{:T(128)} %bitcast), kind=kOutput, calls=%fused_computation.65 | convolution fusion | flops 2448556032 | bytes 14942212 | tf_op jit(solution)/shard_map/nd,fd->nf/dot_general | solution.py:232
  318.9 15.2 %fusion.84 = (bf16[512,768]{1,0:T(8,128)(2,1)}, f32[512,768]{1,0:T(8,128)S(1)}) fusion(f32[]{:T(128)} %bitcast.39, f32[]{:T(128)} %bitcast.37, f32[]{:T(128)} %bitcast.35, f32[]{:T(128)} %bitcast.33, f32[]{:T(128)} %bitcast.31, f32[]{:T(128)} %bitcast.29, f32[]{:T(128)} %bitcast.27, f32[]{:T(128)} %bitcast.25, f32[]{:T(128)} %bitcast, ...), kind=kOutput, calls=%fused_computation.120 | convolution fusion | flops 2440691712 | bytes 21233700 | tf_op jit(solution)/shard_map/dot_general | solution.py:205
  341.3 6.4 convolution_convert_fusion.2
  347.7 6.7 copy.156
  374.8 8.8 %convolution_convert_fusion.1 = bf16[3072,768]{0,1:T(8,128)(2,1)} fusion(bf16[512,768]{1,0:T(8,128)(2,1)} %param.24, f32[]{:T(128)} %bitcast, f32[512,3072]{1,0:T(8,128)} %fusion.111), kind=kOutput, calls=%fused_computation.68 | convolution fusion | flops 2433613824 | bytes 11796484 | tf_op jit(solution)/shard_map/nf,nd->fd/dot_general | solution.py:231
  396.6 239.6 %while.29 = (s32[]{:T(128)}, f32[3,2048,64]{1,2,0:T(8,128)}, f32[3,2048,64]{1,2,0:T(8,128)S(1)}, bf16[4,3,512,64]{2,3,1,0:T(8,128)(2,1)}, s32[4]{0:T(128)S(1)}, ...) while((s32[]{:T(128)}, f32[3,2048,64]{1,2,0:T(8,128)}, ...), condition=%wide.region_13.16_spmd.clone, body=%wide.region_11.15_spmd.clone.sunk | while | flops 2066226688 | bytes 200737024 | solution.py:277
  417.8 18.6 %fusion.173 = bf16[4,3,512,64]{2,3,1,0:T(8,128)(2,1)} fusion(bf16[4,3,512,64]{2,3,1,0:T(8,128)(2,1)} %get-tuple-element.576, s32[]{:T(128)S(6)} %copy.183, bf16[3,2048,64]{1,2,0:T(8,128)(2,1)} %get-tuple-element.594, f32[3,512,2048]{2,1,0:T(8,128)} %copy-done, f32[3,512,2048]{2,1,0:T(8,128)} %fusion.170), kind=kOutput, calls=%fused_computation.39.clone.1 | convolution fusion | flops 418385408 | bytes 51511300 | tf_op jit(solution)/shard_map/while/body/eval_jaxpr/pqk,pkd->pqd/dot_general | solution.py:265
  436.4 22.0 %fusion.171 = f32[3,2048,64]{1,2,0:T(8,128)} fusion(f32[3,512,2048]{2,1,0:T(8,128)} %copy-done, f32[3,512,2048]{2,1,0:T(8,128)} %fusion.170, f32[3,2048,64]{1,2,0:T(8,128)} %get-tuple-element.574, pred[]{:T(512)S(6)} %compare.3, bf16[3,2048,64]{1,2,0:T(8,128)(2,1)} %get-tuple-element.593, s32[]{:T(128)S(6)} %select_n.227), kind=kOutput, calls=%fused_computation.37.clone.1 | convolution fusion | flops 419171840 | bytes 53673988 | tf_op jit(solution)/shard_map/while/body/eval_jaxpr/pqk,pqd->pkd/dot_general | solution.py:268
  479.4 18.5 %fusion.173 = bf16[4,3,512,64]{2,3,1,0:T(8,128)(2,1)} fusion(bf16[4,3,512,64]{2,3,1,0:T(8,128)(2,1)} %get-tuple-element.576, s32[]{:T(128)S(6)} %copy.183, bf16[3,2048,64]{1,2,0:T(8,128)(2,1)} %get-tuple-element.594, f32[3,512,2048]{2,1,0:T(8,128)} %copy-done, f32[3,512,2048]{2,1,0:T(8,128)} %fusion.170), kind=kOutput, calls=%fused_computation.39.clone.1 | convolution fusion | flops 418385408 | bytes 51511300 | tf_op jit(solution)/shard_map/while/body/eval_jaxpr/pqk,pkd->pqd/dot_general | solution.py:265
  497.9 20.1 %fusion.171 = f32[3,2048,64]{1,2,0:T(8,128)} fusion(f32[3,512,2048]{2,1,0:T(8,128)} %copy-done, f32[3,512,2048]{2,1,0:T(8,128)} %fusion.170, f32[3,2048,64]{1,2,0:T(8,128)} %get-tuple-element.574, pred[]{:T(512)S(6)} %compare.3, bf16[3,2048,64]{1,2,0:T(8,128)(2,1)} %get-tuple-element.593, s32[]{:T(128)S(6)} %select_n.227), kind=kOutput, calls=%fused_computation.37.clone.1 | convolution fusion | flops 419171840 | bytes 53673988 | tf_op jit(solution)/shard_map/while/body/eval_jaxpr/pqk,pqd->pkd/dot_general | solution.py:268
  539.0 17.9 %fusion.173 = bf16[4,3,512,64]{2,3,1,0:T(8,128)(2,1)} fusion(bf16[4,3,512,64]{2,3,1,0:T(8,128)(2,1)} %get-tuple-element.576, s32[]{:T(128)S(6)} %copy.183, bf16[3,2048,64]{1,2,0:T(8,128)(2,1)} %get-tuple-element.594, f32[3,512,2048]{2,1,0:T(8,128)} %copy-done, f32[3,512,2048]{2,1,0:T(8,128)} %fusion.170), kind=kOutput, calls=%fused_computation.39.clone.1 | convolution fusion | flops 418385408 | bytes 51511300 | tf_op jit(solution)/shard_map/while/body/eval_jaxpr/pqk,pkd->pqd/dot_general | solution.py:265
  556.9 20.1 %fusion.171 = f32[3,2048,64]{1,2,0:T(8,128)} fusion(f32[3,512,2048]{2,1,0:T(8,128)} %copy-done, f32[3,512,2048]{2,1,0:T(8,128)} %fusion.170, f32[3,2048,64]{1,2,0:T(8,128)} %get-tuple-element.574, pred[]{:T(512)S(6)} %compare.3, bf16[3,2048,64]{1,2,0:T(8,128)(2,1)} %get-tuple-element.593, s32[]{:T(128)S(6)} %select_n.227), kind=kOutput, calls=%fused_computation.37.clone.1 | convolution fusion | flops 419171840 | bytes 53673988 | tf_op jit(solution)/shard_map/while/body/eval_jaxpr/pqk,pqd->pkd/dot_general | solution.py:268
  598.1 17.9 %fusion.173 = bf16[4,3,512,64]{2,3,1,0:T(8,128)(2,1)} fusion(bf16[4,3,512,64]{2,3,1,0:T(8,128)(2,1)} %get-tuple-element.576, s32[]{:T(128)S(6)} %copy.183, bf16[3,2048,64]{1,2,0:T(8,128)(2,1)} %get-tuple-element.594, f32[3,512,2048]{2,1,0:T(8,128)} %copy-done, f32[3,512,2048]{2,1,0:T(8,128)} %fusion.170), kind=kOutput, calls=%fused_computation.39.clone.1 | convolution fusion | flops 418385408 | bytes 51511300 | tf_op jit(solution)/shard_map/while/body/eval_jaxpr/pqk,pkd->pqd/dot_general | solution.py:265
  616.0 20.0 %fusion.171 = f32[3,2048,64]{1,2,0:T(8,128)} fusion(f32[3,512,2048]{2,1,0:T(8,128)} %copy-done, f32[3,512,2048]{2,1,0:T(8,128)} %fusion.170, f32[3,2048,64]{1,2,0:T(8,128)} %get-tuple-element.574, pred[]{:T(512)S(6)} %compare.3, bf16[3,2048,64]{1,2,0:T(8,128)(2,1)} %get-tuple-element.593, s32[]{:T(128)S(6)} %select_n.227), kind=kOutput, calls=%fused_computation.37.clone.1 | convolution fusion | flops 419171840 | bytes 53673988 | tf_op jit(solution)/shard_map/while/body/eval_jaxpr/pqk,pqd->pkd/dot_general | solution.py:268
  663.1 35.9 %all-to-all-done.3 = bf16[8,3,3,16384]{3,1,2,0:T(4,128)(2,1)S(1)} async-done(((bf16[8,3,3,16384]{3,1,2,0:T(4,128)(2,1)}), bf16[8,3,3,16384]{3,1,2,0:T(4,128)(2,1)S(1)}, u32[]{:S(2)}, u32[]{:S(2)}) %all-to-all-start.3) | async-done | bytes 2359328 | tf_op jit(solution)/shard_map/all_to_all | solution.py:282
  703.1 7.2 gather_fusion.4
  713.4 8.4 reshape.610
  721.7 6.5 copy.142
  756.0 31.1 %reduce-scatter.15.cloned.1.call-done = bf16[768,288]{0,1:T(8,128)(2,1)} async-done(((bf16[768,2304]{0,1:T(8,128)(2,1)}), bf16[768,288]{0,1:T(8,128)(2,1)}) %reduce-scatter.15.cloned.1.call-update) | async-done | bytes 442384 | tf_op jit(solution)/shard_map/reduce_scatter | solution.py:295
  795.6 40.6 %all-reduce = (f32[768]{0:T(1024)}, f32[768]{0:T(1024)}, f32[768]{0:T(1024)}, f32[768]{0:T(1024)}, f32[9]{0:T(128)}) all-reduce(f32[768]{0:T(1024)S(1)} %get-tuple-element.307, f32[768]{0:T(1024)S(1)} %get-tuple-element.312, f32[768]{0:T(1024)S(1)} %copy-done.29, ...), channel_id=1, replica_groups=mesh['batch'=4,'seq'=8] {'batch','seq'}, use_global_device_ids=true, to_apply=%region_25.28 | all-reduce | flops 3081 | bytes 24648 | tf_op jit(solution)/shard_map/psum | solution.py:322
  842.3 14.9 %reduce-scatter.25.cloned.1.call-done = bf16[192,288]{1,0:T(8,128)(2,1)} async-done(((bf16[768,288]{1,0:T(8,128)(2,1)}), bf16[192,288]{1,0:T(8,128)(2,1)}) %reduce-scatter.25.cloned.1.call-update) | async-done | bytes 110608
  (331 shorter events, 349.4 us)
Async XLA Ops:
  7.2 34.5 %copy-start.18 = (bf16[192,384]{1,0:T(8,128)(2,1)S(1)}, bf16[192,384]{1,0:T(8,128)(2,1)}, u32[]{:S(2)}) copy-start(bf16[192,384]{1,0:T(8,128)(2,1)} %param.27) | copy-start | bytes 442372
  7.2 51.6 %copy-start.44 = (s32[1,2]{1,0:T(1,128)S(1)}, s32[1,2]{1,0:T(1,128)}, u32[]{:S(2)}) copy-start(s32[1,2]{1,0:T(1,128)} %param.35) | copy-start | bytes 28
  7.2 51.7 %copy-start.37 = (s32[1,24]{1,0:T(1,128)S(1)}, s32[1,24]{1,0:T(1,128)}, u32[]{:S(2)}) copy-start(s32[1,24]{1,0:T(1,128)} %param.34) | copy-start | bytes 292
  7.2 51.8 %copy-start.3 = (bf16[512,768]{1,0:T(8,128)(2,1)S(1)}, bf16[512,768]{1,0:T(8,128)(2,1)}, u32[]{:S(2)}) copy-start(bf16[512,768]{1,0:T(8,128)(2,1)} %param.22) | copy-start | bytes 2359300
  7.2 55.6 %all-gather.5.cloned.1.call-start = ((), (), s32[]{:S(2)}) async-start(), calls=%async_computation.12 | async-start | bytes 3981312 | tf_op jit(solution)/shard_map/all_gather | solution.py:145
  26.9 35.9 %copy-start.31 = (f32[768]{0:T(1024)S(1)}, f32[768]{0:T(1024)}, u32[]{:S(2)}) copy-start(f32[768]{0:T(1024)} %param.29) | copy-start | bytes 9220
  26.9 35.9 %copy-start.42 = (f32[768]{0:T(1024)S(1)}, f32[768]{0:T(1024)}, u32[]{:S(2)}) copy-start(f32[768]{0:T(1024)} %param.30) | copy-start | bytes 9220
  26.9 268.4 %all-gather.7.cloned.1.call-start = ((), (), s32[]{:S(2)}) async-start(), calls=%async_computation.13 | async-start | bytes 1327104 | tf_op jit(solution)/shard_map/all_gather | solution.py:146
  41.6 256.5 %all-gather.9.cloned.1.call-start = ((), (), s32[]{:S(2)}) async-start(), calls=%async_computation.14 | async-start | bytes 5308416 | tf_op jit(solution)/shard_map/all_gather | solution.py:147
  62.7 14.6 %copy-start.13 = (f32[2,256,32]{1,0,2:T(2,128)}, f32[2,256,32]{1,0,2:T(2,128)S(1)}, u32[]{:S(2)}) copy-start(f32[2,256,32]{1,0,2:T(2,128)S(1)} %get-tuple-element.381) | copy-start | bytes 196612
  62.7 14.6 %copy-start.15 = (f32[2,256,32]{1,0,2:T(2,128)}, f32[2,256,32]{1,0,2:T(2,128)S(1)}, u32[]{:S(2)}) copy-start(f32[2,256,32]{1,0,2:T(2,128)S(1)} %get-tuple-element.382) | copy-start | bytes 196612
  62.7 36.9 %copy-start.26 = (s32[1024]{0:T(1024)}, s32[1024]{0:T(1024)S(1)}, u32[]{:S(2)}) copy-start(s32[1024]{0:T(1024)S(1)} %get-tuple-element.404) | copy-start | bytes 12292
  62.7 43.7 %copy-start.33 = (pred[24]{0:T(512)(128)(4,1)}, pred[24]{0:T(512)(128)(4,1)S(1)}, u32[]{:S(2)}) copy-start(pred[24]{0:T(512)(128)(4,1)S(1)} %compare_and_fusion.1) | copy-start | bytes 76
  112.0 50.0 %all-to-all-start = ((bf16[8,3,3,16384]{3,1,2,0:T(4,128)(2,1)}), bf16[8,3,3,16384]{3,1,2,0:T(4,128)(2,1)S(1)}, u32[]{:S(2)}, u32[]{:S(2)}) async-start(bf16[8,3,3,16384]{3,1,2,0:T(4,128)(2,1)} %copy.121), calls=%async_computation | async-start | bytes 6291456 | tf_op jit(solution)/shard_map/all_to_all | solution.py:160
  115.9 189.3 %all-gather.11.cloned.1.call-start = ((), (), s32[]{:S(2)}) async-start(), calls=%async_computation.15 | async-start | bytes 5308416 | tf_op jit(solution)/shard_map/all_gather | solution.py:148
  268.6 18.9 %all-to-all-start.1 = ((bf16[8,3,1,16384]{3,1,2,0:T(4,128)(2,1)}), bf16[8,3,1,16384]{3,1,2,0:T(4,128)(2,1)S(1)}, u32[]{:S(2)}, u32[]{:S(2)}) async-start(bf16[8,3,1,16384]{3,1,2,0:T(4,128)(2,1)} %copy.127), calls=%async_computation.1 | async-start | bytes 2097152 | tf_op jit(solution)/shard_map/all_to_all | solution.py:195
  272.2 389.0 %reduce-scatter.17.cloned.1.call-start = ((), (), s32[]{:S(2)}) async-start(), calls=%async_computation.17 | async-start | bytes 1327104 | tf_op jit(solution)/shard_map/reduce_scatter | solution.py:298
  273.0 16.3 %copy-start.27 = (s32[1024]{0:T(1024)}, s32[1024]{0:T(1024)S(1)}, u32[]{:S(2)}) copy-start(s32[1024]{0:T(1024)S(1)} %pad_clamp_fusion) | copy-start | bytes 12292
  273.7 15.6 %copy-start.35 = (pred[24]{0:T(512)(128)(4,1)}, pred[24]{0:T(512)(128)(4,1)S(1)}, u32[]{:S(2)}) copy-start(pred[24]{0:T(512)(128)(4,1)S(1)} %compare_and_fusion) | copy-start | bytes 76
  318.9 15.2 %slice-start = ((s8[6291456]{0:T(1024)(128)(4,1)}), s8[4194304]{0:T(1024)(128)(4,1)S(1)}, s32[]{:S(2)}) async-start(s8[6291456]{0:T(1024)(128)(4,1)} %bitcast.246), calls=%async_computation.24 | async-start | bytes 8388608
  318.9 15.2 %slice-start.1 = ((s8[6291456]{0:T(1024)(128)(4,1)}), s8[2097152]{0:T(1024)(128)(4,1)S(1)}, s32[]{:S(2)}) async-start(s8[6291456]{0:T(1024)(128)(4,1)} %bitcast.246), calls=%async_computation.25 | async-start | bytes 4194304
  318.9 15.2 %copy-start.10 = (bf16[512,768]{1,0:T(8,128)(2,1)S(1)}, bf16[512,768]{1,0:T(8,128)(2,1)}, u32[]{:S(2)}) copy-start(bf16[512,768]{1,0:T(8,128)(2,1)} %param.24) | copy-start | bytes 2359300
  341.2 398.9 %reduce-scatter.29.cloned.1.call-start = ((), (), s32[]{:S(2)}) async-start(), calls=%async_computation.23 | async-start | bytes 5308416
  371.1 18.9 %all-to-all-start.2 = ((bf16[8,3,1,16384]{3,1,2,0:T(4,128)(2,1)}), bf16[8,3,1,16384]{3,1,2,0:T(4,128)(2,1)S(1)}, u32[]{:S(2)}, u32[]{:S(2)}) async-start(bf16[8,3,1,16384]{3,1,2,0:T(4,128)(2,1)} %bitcast.250), calls=%async_computation.2 | async-start | bytes 2097152 | tf_op jit(solution)/shard_map/all_to_all | solution.py:244
  374.7 367.7 %reduce-scatter.21.cloned.1.call-start = ((), (), s32[]{:S(2)}) async-start(), calls=%async_computation.19 | async-start | bytes 5308416 | tf_op jit(solution)/shard_map/reduce_scatter | solution.py:304
  657.5 41.4 %all-to-all-start.3 = ((bf16[8,3,3,16384]{3,1,2,0:T(4,128)(2,1)}), bf16[8,3,3,16384]{3,1,2,0:T(4,128)(2,1)S(1)}, u32[]{:S(2)}, u32[]{:S(2)}) async-start(bf16[8,3,3,16384]{3,1,2,0:T(4,128)(2,1)} %copy.138), calls=%async_computation.3 | async-start | bytes 6291456 | tf_op jit(solution)/shard_map/all_to_all | solution.py:282
  661.2 93.2 %reduce-scatter.27.cloned.1.call-start = ((), (), s32[]{:S(2)}) async-start(), calls=%async_computation.22 | async-start | bytes 245760
  663.0 124.1 %reduce-scatter.15.cloned.1.call-start = ((), (), s32[]{:S(2)}) async-start(), calls=%async_computation.16 | async-start | bytes 3981312 | tf_op jit(solution)/shard_map/reduce_scatter | solution.py:295
  740.0 98.9 %reduce-scatter.19.cloned.1.call-start = ((), (), s32[]{:S(2)}) async-start(), calls=%async_computation.18 | async-start | bytes 737280 | tf_op jit(solution)/shard_map/reduce_scatter | solution.py:315
  742.4 98.3 %reduce-scatter.23.cloned.1.call-start = ((), (), s32[]{:S(2)}) async-start(), calls=%async_computation.20 | async-start | bytes 737280 | tf_op jit(solution)/shard_map/reduce_scatter | solution.py:318
  743.1 114.1 %reduce-scatter.25.cloned.1.call-start = ((), (), s32[]{:S(2)}) async-start(), calls=%async_computation.21 | async-start | bytes 737280
  789.2 46.9 %copy-start.2 = (f32[512,768]{1,0:T(8,128)S(1)}, f32[512,768]{1,0:T(8,128)}, u32[]{:S(2)}) copy-start(f32[512,768]{1,0:T(8,128)} %copy-done.1) | copy-start | bytes 4718596
  (35 other events, 134.8 us)
Sparse Core Ops, SparseCore 0:
  27.0 35.0 all-gather.4
  64.5 23.9 all-gather.6
  90.4 47.9 all-gather.8
  140.1 55.6 all-gather.10
  341.4 35.5 reduce-scatter.16
  380.2 53.7 reduce-scatter.28
  437.5 53.7 reduce-scatter.20
  664.8 20.7 reduce-scatter.26
  740.2 46.8 reduce-scatter.14
  789.2 22.1 reduce-scatter.18
  813.7 20.7 reduce-scatter.22
  836.7 20.4 reduce-scatter.24
where the time goes:
time: 872 us; the launch traced here: 866 us
  matrix products  330 us (38%)
  local copies, waits for them, and re-layouts  179 us (21%)
  waiting for transfers between devices  131 us (15%)
  blocking collectives  107 us (12%)
  other arithmetic  72.2 us (8%)
  loops' own time  16.2 us (2%)
  between operations  15.5 us (2%)
  starting transfers between devices  15.3 us (2%)
    dot_general x4, matrix products, backward_block(): jnp.einsum('pqk,pqd->pkd', dscore, query_block, preferred_element_type=jn...  82.2 us
    dot_general x4, matrix products, backward_block(): jnp.einsum('pqk,pkd->pqd', dscore, key_pairs, preferred_element_type=jnp....  72.8 us
    dot_general x8, matrix products, masked_scores(): jnp.einsum('pqd,pkd->pqk', query_block, key_pairs, preferred_element_type...  46.4 us
    psum x1, blocking collectives, local(): lax.psum((gain1_local, bias1_local, gain2_local, bias2_local, dwa_local),...  40.6 us
    all_to_all x1, waiting for transfers between devices, local(): lax.all_to_all(pairs_split(dpairs, n_seq), 'seq', split_axis=0, concat_ax...  35.9 us
    reduce_scatter x1, waiting for transfers between devices, local(): lax.psum_scatter(qkv_local.astype(jnp.bfloat16), 'seq', scatter_dimension...  31.1 us
    unnamed x112, local copies, waits for them, and re-layouts  29.7 us
    all_to_all x1, waiting for transfers between devices, local(): lax.all_to_all(to_pairs(stacked, order_row, n_seq, per_dev), 'seq', split...  27.9 us
  transfers between devices with their start and end apart: 16, of which 6 were waited for; matrix products, arithmetic and copies ran while one was open for 61% of the time, Pallas kernels for 0%

commit v1 on v0

--- a/solution.py
+++ b/solution.py
@@ -2,6 +2,9 @@
 import jax.numpy as jnp
 from jax import lax
 from jax.sharding import PartitionSpec as P
+from jax.experimental import pallas as pl
+from jax.experimental.pallas import tpu as pltpu
+import functools
 
 D = 768
 HEADS = 12
@@ -12,6 +15,163 @@
 
 NORM_EPS = 1e-05
 MASKED = -1e30
+NT_DIMS = (((1,), (1,)), ((), ()))
+
+
+def fwd_kernel(seg_ref, q_ref, k_ref, v_ref, o_ref, lse_ref, *, bq, bk, scale):
+    pair = pl.program_id(0)
+    qi = pl.program_id(1)
+    seg_len = seg_ref[pair]
+    q_start = qi * bq
+    seg_start = (q_start // seg_len) * seg_len
+    query = q_ref[0, 0]
+
+    def step(j, carry, masked):
+        m_old, l_old, acc = carry
+        k_off = pl.multiple_of(j * bk, bk)
+        key = k_ref[0, 0, pl.ds(k_off, bk), :]
+        value = v_ref[0, 0, pl.ds(k_off, bk), :]
+        s = lax.dot_general(query, key, NT_DIMS, preferred_element_type=jnp.float32) * scale
+        if masked:
+            rows = q_start + lax.broadcasted_iota(jnp.int32, (bq, bk), 0)
+            cols = k_off + lax.broadcasted_iota(jnp.int32, (bq, bk), 1)
+            s = jnp.where(cols <= rows, s, MASKED)
+        m_new = jnp.maximum(m_old, jnp.max(s, axis=-1, keepdims=True))
+        alpha = jnp.exp(m_old - m_new)
+        weights = jnp.exp(s - m_new)
+        l_new = alpha * l_old + jnp.sum(weights, axis=-1, keepdims=True)
+        acc = alpha * acc + jnp.dot(
+            weights.astype(jnp.bfloat16), value, preferred_element_type=jnp.float32
+        )
+        return m_new, l_new, acc
+
+    carry = (
+        jnp.full((bq, 1), MASKED, jnp.float32),
+        jnp.zeros((bq, 1), jnp.float32),
+        jnp.zeros((bq, HD), jnp.float32),
+    )
+    j_diag = q_start // bk
+    carry = lax.fori_loop(
+        seg_start // bk, j_diag, lambda j, c: step(j, c, False), carry
+    )
+    for r in range(bq // bk):
+        carry = step(j_diag + r, carry, True)
+    m_fin, l_fin, acc = carry
+    o_ref[0] = (acc / l_fin).astype(o_ref.dtype)
+    lse = m_fin + jnp.log(l_fin)
+    lse_ref[0] = jnp.transpose(jnp.broadcast_to(lse, (bq, 128)))[0:1, :]
+
+
+def attn_forward(qkv, seg_pairs, bq=512, bk=256):
+    pairs, _, seq_len, head_size = qkv.shape
+    scale = head_size ** (-0.5)
+    n_q = seq_len // bq
+    blocks_done = pairs * (seq_len // bk) * (seq_len // bk + 1) // 2
+    cost = pl.CostEstimate(
+        flops=4 * blocks_done * bk * bk * head_size,
+        transcendentals=blocks_done * bk * bk,
+        bytes_accessed=pairs * seq_len * head_size * 2 * 4 + pairs * seq_len * 4,
+    )
+    grid_spec = pltpu.PrefetchScalarGridSpec(
+        num_scalar_prefetch=1,
+        grid=(pairs, n_q),
+        in_specs=[
+            pl.BlockSpec((1, 1, bq, head_size), lambda p, i, seg: (p, 0, i, 0)),
+            pl.BlockSpec((1, 1, seq_len, head_size), lambda p, i, seg: (p, 1, 0, 0)),
+            pl.BlockSpec((1, 1, seq_len, head_size), lambda p, i, seg: (p, 2, 0, 0)),
+        ],
+        out_specs=[
+            pl.BlockSpec((1, bq, head_size), lambda p, i, seg: (p, i, 0)),
+            pl.BlockSpec((1, 1, bq), lambda p, i, seg: (p, 0, i)),
+        ],
+    )
+    return pl.pallas_call(
+        functools.partial(fwd_kernel, bq=bq, bk=bk, scale=scale),
+        grid_spec=grid_spec,
+        out_shape=[
+            jax.ShapeDtypeStruct((pairs, seq_len, head_size), jnp.bfloat16),
+            jax.ShapeDtypeStruct((pairs, 1, seq_len), jnp.float32),
+        ],
+        cost_estimate=cost,
+        name="attn_fwd",
+    )(seg_pairs, qkv, qkv, qkv)
+
+
+def bwd_kernel(seg_ref, q_ref, k_ref, v_ref, do_ref, lse_ref, dl_ref, out_ref, dq_acc, *, blk, scale):
+    pair = pl.program_id(0)
+    kj = pl.program_id(1)
+
+    @pl.when(kj == 0)
+    def _():
+        dq_acc[...] = jnp.zeros_like(dq_acc)
+
+    seg_len = seg_ref[pair]
+    k_start = kj * blk
+    seg_end = (k_start // seg_len + 1) * seg_len
+    key = k_ref[0, 0]
+    value = v_ref[0, 0]
+
+    def step(i, carry, masked):
+        dk, dv = carry
+        q_off = pl.multiple_of(i * blk, blk)
+        query = q_ref[0, 0, pl.ds(q_off, blk), :]
+        dout = do_ref[0, pl.ds(q_off, blk), :]
+        lse = lse_ref[0, :, pl.ds(q_off, blk)]
+        delta = dl_ref[0, :, pl.ds(q_off, blk)]
+        s_t = lax.dot_general(key, query, NT_DIMS, preferred_element_type=jnp.float32) * scale
+        if masked:
+            keys_at = k_start + lax.broadcasted_iota(jnp.int32, (blk, blk), 0)
+            queries_at = q_off + lax.broadcasted_iota(jnp.int32, (blk, blk), 1)
+            s_t = jnp.where(keys_at <= queries_at, s_t, MASKED)
+        p_t = jnp.exp(s_t - lse)
+        dv = dv + jnp.dot(p_t.astype(jnp.bfloat16), dout, preferred_element_type=jnp.float32)
+        dp_t = lax.dot_general(value, dout, NT_DIMS, preferred_element_type=jnp.float32)
+        ds_t = p_t * (dp_t - delta) * scale
+        dk = dk + jnp.dot(ds_t.astype(jnp.bfloat16), query, preferred_element_type=jnp.float32)
+        dq_acc[pl.ds(q_off, blk), :] += jnp.dot(
+            ds_t.T.astype(jnp.bfloat16), key, preferred_element_type=jnp.float32
+        )
+        return dk, dv
+
+    carry = (jnp.zeros((blk, HD), jnp.float32), jnp.zeros((blk, HD), jnp.float32))
+    carry = step(kj, carry, True)
+    dk, dv = lax.fori_loop(kj + 1, seg_end // blk, lambda i, c: step(i, c, False), carry)
+    out_ref[0, 0] = dq_acc[pl.ds(pl.multiple_of(k_start, blk), blk), :].astype(out_ref.dtype)
+    out_ref[0, 1] = dk.astype(out_ref.dtype)
+    out_ref[0, 2] = dv.astype(out_ref.dtype)
+
+
+def attn_backward(qkv, dout, lse, delta, seg_pairs, blk=256):
+    pairs, _, seq_len, head_size = qkv.shape
+    scale = head_size ** (-0.5)
+    n_k = seq_len // blk
+    blocks_done = pairs * n_k * (n_k + 1) // 2
+    cost = pl.CostEstimate(
+        flops=10 * blocks_done * blk * blk * head_size,
+        transcendentals=blocks_done * blk * blk,
+        bytes_accessed=pairs * seq_len * head_size * 2 * 7 + pairs * seq_len * 8,
+    )
+    grid_spec = pltpu.PrefetchScalarGridSpec(
+        num_scalar_prefetch=1,
+        grid=(pairs, n_k),
+        in_specs=[
+            pl.BlockSpec((1, 1, seq_len, head_size), lambda p, j, seg: (p, 0, 0, 0)),
+            pl.BlockSpec((1, 1, blk, head_size), lambda p, j, seg: (p, 1, j, 0)),
+            pl.BlockSpec((1, 1, blk, head_size), lambda p, j, seg: (p, 2, j, 0)),
+            pl.BlockSpec((1, seq_len, head_size), lambda p, j, seg: (p, 0, 0)),
+            pl.BlockSpec((1, 1, seq_len), lambda p, j, seg: (p, 0, 0)),
+            pl.BlockSpec((1, 1, seq_len), lambda p, j, seg: (p, 0, 0)),
+        ],
+        out_specs=pl.BlockSpec((1, 3, blk, head_size), lambda p, j, seg: (p, 0, j, 0)),
+        scratch_shapes=[pltpu.VMEM((seq_len, head_size), jnp.float32)],
+    )
+    return pl.pallas_call(
+        functools.partial(bwd_kernel, blk=blk, scale=scale),
+        grid_spec=grid_spec,
+        out_shape=jax.ShapeDtypeStruct((pairs, 3, seq_len, head_size), jnp.bfloat16),
+        cost_estimate=cost,
+        name="attn_bwd",
+    )(seg_pairs, qkv, qkv, qkv, dout, lse, delta)
 
 
 def norm_rows(values, gain, shift):
@@ -113,13 +273,9 @@
     slot_count = row_count // piece_len
     pair_count = slot_count * HEADS
     per_dev = pair_count // n_seq
-    block_rows = min(512, SLOT)
-    block_count = SLOT // block_rows
-    score_scale = HD ** (-0.5)
     slot_flags = long_group[0]
     seg_len = SLOT // jnp.left_shift(jnp.ones_like(slot_flags), slot_flags)
     position = jnp.arange(SLOT, dtype=jnp.int32)
-    segment_all = position[None, :] // seg_len[:, None]
     doc_place = (position[None, :] % seg_len[:, None]).astype(jnp.float32)
     frequency = jnp.power(10000.0, jnp.arange(HD // 2, dtype=jnp.float32) * (-2.0 / HD))
     angles = doc_place[..., None] * frequency
@@ -134,7 +290,6 @@
         .set(jnp.arange(pair_count, dtype=jnp.int32))
     )
     held_pairs = lax.dynamic_slice_in_dim(order_row, my_index * per_dev, per_dev, 0)
-    pair_segment = jnp.take(segment_all, held_pairs // HEADS, axis=0)
     row_parts = (
         lax.all_gather(qkv_weight, "batch", axis=0, tiled=True),
         lax.all_gather(proj_weight, "batch", axis=0, tiled=True),
@@ -161,37 +316,10 @@
         to_pairs(stacked, order_row, n_seq, per_dev), "seq", split_axis=0, concat_axis=0, tiled=True
     )
     sequences = pairs_whole(incoming, HD)
-    query_pairs = sequences[:, 0]
-    key_pairs = sequences[:, 1]
-    value_pairs = sequences[:, 2]
-
-    def masked_scores(start_row, query_block):
-        raw_scores = jnp.einsum(
-            "pqd,pkd->pqk", query_block, key_pairs, preferred_element_type=jnp.float32
-        )
-        query_place = start_row + jnp.arange(block_rows, dtype=jnp.int32)
-        query_seg = lax.dynamic_slice_in_dim(pair_segment, start_row, block_rows, 1)
-        allowed = (position[None, None, :] <= query_place[None, :, None]) & (
-            pair_segment[:, None, :] == query_seg[:, :, None]
-        )
-        return jnp.where(allowed, raw_scores * score_scale, MASKED)
-
-    def forward_block(start_row):
-        query_block = lax.dynamic_slice_in_dim(query_pairs, start_row, block_rows, 1)
-        scores = masked_scores(start_row, query_block)
-        row_top = jnp.max(scores, axis=-1, keepdims=True)
-        weights_exp = jnp.exp(scores - row_top)
-        row_total = jnp.sum(weights_exp, axis=-1, keepdims=True)
-        probability = (weights_exp / row_total).astype(jnp.bfloat16)
-        attn_block = jnp.einsum(
-            "pqk,pkd->pqd", probability, value_pairs, preferred_element_type=jnp.float32
-        ).astype(jnp.bfloat16)
-        return (attn_block, row_top[..., 0] + jnp.log(row_total[..., 0]))
-
-    starts = jnp.arange(block_count, dtype=jnp.int32) * block_rows
-    attn_blocks, totals = lax.map(forward_block, starts)
-    attended_pairs = jnp.transpose(attn_blocks, (1, 0, 2, 3)).reshape(per_dev, 1, SLOT, HD)
-    log_total = jnp.transpose(totals, (1, 0, 2)).reshape(per_dev, SLOT)
+    seg_pairs = jnp.take(seg_len, held_pairs // HEADS).astype(jnp.int32)
+    attn_out, lse_rows = attn_forward(sequences, seg_pairs)
+    attended_pairs = attn_out.reshape(per_dev, 1, SLOT, HD)
+    log_total = lse_rows.reshape(per_dev, SLOT)
     returned = lax.all_to_all(
         pairs_split(attended_pairs, n_seq), "seq", split_axis=0, concat_axis=0, tiled=True
     )
@@ -249,36 +377,10 @@
         tiled=True,
     )
     dout_pairs = pairs_whole(dattn_in, HD)[:, 0]
-
-    def backward_block(sums_carry, start_row):
-        dkeys_sum, dvalues_sum = sums_carry
-        query_block = lax.dynamic_slice_in_dim(query_pairs, start_row, block_rows, 1)
-        dout_block = lax.dynamic_slice_in_dim(dout_pairs, start_row, block_rows, 1)
-        total_block = lax.dynamic_slice_in_dim(log_total, start_row, block_rows, 1)
-        probability = jnp.exp(masked_scores(start_row, query_block) - total_block[..., None])
-        prob_low = probability.astype(jnp.bfloat16)
-        dprob_full = jnp.einsum(
-            "pqd,pkd->pqk", dout_block, value_pairs, preferred_element_type=jnp.float32
-        )
-        row_delta = jnp.sum(probability * dprob_full, axis=-1, keepdims=True)
-        dscore = (probability * (dprob_full - row_delta) * score_scale).astype(jnp.bfloat16)
-        dquery_block = jnp.einsum(
-            "pqk,pkd->pqd", dscore, key_pairs, preferred_element_type=jnp.float32
-        )
-        dkeys_sum = dkeys_sum + jnp.einsum(
-            "pqk,pqd->pkd", dscore, query_block, preferred_element_type=jnp.float32
-        )
-        dvalues_sum = dvalues_sum + jnp.einsum(
-            "pqk,pqd->pkd", prob_low, dout_block, preferred_element_type=jnp.float32
-        )
-        return ((dkeys_sum, dvalues_sum), dquery_block)
-
-    zero_pairs = jnp.zeros((per_dev, SLOT, HD), jnp.float32)
-    (dkeys_sum, dvalues_sum), dquery_blocks = lax.scan(
-        backward_block, (zero_pairs, zero_pairs), starts
-    )
-    dquery = jnp.transpose(dquery_blocks, (1, 0, 2, 3)).reshape(per_dev, SLOT, HD)
-    dpairs = jnp.stack([dquery, dkeys_sum, dvalues_sum], axis=1).astype(jnp.bfloat16)
+    delta = jnp.sum(
+        dout_pairs.astype(jnp.float32) * attn_out.astype(jnp.float32), axis=-1
+    ).reshape(per_dev, 1, SLOT)
+    dpairs = attn_backward(sequences, dout_pairs, lse_rows, delta, seg_pairs)
     dreturned = lax.all_to_all(
         pairs_split(dpairs, n_seq), "seq", split_axis=0, concat_axis=0, tiled=True
     )

time: 872 us -> 659 us (0.76)
  matrix products: 330 us -> 71 us
  Pallas kernels: 0 us -> 111 us
  local copies, waits for them, and re-layouts: 179 us -> 136 us
  other arithmetic: 72.2 us -> 42.5 us
  blocking collectives: 107 us -> 125 us
  loops' own time: 16.2 us -> 0 us
    dot_general x28 -> x0, matrix products: 256 us -> none  [the longest x4 82.2 us: backward_block(): jnp.einsum('pqk,pqd->pkd', dscore, query_block, preferred_element_type=jn...]
    pallas_call x0 -> x2, Pallas kernels: none -> 111 us  [the longest x1 77 us: attn_backward(): pl.pallas_call(functools.partial(bwd_kernel, blk=blk, scale=scale), grid_...]
    all_to_all x0 -> x1, blocking collectives: none -> 18.2 us  [local(): lax.all_to_all(to_pairs(dattn_tokens, order_row, n_seq, per_dev), 'seq',...]
    reduce_sum x4 -> x1, other arithmetic: 19.9 us -> 3.05 us  [local(): jnp.sum(dout_pairs.astype(jnp.float32) * attn_out.astype(jnp.float32), ax...]
    another operation x2 -> x0, loops' own time: 16.2 us -> none  [the longest x1 8.34 us: local(): lax.scan(backward_block, (zero_pairs, zero_pairs), starts)]
    while x8 -> x0, local copies, waits for them, and re-layouts: 12 us -> none
    another operation x6 -> x0, local copies, waits for them, and re-layouts: 11.9 us -> none  [the longest x3 7.88 us: local(): jnp.stack([dquery, dkeys_sum, dvalues_sum], axis=1).astype(jnp.bfloat16)]
    unnamed x112 -> x70, local copies, waits for them, and re-layouts: 29.7 us -> 20.2 us
  transfers between devices with their start and end apart: 16 -> 15, of which waited for: 6 -> 6; matrix products, arithmetic and copies ran while one was open for 61% -> 32% of each run, Pallas kernels for 0% -> 17%
where the time goes in v1:
time: 659 us; the launch traced here: 646 us
  local copies, waits for them, and re-layouts  136 us (21%)
  waiting for transfers between devices  133 us (20%)
  blocking collectives  125 us (19%)
  Pallas kernels  111 us (17%)
  matrix products  71 us (11%)
  other arithmetic  42.5 us (6%)
  between operations  15.2 us (2%)
  starting transfers between devices  12.5 us (2%)
    pallas_call x1, Pallas kernels, attn_backward(): pl.pallas_call(functools.partial(bwd_kernel, blk=blk, scale=scale), grid_...  77 us
    all_to_all x1, waiting for transfers between devices, local(): lax.all_to_all(pairs_split(dpairs, n_seq), 'seq', split_axis=0, concat_ax...  42.3 us
    psum x1, blocking collectives, local(): lax.psum((gain1_local, bias1_local, gain2_local, bias2_local, dwa_local),...  40.5 us
    pallas_call x1, Pallas kernels, attn_forward(): pl.pallas_call(functools.partial(fwd_kernel, bq=bq, bk=bk, scale=scale),...  33.8 us
    reduce_scatter x1, waiting for transfers between devices, local(): lax.psum_scatter(qkv_local.astype(jnp.bfloat16), 'seq', scatter_dimension...  30.8 us
    all_to_all x1, waiting for transfers between devices, local(): lax.all_to_all(to_pairs(stacked, order_row, n_seq, per_dev), 'seq', split...  29.9 us
    unnamed x70, local copies, waits for them, and re-layouts  20.2 us
    all_gather x1, blocking collectives, local(): lax.all_gather(qkv_weight, 'batch', axis=0, tiled=True)  18.6 us
  transfers between devices with their start and end apart: 15, of which 6 were waited for; matrix products, arithmetic and copies ran while one was open for 32% of the time, Pallas kernels for 17%

profile of v1, /device:TPU:0, one launch (start us, length us, event | category | flops | bytes accessed | tf_op | source)
XLA Modules:
  0.0 646.2 jit_solution(11147605986137018609)
XLA Ops:
  7.2 18.6 %all_gather.32 = bf16[768,288]{1,0:T(8,128)(2,1)S(1)} all-gather(bf16[192,288]{1,0:T(8,128)(2,1)} %param.21), channel_id=1, replica_groups=mesh['batch'=4,'seq'=8] {'batch'}, dimensions={0}, use_global_device_ids=true | all-gather | bytes 552960 | tf_op jit(solution)/shard_map/all_gather | solution.py:294
  26.9 13.7 %all_gather.34 = bf16[768,96]{1,0:T(8,128)(2,1)S(1)} all-gather(bf16[192,96]{1,0:T(8,128)(2,1)S(1)} %copy-done.16), channel_id=1, replica_groups=mesh['batch'=4,'seq'=8] {'batch'}, dimensions={0}, use_global_device_ids=true | all-gather | bytes 184320 | tf_op jit(solution)/shard_map/all_gather | solution.py:295
  41.5 17.1 %all_gather.36 = bf16[768,384]{1,0:T(8,128)(2,1)} all-gather(bf16[192,384]{1,0:T(8,128)(2,1)S(1)} %copy-done.13), channel_id=1, replica_groups=mesh['batch'=4,'seq'=8] {'batch'}, dimensions={0}, use_global_device_ids=true | all-gather | bytes 737280 | tf_op jit(solution)/shard_map/all_gather | solution.py:296
  87.2 5.2 copy.110
  92.4 8.2 %reshape.490 = bf16[24,3,16384]{2,1,0:T(4,128)(2,1)} reshape(bf16[2,12,3,256,64]{4,3,2,1,0:T(8,128)(2,1)} %copy.110) | data formatting | bytes 4718592 | tf_op jit(solution)/shard_map/reshape | solution.py:220
  100.6 6.9 %gather_fusion.1 = bf16[24,3,16384]{2,1,0:T(4,128)(2,1)S(1)} fusion(bf16[24,3,16384]{2,1,0:T(4,128)(2,1)} %reshape.490, s32[1024]{0:T(1024)S(1)} %get-tuple-element.145), kind=kCustom, calls=%fused_computation.clone | custom fusion | bytes 4718688 | tf_op jit(solution)/shard_map/jit(_take)/gather | solution.py:223
  116.9 17.2 %all_gather.38 = bf16[3072,96]{0,1:T(8,128)(2,1)} all-gather(bf16[768,96]{0,1:T(8,128)(2,1)S(1)} %copy-done.14), channel_id=1, replica_groups=mesh['batch'=4,'seq'=8] {'batch'}, dimensions={0}, use_global_device_ids=true | all-gather | bytes 737280 | tf_op jit(solution)/shard_map/all_gather | solution.py:297
  135.3 29.9 %all-to-all-done = bf16[8,3,3,16384]{3,1,2,0:T(4,128)(2,1)S(1)} async-done(((bf16[8,3,3,16384]{3,1,2,0:T(4,128)(2,1)}), bf16[8,3,3,16384]{3,1,2,0:T(4,128)(2,1)S(1)}, u32[]{:S(2)}, u32[]{:S(2)}) %all-to-all-start) | async-done | bytes 2359328 | tf_op jit(solution)/shard_map/all_to_all | solution.py:315
  168.4 7.5 %reshape.397 = bf16[8,3,3,256,64]{4,3,0,2,1:T(8,128)(2,1)} reshape(bf16[8,3,3,16384]{3,0,2,1:T(8,128)(2,1)} %copy.95) | data formatting | bytes 4718592 | tf_op jit(solution)/shard_map/reshape | solution.py:232
  175.8 33.8 %attn_fwd.1 = (bf16[3,2048,64]{2,1,0:T(8,128)(2,1)}, f32[3,1,2048]{2,1,0:T(1,128)}) custom-call(s32[3]{0:T(128)} %and_select_fusion.1.seg_ref, bf16[3,3,2048,64]{3,2,1,0:T(8,128)(2,1)} %bitcast.186, bf16[3,3,2048,64]{3,2,1,0:T(8,128)(2,1)} %bitcast.187, bf16[3,3,2048,64]{3,2,1,0:T(8,128)(2,1)} %bitcast.188), custom_call_target="tpu_custom_call" | custom-call | flops 1811939328 | bytes 3170304 | tf_op jit(solution)/shard_map/attn_fwd/pallas_call | solution.py:88
  218.8 13.9 %all-to-all-done.1 = bf16[8,3,1,16384]{3,1,2,0:T(4,128)(2,1)S(1)} async-done(((bf16[8,3,1,16384]{3,1,2,0:T(4,128)(2,1)}), bf16[8,3,1,16384]{3,1,2,0:T(4,128)(2,1)S(1)}, u32[]{:S(2)}, u32[]{:S(2)}) %all-to-all-start.1) | async-done | bytes 786464 | tf_op jit(solution)/shard_map/all_to_all | solution.py:323
  240.7 7.0 %fusion.59 = f32[512,3072]{1,0:T(8,128)} fusion(bf16[768,3072]{1,0:T(8,128)(2,1)} %all-gather.9.cloned.1.call-done, f32[512,768]{1,0:T(8,128)S(1)} %get-tuple-element.140, f32[768]{0:T(1024)S(1)} %copy-done.22, f32[768]{0:T(1024)S(1)} %copy-done.17, f32[512]{0:T(512)S(1)} %add_rsqrt_fusion, f32[512]{0:T(512)S(1)} %broadcast_multiply_fusion.5), kind=kOutput, calls=%fused_computation.153 | convolution fusion | flops 2417885184 | bytes 12593152 | tf_op jit(solution)/shard_map/dot_general | solution.py:330
  247.7 10.1 %fusion.6 = bf16[512,3072]{1,0:T(8,128)(2,1)S(1)} fusion(f32[512,3072]{1,0:T(8,128)} %fusion.59, bf16[3072,768]{0,1:T(8,128)(2,1)} %all-gather.11.cloned.1.call-done, bf16[512,768]{1,0:T(8,128)(2,1)S(1)} %copy-done.8, f32[]{:T(128)} %bitcast), kind=kOutput, calls=%fused_computation.15 | convolution fusion | flops 2448556032 | bytes 14942212 | tf_op jit(solution)/shard_map/nd,fd->nf/dot_general | solution.py:360
  261.3 15.0 %fusion.32 = (bf16[512,768]{1,0:T(8,128)(2,1)}, f32[512,768]{1,0:T(8,128)S(1)}) fusion(f32[]{:T(128)} %bitcast.34, f32[]{:T(128)} %bitcast.32, f32[]{:T(128)} %bitcast.30, f32[]{:T(128)} %bitcast.28, f32[]{:T(128)} %bitcast.26, f32[]{:T(128)} %bitcast.24, f32[]{:T(128)} %bitcast.22, f32[]{:T(128)} %bitcast.20, f32[]{:T(128)} %bitcast, ...), kind=kOutput, calls=%fused_computation.70 | convolution fusion | flops 2440691712 | bytes 21233700 | tf_op jit(solution)/shard_map/dot_general | solution.py:333
  282.1 6.4 convolution_convert_fusion.2
  288.6 6.7 %copy.120 = bf16[768,3072]{0,1:T(8,128)(2,1)} copy(bf16[768,3072]{1,0:T(8,128)(2,1)} %convolution_convert_fusion.2) | data formatting | bytes 9437184
  296.4 8.6 %convolution_convert_fusion.1 = bf16[3072,768]{0,1:T(8,128)(2,1)} fusion(bf16[512,768]{1,0:T(8,128)(2,1)S(1)} %copy-done.10, f32[]{:T(128)} %bitcast, f32[512,3072]{1,0:T(8,128)} %fusion.59), kind=kOutput, calls=%fused_computation.18 | convolution fusion | flops 2433613824 | bytes 11796484 | tf_op jit(solution)/shard_map/nf,nd->fd/dot_general | solution.py:359
  315.9 18.2 %all_to_all.20 = bf16[8,3,1,16384]{3,1,2,0:T(4,128)(2,1)S(1)} all-to-all(bf16[8,3,1,16384]{3,1,2,0:T(4,128)(2,1)S(1)} %bitcast.201), channel_id=1, replica_groups=mesh['batch'=4,'seq'=8] {'seq'}, dimensions={0} | all-to-all | bytes 1572864 | tf_op jit(solution)/shard_map/all_to_all | solution.py:372
  341.9 77.0 %attn_bwd.1 = bf16[3,3,2048,64]{3,2,1,0:T(8,128)(2,1)} custom-call(s32[3]{0:T(128)} %and_select_fusion.1.seg_ref, bf16[3,3,2048,64]{3,2,1,0:T(8,128)(2,1)} %bitcast.189, bf16[3,3,2048,64]{3,2,1,0:T(8,128)(2,1)} %bitcast.190, bf16[3,3,2048,64]{3,2,1,0:T(8,128)(2,1)} %bitcast.191, bf16[3,2048,64]{2,1,0:T(8,128)(2,1)} %bitcast.194, ...), custom_call_target="tpu_custom_call" | custom-call | flops 4529848320 | bytes 5554176 | tf_op jit(solution)/shard_map/attn_bwd/pallas_call | solution.py:168
  418.9 6.8 %reshape.407 = bf16[3,3,8,16384]{3,2,1,0:T(8,128)(2,1)} reshape(bf16[3,3,2048,64]{3,2,1,0:T(8,128)(2,1)} %attn_bwd.1) | data formatting | bytes 4718592 | tf_op jit(solution)/shard_map/reshape | solution.py:240
  425.7 5.4 copy.103
  437.4 42.3 %all-to-all-done.3 = bf16[8,3,3,16384]{3,2,1,0:T(4,128)(2,1)} async-done(((bf16[8,3,3,16384]{3,2,1,0:T(4,128)(2,1)}), bf16[8,3,3,16384]{3,2,1,0:T(4,128)(2,1)}, u32[]{:S(2)}, u32[]{:S(2)}) %all-to-all-start.3) | async-done | bytes 2359328 | tf_op jit(solution)/shard_map/all_to_all | solution.py:384
  479.7 7.5 %gather_fusion.4 = bf16[24,3,16384]{2,1,0:T(4,128)(2,1)} fusion(bf16[24,3,16384]{2,1,0:T(4,128)(2,1)} %bitcast.44, s32[1024]{0:T(1024)S(1)} %pad_clamp_fusion), kind=kCustom, calls=%fused_computation.2.clone | custom fusion | bytes 4718688 | tf_op jit(solution)/shard_map/jit(_take)/gather | solution.py:247
  487.2 5.0 broadcast_select_fusion
  492.2 8.4 %reshape.493 = bf16[2,12,3,256,64]{4,3,2,1,0:T(8,128)(2,1)} reshape(bf16[24,3,16384]{2,1,0:T(4,128)(2,1)} %broadcast_select_fusion) | data formatting | bytes 4718592 | tf_op jit(solution)/shard_map/reshape | solution.py:250
  500.6 7.6 %copy.107 = bf16[2,12,3,256,64]{3,0,4,1,2:T(2,128)(2,1)} copy(bf16[2,12,3,256,64]{4,3,2,1,0:T(8,128)(2,1)} %reshape.493) | data formatting | bytes 4718592 | tf_op jit(solution)/shard_map/reshape | solution.py:250
  524.5 4.6 multiply_convert_fusion
  529.1 5.9 stack.54
  536.6 30.8 %reduce-scatter.15.cloned.1.call-done = bf16[768,288]{0,1:T(8,128)(2,1)} async-done(((bf16[768,2304]{0,1:T(8,128)(2,1)}), bf16[768,288]{0,1:T(8,128)(2,1)}) %reduce-scatter.15.cloned.1.call-update) | async-done | bytes 442384 | tf_op jit(solution)/shard_map/reduce_scatter | solution.py:397
  569.5 6.2 fusion.22
  575.7 40.5 %all-reduce = (f32[768]{0:T(1024)}, f32[768]{0:T(1024)}, f32[768]{0:T(1024)}, f32[768]{0:T(1024)}, f32[9]{0:T(128)}) all-reduce(f32[768]{0:T(1024)S(1)} %get-tuple-element.94, f32[768]{0:T(1024)S(1)} %get-tuple-element.99, f32[768]{0:T(1024)S(1)} %get-tuple-element.92, ...), channel_id=1, replica_groups=mesh['batch'=4,'seq'=8] {'batch','seq'}, use_global_device_ids=true, to_apply=%region_19.22 | all-reduce | flops 3081 | bytes 24648 | tf_op jit(solution)/shard_map/psum | solution.py:424
  622.3 15.0 %reduce-scatter.25.cloned.1.call-done = bf16[192,288]{1,0:T(8,128)(2,1)} async-done(((bf16[768,288]{1,0:T(8,128)(2,1)}), bf16[192,288]{1,0:T(8,128)(2,1)}) %reduce-scatter.25.cloned.1.call-update) | async-done | bytes 110608
  (187 shorter events, 124.3 us)
Async XLA Ops:
  7.2 19.8 %copy-start.16 = (bf16[192,96]{1,0:T(8,128)(2,1)S(1)}, bf16[192,96]{1,0:T(8,128)(2,1)}, u32[]{:S(2)}) copy-start(bf16[192,96]{1,0:T(8,128)(2,1)} %param.22) | copy-start | bytes 110596
  7.2 34.4 %copy-start.13 = (bf16[192,384]{1,0:T(8,128)(2,1)S(1)}, bf16[192,384]{1,0:T(8,128)(2,1)}, u32[]{:S(2)}) copy-start(bf16[192,384]{1,0:T(8,128)(2,1)} %param.23) | copy-start | bytes 442372
  7.2 54.9 %all-gather.5.cloned.1.call-start = ((), (), s32[]{:S(2)}) async-start(), calls=%async_computation.12 | async-start | bytes 3981312 | tf_op jit(solution)/shard_map/all_gather | solution.py:300
  25.8 32.8 %copy-start.24 = (s32[1,2]{1,0:T(1,128)S(1)}, s32[1,2]{1,0:T(1,128)}, u32[]{:S(2)}) copy-start(s32[1,2]{1,0:T(1,128)} %param.31) | copy-start | bytes 28
  25.9 32.9 %copy-start.19 = (s32[1,24]{1,0:T(1,128)S(1)}, s32[1,24]{1,0:T(1,128)}, u32[]{:S(2)}) copy-start(s32[1,24]{1,0:T(1,128)} %param.30) | copy-start | bytes 292
  26.9 34.0 %copy-start.1 = (bf16[512,768]{1,0:T(8,128)(2,1)S(1)}, bf16[512,768]{1,0:T(8,128)(2,1)}, u32[]{:S(2)}) copy-start(bf16[512,768]{1,0:T(8,128)(2,1)} %param.18) | copy-start | bytes 2359300
  26.9 210.7 %all-gather.7.cloned.1.call-start = ((), (), s32[]{:S(2)}) async-start(), calls=%async_computation.13 | async-start | bytes 1327104 | tf_op jit(solution)/shard_map/all_gather | solution.py:301
  41.5 198.9 %all-gather.9.cloned.1.call-start = ((), (), s32[]{:S(2)}) async-start(), calls=%async_computation.14 | async-start | bytes 5308416 | tf_op jit(solution)/shard_map/all_gather | solution.py:302
  58.6 3.5 copy-start.18
  58.6 3.5 copy-start.23
  74.1 5.3 copy-start.4
  113.0 3.8 copy-start.14
  113.0 52.2 %all-to-all-start = ((bf16[8,3,3,16384]{3,1,2,0:T(4,128)(2,1)}), bf16[8,3,3,16384]{3,1,2,0:T(4,128)(2,1)S(1)}, u32[]{:S(2)}, u32[]{:S(2)}) async-start(bf16[8,3,3,16384]{3,1,2,0:T(4,128)(2,1)} %copy.94), calls=%async_computation | async-start | bytes 6291456 | tf_op jit(solution)/shard_map/all_to_all | solution.py:315
  116.8 130.9 %all-gather.11.cloned.1.call-start = ((), (), s32[]{:S(2)}) async-start(), calls=%async_computation.15 | async-start | bytes 5308416 | tf_op jit(solution)/shard_map/all_gather | solution.py:303
  212.2 6.0 copy-start.15
  213.8 18.9 %all-to-all-start.1 = ((bf16[8,3,1,16384]{3,1,2,0:T(4,128)(2,1)}), bf16[8,3,1,16384]{3,1,2,0:T(4,128)(2,1)S(1)}, u32[]{:S(2)}, u32[]{:S(2)}) async-start(bf16[8,3,1,16384]{3,1,2,0:T(4,128)(2,1)} %copy.96), calls=%async_computation.1 | async-start | bytes 2097152 | tf_op jit(solution)/shard_map/all_to_all | solution.py:323
  217.4 218.2 %reduce-scatter.17.cloned.1.call-start = ((), (), s32[]{:S(2)}) async-start(), calls=%async_computation.17 | async-start | bytes 1327104 | tf_op jit(solution)/shard_map/reduce_scatter | solution.py:400
  240.3 7.4 %copy-start.8 = (bf16[512,768]{1,0:T(8,128)(2,1)S(1)}, bf16[512,768]{1,0:T(8,128)(2,1)}, u32[]{:S(2)}) copy-start(bf16[512,768]{1,0:T(8,128)(2,1)} %param.20) | copy-start | bytes 2359300
  247.7 10.1 %copy-start.20 = (bf16[768,3072]{1,0:T(8,128)(2,1)S(1)}, bf16[768,3072]{1,0:T(8,128)(2,1)}, u32[]{:S(2)}) copy-start(bf16[768,3072]{1,0:T(8,128)(2,1)} %all-gather.9.cloned.1.call-done) | copy-start | bytes 14155780
  257.8 3.5 copy-start.21
  260.9 15.4 %slice-start = ((s8[6291456]{0:T(1024)(128)(4,1)}), s8[4194304]{0:T(1024)(128)(4,1)S(1)}, s32[]{:S(2)}) async-start(s8[6291456]{0:T(1024)(128)(4,1)} %bitcast.198), calls=%async_computation.24 | async-start | bytes 8388608
  261.3 15.1 %slice-start.1 = ((s8[6291456]{0:T(1024)(128)(4,1)}), s8[2097152]{0:T(1024)(128)(4,1)S(1)}, s32[]{:S(2)}) async-start(s8[6291456]{0:T(1024)(128)(4,1)} %bitcast.198), calls=%async_computation.25 | async-start | bytes 4194304
  261.3 15.1 %copy-start.9 = (bf16[512,768]{1,0:T(8,128)(2,1)S(1)}, bf16[512,768]{1,0:T(8,128)(2,1)}, u32[]{:S(2)}) copy-start(bf16[512,768]{1,0:T(8,128)(2,1)} %param.20) | copy-start | bytes 2359300
  276.4 3.8 copy-start.6
  282.1 239.1 %reduce-scatter.29.cloned.1.call-start = ((), (), s32[]{:S(2)}) async-start(), calls=%async_computation.23 | async-start | bytes 5308416
  295.3 228.2 %reduce-scatter.21.cloned.1.call-start = ((), (), s32[]{:S(2)}) async-start(), calls=%async_computation.19 | async-start | bytes 5308416 | tf_op jit(solution)/shard_map/reduce_scatter | solution.py:406
  431.0 48.7 %all-to-all-start.3 = ((bf16[8,3,3,16384]{3,2,1,0:T(4,128)(2,1)}), bf16[8,3,3,16384]{3,2,1,0:T(4,128)(2,1)}, u32[]{:S(2)}, u32[]{:S(2)}) async-start(bf16[8,3,3,16384]{3,2,1,0:T(4,128)(2,1)} %copy.103), calls=%async_computation.3 | async-start | bytes 6291456 | tf_op jit(solution)/shard_map/all_to_all | solution.py:384
  435.5 99.4 %reduce-scatter.27.cloned.1.call-start = ((), (), s32[]{:S(2)}) async-start(), calls=%async_computation.22 | async-start | bytes 245760
  437.4 130.0 %reduce-scatter.15.cloned.1.call-start = ((), (), s32[]{:S(2)}) async-start(), calls=%async_computation.16 | async-start | bytes 3981312 | tf_op jit(solution)/shard_map/reduce_scatter | solution.py:397
  521.1 97.9 %reduce-scatter.19.cloned.1.call-start = ((), (), s32[]{:S(2)}) async-start(), calls=%async_computation.18 | async-start | bytes 737280 | tf_op jit(solution)/shard_map/reduce_scatter | solution.py:417
  523.4 97.3 %reduce-scatter.23.cloned.1.call-start = ((), (), s32[]{:S(2)}) async-start(), calls=%async_computation.20 | async-start | bytes 737280 | tf_op jit(solution)/shard_map/reduce_scatter | solution.py:420
  524.1 113.2 %reduce-scatter.25.cloned.1.call-start = ((), (), s32[]{:S(2)}) async-start(), calls=%async_computation.21 | async-start | bytes 737280
  (11 other events, 20.8 us)
Sparse Core Ops, SparseCore 0:
  27.0 35.0 all-gather.4
  64.5 23.9 all-gather.6
  90.3 47.0 all-gather.8
  139.2 50.1 all-gather.10
  282.2 39.6 reduce-scatter.16
  325.2 57.0 reduce-scatter.28
  385.8 84.5 reduce-scatter.20
  473.2 25.7 reduce-scatter.26
  521.2 46.1 reduce-scatter.14
  569.5 22.0 reduce-scatter.18
  593.9 20.7 reduce-scatter.22
  616.8 20.3 reduce-scatter.24

commit v2 on v1

--- a/solution.py
+++ b/solution.py
@@ -290,18 +290,24 @@
         .set(jnp.arange(pair_count, dtype=jnp.int32))
     )
     held_pairs = lax.dynamic_slice_in_dim(order_row, my_index * per_dev, per_dev, 0)
-    row_parts = (
-        lax.all_gather(qkv_weight, "batch", axis=0, tiled=True),
-        lax.all_gather(proj_weight, "batch", axis=0, tiled=True),
-        lax.all_gather(up_weight, "batch", axis=0, tiled=True),
-        lax.all_gather(down_weight, "batch", axis=0, tiled=True),
-    )
-    w_qkv, w_proj, w_up, w_down = (
-        lax.all_gather(row_parts[0], "seq", axis=1, tiled=True),
-        lax.all_gather(row_parts[1], "seq", axis=1, tiled=True),
-        lax.all_gather(row_parts[2], "seq", axis=1, tiled=True),
-        lax.all_gather(row_parts[3], "seq", axis=1, tiled=True),
-    )
+    n_batch = lax.axis_size("batch")
+    both = ("batch", "seq")
+    g_qkv = lax.all_gather(qkv_weight, both, axis=0, tiled=False)
+    rest = jnp.concatenate(
+        [proj_weight.reshape(-1), up_weight.reshape(-1), down_weight.reshape(-1)]
+    )
+    g_rest = lax.all_gather(rest, both, axis=0, tiled=False)
+
+    def regroup(flat, rows, cols):
+        return jnp.transpose(flat.reshape(n_batch, n_seq, rows, cols), (0, 2, 1, 3)).reshape(
+            n_batch * rows, n_seq * cols
+        )
+
+    w_qkv = regroup(g_qkv, *qkv_weight.shape)
+    sizes = [proj_weight.size, up_weight.size, down_weight.size]
+    w_proj = regroup(g_rest[:, : sizes[0]], *proj_weight.shape)
+    w_up = regroup(g_rest[:, sizes[0] : sizes[0] + sizes[1]], *up_weight.shape)
+    w_down = regroup(g_rest[:, sizes[0] + sizes[1] :], *down_weight.shape)
     inputs32 = block_input.astype(jnp.float32)
     norm1_out, normed1, inv_std1 = norm_rows(inputs32, norm1_gain, norm1_bias)
     norm1_low = norm1_out.astype(jnp.bfloat16)
@@ -342,18 +348,6 @@
     ]
     dwa_terms.append(jnp.sum(block_out * grad_out))
     dwa_local = jnp.stack(dwa_terms)
-    again_parts = (
-        lax.all_gather(qkv_weight, "batch", axis=0, tiled=True),
-        lax.all_gather(proj_weight, "batch", axis=0, tiled=True),
-        lax.all_gather(up_weight, "batch", axis=0, tiled=True),
-        lax.all_gather(down_weight, "batch", axis=0, tiled=True),
-    )
-    w_qkv, w_proj, w_up, w_down = (
-        lax.all_gather(again_parts[0], "seq", axis=1, tiled=True),
-        lax.all_gather(again_parts[1], "seq", axis=1, tiled=True),
-        lax.all_gather(again_parts[2], "seq", axis=1, tiled=True),
-        lax.all_gather(again_parts[3], "seq", axis=1, tiled=True),
-    )
     dy_full = dwa_weights[HIST] * grad_out
     dmlp_low = dy_full.astype(jnp.bfloat16)
     down_local = jnp.einsum("nf,nd->fd", gelu_low, dmlp_low, preferred_element_type=jnp.float32)
@@ -363,6 +357,11 @@
     dnorm2 = jnp.einsum("nf,df->nd", dup_low, w_up, preferred_element_type=jnp.float32)
     dmid_norm, gain2_local, bias2_local = norm_back(dnorm2, normed2, inv_std2, norm2_gain)
     dmiddle = dy_full + dmid_norm
+    early_sums = jnp.sum(
+        lax.all_gather(jnp.concatenate([gain2_local, bias2_local, dwa_local]), both, axis=0),
+        axis=0,
+    )
+    gain2_grad, bias2_grad, dwa_grad = early_sums[:D], early_sums[D : 2 * D], early_sums[2 * D :]
     dmiddle_low = dmiddle.astype(jnp.bfloat16)
     proj_local = jnp.einsum("nd,ne->de", attended, dmiddle_low, preferred_element_type=jnp.float32)
     dattended = jnp.einsum(
@@ -393,37 +392,22 @@
     dnorm1 = jnp.einsum("nf,df->nd", dqkv_low, w_qkv, preferred_element_type=jnp.float32)
     dinput_norm, gain1_local, bias1_local = norm_back(dnorm1, normed1, inv_std1, norm1_gain)
     input_grad = (dmiddle + dinput_norm).astype(jnp.bfloat16)
-    col_sums = (
-        lax.psum_scatter(
-            qkv_local.astype(jnp.bfloat16), "seq", scatter_dimension=1, tiled=True
-        ).astype(jnp.float32),
-        lax.psum_scatter(
-            proj_local.astype(jnp.bfloat16), "seq", scatter_dimension=1, tiled=True
-        ).astype(jnp.float32),
-        lax.psum_scatter(
-            up_local.astype(jnp.bfloat16), "seq", scatter_dimension=1, tiled=True
-        ).astype(jnp.float32),
-        lax.psum_scatter(
-            down_local.astype(jnp.bfloat16), "seq", scatter_dimension=1, tiled=True
-        ).astype(jnp.float32),
-    )
-    qkv_grad, proj_grad, up_grad, down_grad = (
-        lax.psum_scatter(
-            col_sums[0].astype(jnp.bfloat16), "batch", scatter_dimension=0, tiled=True
-        ).astype(jnp.float32),
-        lax.psum_scatter(
-            col_sums[1].astype(jnp.bfloat16), "batch", scatter_dimension=0, tiled=True
-        ).astype(jnp.float32),
-        lax.psum_scatter(
-            col_sums[2].astype(jnp.bfloat16), "batch", scatter_dimension=0, tiled=True
-        ).astype(jnp.float32),
-        lax.psum_scatter(
-            col_sums[3].astype(jnp.bfloat16), "batch", scatter_dimension=0, tiled=True
-        ).astype(jnp.float32),
-    )
-    gain1_grad, bias1_grad, gain2_grad, bias2_grad, dwa_grad = lax.psum(
-        (gain1_local, bias1_local, gain2_local, bias2_local, dwa_local), ("batch", "seq")
-    )
+    def scatter_grad(partial):
+        by_cols = lax.psum_scatter(
+            partial.astype(jnp.bfloat16), "seq", scatter_dimension=1, tiled=True
+        )
+        return lax.psum_scatter(by_cols, "batch", scatter_dimension=0, tiled=True).astype(
+            jnp.float32
+        )
+
+    down_grad = scatter_grad(down_local)
+    up_grad = scatter_grad(up_local)
+    proj_grad = scatter_grad(proj_local)
+    qkv_grad = scatter_grad(qkv_local)
+    late_sums = lax.psum(
+        lax.psum(jnp.concatenate([gain1_local, bias1_local]), "seq"), "batch"
+    )
+    gain1_grad, bias1_grad = late_sums[:D], late_sums[D:]
     row_lse = log_total.reshape(1, per_dev, SLOT)
     return (
         block_output,

time: 659 us -> 819 us (1.24); the launches traced: 646 us -> 815 us
  waiting for transfers between devices: 133 us -> 321 us
  blocking collectives: 125 us -> 42.9 us
  local copies, waits for them, and re-layouts: 136 us -> 209 us
  Pallas kernels: 111 us -> 45 us
  starting transfers between devices: 12.5 us -> 74 us
  matrix products: 71 us -> 60.6 us
    unnamed x15, waiting for transfers between devices: 15.8 us -> 115 us
    all_gather x4 -> x0, blocking collectives: 66.6 us -> none  [the longest x1 18.6 us: local(): lax.all_gather(qkv_weight, 'batch', axis=0, tiled=True)]
    all_gather x4 -> x2, waiting for transfers between devices: 0.68 us -> 62.4 us  [the longest x1 62.4 us: local(): g_qkv = lax.all_gather(qkv_weight, both, axis=0, tiled=False)]
    pallas_call x1, Pallas kernels: 77 us -> 31.1 us  [attn_backward(): pl.pallas_call(functools.partial(bwd_kernel, blk=blk, scale=scale), grid_...]
    all_to_all x1, starting transfers between devices: 4.48 us -> 47.6 us  [local(): lax.all_to_all(pairs_split(dpairs, n_seq), 'seq', split_axis=0, concat_ax...]
    reshape x0 -> x9, local copies, waits for them, and re-layouts: none -> 33.5 us  [the longest x4 20.3 us: regroup(): flat.reshape(n_batch, n_seq, rows, cols)]
    reduce_scatter x5, waiting for transfers between devices: 30.8 us -> 56.9 us  [the longest x3 41.8 us: scatter_grad(): lax.psum_scatter(partial.astype(jnp.bfloat16), 'seq', scatter_dimension=1...]
    pallas_call x1, Pallas kernels: 33.8 us -> 13.9 us  [attn_forward(): pl.pallas_call(functools.partial(fwd_kernel, bq=bq, bk=bk, scale=scale),...]
  transfers between devices with their start and end apart: 15 -> 14, of which waited for: 6 -> 9; matrix products, arithmetic and copies ran while one was open for 32% -> 27% of each run, Pallas kernels for 17% -> 6%
where the time goes in v2:
time: 819 us; the launch traced here: 815 us
  waiting for transfers between devices  321 us (39%)
  local copies, waits for them, and re-layouts  209 us (26%)
  starting transfers between devices  74 us (9%)
  matrix products  60.6 us (7%)
  other arithmetic  46.9 us (6%)
  Pallas kernels  45 us (5%)
  blocking collectives  42.9 us (5%)
  between operations  15.3 us (2%)
    unnamed x15, waiting for transfers between devices  115 us
    all_gather x1, waiting for transfers between devices, local(): g_qkv = lax.all_gather(qkv_weight, both, axis=0, tiled=False)  62.4 us
    all_to_all x1, starting transfers between devices, local(): lax.all_to_all(pairs_split(dpairs, n_seq), 'seq', split_axis=0, concat_ax...  47.6 us
    reduce_scatter x3, waiting for transfers between devices, scatter_grad(): lax.psum_scatter(partial.astype(jnp.bfloat16), 'seq', scatter_dimension=1...  41.8 us
    all_to_all x1, waiting for transfers between devices, local(): lax.all_to_all(to_pairs(stacked, order_row, n_seq, per_dev), 'seq', split...  36.5 us
    all_to_all x1, waiting for transfers between devices, local(): lax.all_to_all(pairs_split(dpairs, n_seq), 'seq', split_axis=0, concat_ax...  35.8 us
    unnamed x99, local copies, waits for them, and re-layouts  32.7 us
    pallas_call x1, Pallas kernels, attn_backward(): pl.pallas_call(functools.partial(bwd_kernel, blk=blk, scale=scale), grid_...  31.1 us
  transfers between devices with their start and end apart: 14, of which 9 were waited for; matrix products, arithmetic and copies ran while one was open for 27% of the time, Pallas kernels for 6%

profile of v2, /device:TPU:0, one launch (start us, length us, event | category | flops | bytes accessed | tf_op | source)
XLA Modules:
  0.0 814.5 jit_solution(4833127092527509670)
XLA Ops:
  14.9 62.4 %all-gather.6.cloned.1.call-done = bf16[6144,288]{1,0:T(8,128)(2,1)} async-done(((bf16[192,288]{1,0:T(8,128)(2,1)}), bf16[6144,288]{1,0:T(8,128)(2,1)}) %all-gather.6.cloned.1.call-update) | async-done | bytes 3538960 | tf_op jit(solution)/shard_map/all_gather | solution.py:295
  77.3 7.3 copy.143
  84.6 8.1 reshape.427
  123.9 8.3 %reshape.540 = bf16[24,3,16384]{2,1,0:T(4,128)(2,1)} reshape(bf16[2,12,3,256,64]{4,3,2,1,0:T(8,128)(2,1)} %copy.122) | data formatting | bytes 4718592 | tf_op jit(solution)/shard_map/reshape | solution.py:220
  149.8 36.5 %all-to-all-done = bf16[8,3,3,16384]{3,1,2,0:T(4,128)(2,1)S(1)} async-done(((bf16[8,3,3,16384]{3,1,2,0:T(4,128)(2,1)}), bf16[8,3,3,16384]{3,1,2,0:T(4,128)(2,1)S(1)}, u32[]{:S(2)}, u32[]{:S(2)}) %all-to-all-start) | async-done | bytes 2359328 | tf_op jit(solution)/shard_map/all_to_all | solution.py:321
  189.4 7.0 reshape.432
  196.4 13.9 %attn_fwd.1 = (bf16[3,2048,64]{2,1,0:T(8,128)(2,1)}, f32[3,1,2048]{2,1,0:T(1,128)}) custom-call(s32[3]{0:T(128)} %and_select_fusion.1.seg_ref, bf16[3,3,2048,64]{3,2,1,0:T(8,128)(2,1)} %bitcast.209, bf16[3,3,2048,64]{3,2,1,0:T(8,128)(2,1)} %bitcast.210, bf16[3,3,2048,64]{3,2,1,0:T(8,128)(2,1)} %bitcast.211), custom_call_target="tpu_custom_call" | custom-call | flops 1811939328 | bytes 3170304 | tf_op jit(solution)/shard_map/attn_fwd/pallas_call | solution.py:88
  214.6 21.0 %all-to-all-start.1 = ((bf16[8,3,1,16384]{3,1,2,0:T(4,128)(2,1)}), bf16[8,3,1,16384]{3,1,2,0:T(4,128)(2,1)S(1)}, u32[]{:S(2)}, u32[]{:S(2)}) async-start(bf16[8,3,1,16384]{3,1,2,0:T(4,128)(2,1)} %copy.106), calls=%async_computation.1 | async-start | bytes 2097152 | tf_op jit(solution)/shard_map/all_to_all | solution.py:329
  237.1 13.9 %all-to-all-done.1 = bf16[8,3,1,16384]{3,1,2,0:T(4,128)(2,1)S(1)} async-done(((bf16[8,3,1,16384]{3,1,2,0:T(4,128)(2,1)}), bf16[8,3,1,16384]{3,1,2,0:T(4,128)(2,1)S(1)}, u32[]{:S(2)}, u32[]{:S(2)}) %all-to-all-start.1) | async-done | bytes 786464 | tf_op jit(solution)/shard_map/all_to_all | solution.py:329
  255.9 10.5 %reshape.519 = bf16[32,165888]{1,0:T(8,128)(2,1)} reshape(bf16[5308416]{0:T(1024)(128)(2,1)} %all-gather.8.cloned.1.call-done) | data formatting | bytes 21233664 | tf_op jit(solution)/shard_map/all_gather | solution.py:299
  266.4 8.1 fusion.60
  281.2 9.2 %reshape.444 = bf16[4,8,768,96]{3,2,1,0:T(8,128)(2,1)} reshape(bf16[32,73728]{1,0:T(8,128)(2,1)} %get-tuple-element.106) | data formatting | bytes 9437184 | tf_op jit(solution)/shard_map/reshape | solution.py:302
  290.4 10.2 %copy.110 = bf16[4,768,8,96]{1,0,3,2:T(4,128)(2,1)} copy(bf16[4,768,8,96]{3,1,2,0:T(8,128)(2,1)} %bitcast.215) | data formatting | bytes 9437184 | tf_op jit(solution)/shard_map/transpose | solution.py:302
  312.6 7.2 fusion.6
  322.9 13.5 %fusion.32 = (bf16[512,768]{1,0:T(8,128)(2,1)}, f32[512,768]{1,0:T(8,128)S(1)}) fusion(f32[]{:T(128)} %bitcast.40, f32[]{:T(128)} %bitcast.38, f32[]{:T(128)} %bitcast.36, f32[]{:T(128)} %bitcast.34, f32[]{:T(128)} %bitcast.32, f32[]{:T(128)} %bitcast.30, f32[]{:T(128)} %bitcast.28, f32[]{:T(128)} %bitcast.26, f32[]{:T(128)} %bitcast, ...), kind=kOutput, calls=%fused_computation.71 | convolution fusion | flops 2440691712 | bytes 21233700 | tf_op jit(solution)/shard_map/dot_general | solution.py:339
  348.5 6.8 copy.132
  356.4 8.6 %convolution_convert_fusion.1 = bf16[3072,768]{0,1:T(8,128)(2,1)} fusion(bf16[512,768]{1,0:T(8,128)(2,1)S(1)} %copy-done.9, f32[]{:T(128)} %bitcast, f32[512,3072]{1,0:T(8,128)} %copy-done.34), kind=kOutput, calls=%fused_computation.18 | convolution fusion | flops 2433613824 | bytes 11796484 | tf_op jit(solution)/shard_map/nf,nd->fd/dot_general | solution.py:353
  377.9 17.9 %all_to_all.20 = bf16[8,3,1,16384]{3,1,2,0:T(4,128)(2,1)S(1)} all-to-all(bf16[8,3,1,16384]{3,1,2,0:T(4,128)(2,1)S(1)} %bitcast.236), channel_id=1, replica_groups=mesh['batch'=4,'seq'=8] {'seq'}, dimensions={0} | all-to-all | bytes 1572864 | tf_op jit(solution)/shard_map/all_to_all | solution.py:371
  403.4 31.1 %attn_bwd.1 = bf16[3,3,2048,64]{3,2,1,0:T(8,128)(2,1)} custom-call(s32[3]{0:T(128)} %and_select_fusion.1.seg_ref, bf16[3,3,2048,64]{3,2,1,0:T(8,128)(2,1)} %bitcast.212, bf16[3,3,2048,64]{3,2,1,0:T(8,128)(2,1)} %bitcast.213, bf16[3,3,2048,64]{3,2,1,0:T(8,128)(2,1)} %bitcast.214, bf16[3,2048,64]{2,1,0:T(8,128)(2,1)} %bitcast.223, ...), custom_call_target="tpu_custom_call" | custom-call | flops 4529848320 | bytes 5554176 | tf_op jit(solution)/shard_map/attn_bwd/pallas_call | solution.py:168
  434.5 6.8 reshape.451
  446.7 47.6 %all-to-all-start.3 = ((bf16[8,3,3,16384]{3,2,1,0:T(4,128)(2,1)}), bf16[8,3,3,16384]{3,2,1,0:T(4,128)(2,1)}, u32[]{:S(2)}, u32[]{:S(2)}) async-start(bf16[8,3,3,16384]{3,2,1,0:T(4,128)(2,1)} %copy.115), calls=%async_computation.3 | async-start | bytes 6291456 | tf_op jit(solution)/shard_map/all_to_all | solution.py:383
  503.1 35.8 %all-to-all-done.3 = bf16[8,3,3,16384]{3,2,1,0:T(4,128)(2,1)} async-done(((bf16[8,3,3,16384]{3,2,1,0:T(4,128)(2,1)}), bf16[8,3,3,16384]{3,2,1,0:T(4,128)(2,1)}, u32[]{:S(2)}, u32[]{:S(2)}) %all-to-all-start.3) | async-done | bytes 2359328 | tf_op jit(solution)/shard_map/all_to_all | solution.py:383
  539.0 7.3 gather_fusion.4
  551.3 8.4 %reshape.543 = bf16[2,12,3,256,64]{4,3,2,1,0:T(8,128)(2,1)} reshape(bf16[24,3,16384]{2,1,0:T(4,128)(2,1)} %broadcast_select_fusion) | data formatting | bytes 4718592 | tf_op jit(solution)/shard_map/reshape | solution.py:250
  559.7 7.6 copy.119
  590.3 72.3 %all-reduce.3.cloned.1.call-done = f32[49440]{0:T(1024)} async-done(((f32[49440]{0:T(1024)}), f32[49440]{0:T(1024)}) %all-reduce.3.cloned.1.call-update) | async-done | bytes 197776
  664.8 21.1 %reduce-scatter.27.cloned.1.call-done = bf16[192,96]{1,0:T(8,128)(2,1)} async-done(((bf16[768,96]{1,0:T(8,128)(2,1)}), bf16[192,96]{1,0:T(8,128)(2,1)}) %reduce-scatter.27.cloned.1.call-update) | async-done | bytes 36880
  693.9 41.8 %reduce-scatter.15.cloned.1.call-done = bf16[768,288]{0,1:T(8,128)(2,1)} async-done(((bf16[768,2304]{0,1:T(8,128)(2,1)}), bf16[768,288]{0,1:T(8,128)(2,1)}) %reduce-scatter.15.cloned.1.call-update) | async-done | bytes 442384 | tf_op jit(solution)/shard_map/reduce_scatter | solution.py:396
  737.7 12.8 %psum.14 = f32[1536]{0:T(1024)S(1)} all-reduce(f32[1536]{0:T(1024)S(1)} %pad_maximum_fusion.3), channel_id=1, replica_groups=mesh['batch'=4,'seq'=8] {'seq'}, use_global_device_ids=true, to_apply=%region_20.23 | all-reduce | flops 1536 | bytes 12288 | tf_op jit(solution)/shard_map/psum | solution.py:408
  750.6 12.2 %psum.15 = f32[1536]{0:T(1024)S(1)} all-reduce(f32[1536]{0:T(1024)S(1)} %psum.14), channel_id=1, replica_groups=mesh['batch'=4,'seq'=8] {'batch'}, use_global_device_ids=true, to_apply=%region_21.24 | all-reduce | flops 1536 | bytes 12288 | tf_op jit(solution)/shard_map/psum | solution.py:407
  767.9 15.1 %reduce-scatter.23.cloned.1.call-done = bf16[768,96]{0,1:T(8,128)(2,1)} async-done(((bf16[3072,96]{0,1:T(8,128)(2,1)}), bf16[768,96]{0,1:T(8,128)(2,1)}) %reduce-scatter.23.cloned.1.call-update) | async-done | bytes 147472 | tf_op jit(solution)/shard_map/reduce_scatter | solution.py:399
  784.6 21.1 %reduce-scatter.25.cloned.1.call-done = bf16[192,288]{1,0:T(8,128)(2,1)} async-done(((bf16[768,288]{1,0:T(8,128)(2,1)}), bf16[192,288]{1,0:T(8,128)(2,1)}) %reduce-scatter.25.cloned.1.call-update) | async-done | bytes 110608
  (230 shorter events, 187.8 us)
Async XLA Ops:
  7.2 4.9 copy-start.29
  7.2 5.0 copy-start.33
  7.2 7.1 copy-start.1
  7.2 70.1 %all-gather.6.cloned.1.call-start = ((), (), s32[]{:S(2)}) async-start(), calls=%async_computation.17 | async-start | bytes 4866048 | tf_op jit(solution)/shard_map/all_gather | solution.py:295
  7.9 247.9 %all-gather.8.cloned.1.call-start = ((), (), s32[]{:S(2)}) async-start(), calls=%async_computation.18 | async-start | bytes 10948608 | tf_op jit(solution)/shard_map/all_gather | solution.py:299
  14.3 95.2 %copy-start.14 = (f32[2,256,32]{1,0,2:T(2,128)}, f32[2,256,32]{1,0,2:T(2,128)S(1)}, u32[]{:S(2)}) copy-start(f32[2,256,32]{1,0,2:T(2,128)S(1)} %get-tuple-element.121) | copy-start | bytes 196612
  14.3 95.2 %copy-start.16 = (f32[2,256,32]{1,0,2:T(2,128)}, f32[2,256,32]{1,0,2:T(2,128)S(1)}, u32[]{:S(2)}) copy-start(f32[2,256,32]{1,0,2:T(2,128)S(1)} %get-tuple-element.122) | copy-start | bytes 196612
  14.5 78.2 %copy-start.20 = (f32[512]{0:T(512)}, f32[512]{0:T(512)S(1)}, u32[]{:S(2)}) copy-start(f32[512]{0:T(512)S(1)} %broadcast_multiply_fusion.6) | copy-start | bytes 6148
  14.9 77.8 %copy-start.22 = (f32[512]{0:T(512)}, f32[512]{0:T(512)S(1)}, u32[]{:S(2)}) copy-start(f32[512]{0:T(512)S(1)} %add_rsqrt_fusion.1) | copy-start | bytes 6148
  84.6 8.1 copy-start.25
  84.6 8.1 copy-start.31
  144.4 41.8 %all-to-all-start = ((bf16[8,3,3,16384]{3,1,2,0:T(4,128)(2,1)}), bf16[8,3,3,16384]{3,1,2,0:T(4,128)(2,1)S(1)}, u32[]{:S(2)}, u32[]{:S(2)}) async-start(bf16[8,3,3,16384]{3,1,2,0:T(4,128)(2,1)} %copy.104), calls=%async_computation | async-start | bytes 6291456 | tf_op jit(solution)/shard_map/all_to_all | solution.py:321
  213.0 23.5 %copy-start.19 = (f32[9]{0:T(128)S(1)}, f32[9]{0:T(128)}, u32[]{:S(2)}) copy-start(f32[9]{0:T(128)} %param.29) | copy-start | bytes 112
  214.6 36.4 %all-to-all-start.1 = ((bf16[8,3,1,16384]{3,1,2,0:T(4,128)(2,1)}), bf16[8,3,1,16384]{3,1,2,0:T(4,128)(2,1)S(1)}, u32[]{:S(2)}, u32[]{:S(2)}) async-start(bf16[8,3,1,16384]{3,1,2,0:T(4,128)(2,1)} %copy.106), calls=%async_computation.1 | async-start | bytes 2097152 | tf_op jit(solution)/shard_map/all_to_all | solution.py:329
  235.7 265.4 %reduce-scatter.17.cloned.1.call-start = ((), (), s32[]{:S(2)}) async-start(), calls=%async_computation.13 | async-start | bytes 1327104 | tf_op jit(solution)/shard_map/reduce_scatter | solution.py:396
  237.1 15.7 %copy-start.27 = (pred[24]{0:T(512)(128)(4,1)}, pred[24]{0:T(512)(128)(4,1)S(1)}, u32[]{:S(2)}) copy-start(pred[24]{0:T(512)(128)(4,1)S(1)} %compare_and_fusion) | copy-start | bytes 76
  255.8 49.6 %copy-start.5 = (bf16[96,8,2,256]{3,1,2,0:T(8,128)(2,1)}, bf16[96,8,2,256]{3,1,2,0:T(8,128)(2,1)S(1)}, u32[]{:S(2)}) copy-start(bf16[96,8,2,256]{3,1,2,0:T(8,128)(2,1)S(1)} %copy.135) | copy-start | bytes 2359300
  266.4 8.1 slice-start
  281.2 24.3 %copy-start.11 = (bf16[768,768]{1,0:T(8,128)(2,1)}, bf16[768,768]{1,0:T(8,128)(2,1)S(1)}, u32[]{:S(2)}) copy-start(bf16[768,768]{1,0:T(8,128)(2,1)S(1)} %reshape.441) | copy-start | bytes 3538948
  307.1 5.5 copy-start.8
  307.1 15.8 %slice-start.3 = ((s8[6291456]{0:T(1024)(128)(4,1)}), s8[4194304]{0:T(1024)(128)(4,1)S(1)}, s32[]{:S(2)}) async-start(s8[6291456]{0:T(1024)(128)(4,1)} %bitcast.227), calls=%async_computation.26 | async-start | bytes 8388608
  312.6 10.3 %slice-start.4 = ((s8[6291456]{0:T(1024)(128)(4,1)}), s8[2097152]{0:T(1024)(128)(4,1)S(1)}, s32[]{:S(2)}) async-start(s8[6291456]{0:T(1024)(128)(4,1)} %bitcast.227), calls=%async_computation.27 | async-start | bytes 4194304
  342.0 238.4 %reduce-scatter.29.cloned.1.call-start = ((), (), s32[]{:S(2)}) async-start(), calls=%async_computation.22 | async-start | bytes 5308416
  355.3 228.7 %reduce-scatter.21.cloned.1.call-start = ((), (), s32[]{:S(2)}) async-start(), calls=%async_computation.15 | async-start | bytes 5308416 | tf_op jit(solution)/shard_map/reduce_scatter | solution.py:396
  446.7 92.3 %all-to-all-start.3 = ((bf16[8,3,3,16384]{3,2,1,0:T(4,128)(2,1)}), bf16[8,3,3,16384]{3,2,1,0:T(4,128)(2,1)}, u32[]{:S(2)}, u32[]{:S(2)}) async-start(bf16[8,3,3,16384]{3,2,1,0:T(4,128)(2,1)} %copy.115), calls=%async_computation.3 | async-start | bytes 6291456 | tf_op jit(solution)/shard_map/all_to_all | solution.py:383
  494.2 168.3 %all-reduce.3.cloned.1.call-start = ((), (), s32[]{:S(2)}) async-start(), calls=%async_computation.19 | async-start | bytes 401408
  501.0 184.9 %reduce-scatter.27.cloned.1.call-start = ((), (), s32[]{:S(2)}) async-start(), calls=%async_computation.21 | async-start | bytes 245760
  502.9 232.8 %reduce-scatter.15.cloned.1.call-start = ((), (), s32[]{:S(2)}) async-start(), calls=%async_computation.12 | async-start | bytes 3981312 | tf_op jit(solution)/shard_map/reduce_scatter | solution.py:396
  539.0 7.3 copy-start.28
  580.4 185.8 %reduce-scatter.19.cloned.1.call-start = ((), (), s32[]{:S(2)}) async-start(), calls=%async_computation.14 | async-start | bytes 737280 | tf_op jit(solution)/shard_map/reduce_scatter | solution.py:399
  582.7 200.3 %reduce-scatter.23.cloned.1.call-start = ((), (), s32[]{:S(2)}) async-start(), calls=%async_computation.16 | async-start | bytes 737280 | tf_op jit(solution)/shard_map/reduce_scatter | solution.py:399
  584.0 221.7 %reduce-scatter.25.cloned.1.call-start = ((), (), s32[]{:S(2)}) async-start(), calls=%async_computation.20 | async-start | bytes 737280
  (23 other events, 47.4 us)
Sparse Core Ops, SparseCore 0:
  10.9 66.3 all-gather.5
  80.8 84.7 all-gather.7
  342.1 35.6 reduce-scatter.16
  381.1 55.9 reduce-scatter.28
  440.4 89.1 reduce-scatter.20
  535.6 126.8 all-reduce.2
  665.4 20.5 reduce-scatter.26
  689.4 46.1 reduce-scatter.14
  737.9 22.1 reduce-scatter.18
  762.2 20.6 reduce-scatter.22
  785.2 20.4 reduce-scatter.24

commit v3 on v1

--- a/solution.py
+++ b/solution.py
@@ -24,14 +24,14 @@
     seg_len = seg_ref[pair]
     q_start = qi * bq
     seg_start = (q_start // seg_len) * seg_len
-    query = q_ref[0, 0]
+    query = (q_ref[0, 0].astype(jnp.float32) * scale).astype(jnp.bfloat16)
 
     def step(j, carry, masked):
         m_old, l_old, acc = carry
         k_off = pl.multiple_of(j * bk, bk)
         key = k_ref[0, 0, pl.ds(k_off, bk), :]
         value = v_ref[0, 0, pl.ds(k_off, bk), :]
-        s = lax.dot_general(query, key, NT_DIMS, preferred_element_type=jnp.float32) * scale
+        s = lax.dot_general(query, key, NT_DIMS, preferred_element_type=jnp.float32)
         if masked:
             rows = q_start + lax.broadcasted_iota(jnp.int32, (bq, bk), 0)
             cols = k_off + lax.broadcasted_iota(jnp.int32, (bq, bk), 1)
@@ -62,7 +62,7 @@
     lse_ref[0] = jnp.transpose(jnp.broadcast_to(lse, (bq, 128)))[0:1, :]
 
 
-def attn_forward(qkv, seg_pairs, bq=512, bk=256):
+def attn_forward(qkv, seg_pairs, bq=512, bk=512):
     pairs, _, seq_len, head_size = qkv.shape
     scale = head_size ** (-0.5)
     n_q = seq_len // bq
@@ -97,7 +97,7 @@
     )(seg_pairs, qkv, qkv, qkv)
 
 
-def bwd_kernel(seg_ref, q_ref, k_ref, v_ref, do_ref, lse_ref, dl_ref, out_ref, dq_acc, *, blk, scale):
+def bwd_kernel(seg_ref, q_ref, k_ref, v_ref, do_ref, lse_ref, dl_ref, out_ref, dq_acc, *, bk, bq, scale):
     pair = pl.program_id(0)
     kj = pl.program_id(1)
 
@@ -106,49 +106,53 @@
         dq_acc[...] = jnp.zeros_like(dq_acc)
 
     seg_len = seg_ref[pair]
-    k_start = kj * blk
+    k_start = kj * bk
     seg_end = (k_start // seg_len + 1) * seg_len
     key = k_ref[0, 0]
-    value = v_ref[0, 0]
+    value = (v_ref[0, 0].astype(jnp.float32) * scale).astype(jnp.bfloat16)
 
     def step(i, carry, masked):
         dk, dv = carry
-        q_off = pl.multiple_of(i * blk, blk)
-        query = q_ref[0, 0, pl.ds(q_off, blk), :]
-        dout = do_ref[0, pl.ds(q_off, blk), :]
-        lse = lse_ref[0, :, pl.ds(q_off, blk)]
-        delta = dl_ref[0, :, pl.ds(q_off, blk)]
-        s_t = lax.dot_general(key, query, NT_DIMS, preferred_element_type=jnp.float32) * scale
+        q_off = pl.multiple_of(i * bq, bq)
+        query = q_ref[0, 0, pl.ds(q_off, bq), :]
+        query_s = (query.astype(jnp.float32) * scale).astype(jnp.bfloat16)
+        dout = do_ref[0, pl.ds(q_off, bq), :]
+        lse = lse_ref[0, :, pl.ds(q_off, bq)]
+        delta = dl_ref[0, :, pl.ds(q_off, bq)] * scale
+        s_t = lax.dot_general(key, query_s, NT_DIMS, preferred_element_type=jnp.float32)
         if masked:
-            keys_at = k_start + lax.broadcasted_iota(jnp.int32, (blk, blk), 0)
-            queries_at = q_off + lax.broadcasted_iota(jnp.int32, (blk, blk), 1)
+            keys_at = k_start + lax.broadcasted_iota(jnp.int32, (bk, bq), 0)
+            queries_at = q_off + lax.broadcasted_iota(jnp.int32, (bk, bq), 1)
             s_t = jnp.where(keys_at <= queries_at, s_t, MASKED)
         p_t = jnp.exp(s_t - lse)
         dv = dv + jnp.dot(p_t.astype(jnp.bfloat16), dout, preferred_element_type=jnp.float32)
         dp_t = lax.dot_general(value, dout, NT_DIMS, preferred_element_type=jnp.float32)
-        ds_t = p_t * (dp_t - delta) * scale
+        ds_t = p_t * (dp_t - delta)
         dk = dk + jnp.dot(ds_t.astype(jnp.bfloat16), query, preferred_element_type=jnp.float32)
-        dq_acc[pl.ds(q_off, blk), :] += jnp.dot(
+        dq_acc[pl.ds(q_off, bq), :] += jnp.dot(
             ds_t.T.astype(jnp.bfloat16), key, preferred_element_type=jnp.float32
         )
         return dk, dv
 
-    carry = (jnp.zeros((blk, HD), jnp.float32), jnp.zeros((blk, HD), jnp.float32))
-    carry = step(kj, carry, True)
-    dk, dv = lax.fori_loop(kj + 1, seg_end // blk, lambda i, c: step(i, c, False), carry)
-    out_ref[0, 0] = dq_acc[pl.ds(pl.multiple_of(k_start, blk), blk), :].astype(out_ref.dtype)
+    carry = (jnp.zeros((bk, HD), jnp.float32), jnp.zeros((bk, HD), jnp.float32))
+    for r in range(bk // bq):
+        carry = step(k_start // bq + r, carry, True)
+    dk, dv = lax.fori_loop(
+        (k_start + bk) // bq, seg_end // bq, lambda i, c: step(i, c, False), carry
+    )
+    out_ref[0, 0] = dq_acc[pl.ds(pl.multiple_of(k_start, bk), bk), :].astype(out_ref.dtype)
     out_ref[0, 1] = dk.astype(out_ref.dtype)
     out_ref[0, 2] = dv.astype(out_ref.dtype)
 
 
-def attn_backward(qkv, dout, lse, delta, seg_pairs, blk=256):
+def attn_backward(qkv, dout, lse, delta, seg_pairs, bk=512, bq=512):
     pairs, _, seq_len, head_size = qkv.shape
     scale = head_size ** (-0.5)
-    n_k = seq_len // blk
-    blocks_done = pairs * n_k * (n_k + 1) // 2
+    n_k = seq_len // bk
+    blocks_done = pairs * (seq_len // bq) * (seq_len // bq + 1) // 2
     cost = pl.CostEstimate(
-        flops=10 * blocks_done * blk * blk * head_size,
-        transcendentals=blocks_done * blk * blk,
+        flops=10 * blocks_done * bq * bq * head_size,
+        transcendentals=blocks_done * bq * bq,
         bytes_accessed=pairs * seq_len * head_size * 2 * 7 + pairs * seq_len * 8,
     )
     grid_spec = pltpu.PrefetchScalarGridSpec(
@@ -156,17 +160,17 @@
         grid=(pairs, n_k),
         in_specs=[
             pl.BlockSpec((1, 1, seq_len, head_size), lambda p, j, seg: (p, 0, 0, 0)),
-            pl.BlockSpec((1, 1, blk, head_size), lambda p, j, seg: (p, 1, j, 0)),
-            pl.BlockSpec((1, 1, blk, head_size), lambda p, j, seg: (p, 2, j, 0)),
+            pl.BlockSpec((1, 1, bk, head_size), lambda p, j, seg: (p, 1, j, 0)),
+            pl.BlockSpec((1, 1, bk, head_size), lambda p, j, seg: (p, 2, j, 0)),
             pl.BlockSpec((1, seq_len, head_size), lambda p, j, seg: (p, 0, 0)),
             pl.BlockSpec((1, 1, seq_len), lambda p, j, seg: (p, 0, 0)),
             pl.BlockSpec((1, 1, seq_len), lambda p, j, seg: (p, 0, 0)),
         ],
-        out_specs=pl.BlockSpec((1, 3, blk, head_size), lambda p, j, seg: (p, 0, j, 0)),
+        out_specs=pl.BlockSpec((1, 3, bk, head_size), lambda p, j, seg: (p, 0, j, 0)),
         scratch_shapes=[pltpu.VMEM((seq_len, head_size), jnp.float32)],
     )
     return pl.pallas_call(
-        functools.partial(bwd_kernel, blk=blk, scale=scale),
+        functools.partial(bwd_kernel, bk=bk, bq=bq, scale=scale),
         grid_spec=grid_spec,
         out_shape=jax.ShapeDtypeStruct((pairs, 3, seq_len, head_size), jnp.bfloat16),
         cost_estimate=cost,
@@ -290,12 +294,15 @@
         .set(jnp.arange(pair_count, dtype=jnp.int32))
     )
     held_pairs = lax.dynamic_slice_in_dim(order_row, my_index * per_dev, per_dev, 0)
-    row_parts = (
-        lax.all_gather(qkv_weight, "batch", axis=0, tiled=True),
-        lax.all_gather(proj_weight, "batch", axis=0, tiled=True),
-        lax.all_gather(up_weight, "batch", axis=0, tiled=True),
-        lax.all_gather(down_weight, "batch", axis=0, tiled=True),
-    )
+    shards = (qkv_weight, proj_weight, up_weight, down_weight)
+    gathered = lax.all_gather(
+        jnp.concatenate([w.reshape(-1) for w in shards]), "batch", axis=0
+    )
+    row_parts = []
+    offset = 0
+    for w in shards:
+        row_parts.append(gathered[:, offset : offset + w.size].reshape(-1, w.shape[1]))
+        offset += w.size
     w_qkv, w_proj, w_up, w_down = (
         lax.all_gather(row_parts[0], "seq", axis=1, tiled=True),
         lax.all_gather(row_parts[1], "seq", axis=1, tiled=True),
@@ -342,18 +349,6 @@
     ]
     dwa_terms.append(jnp.sum(block_out * grad_out))
     dwa_local = jnp.stack(dwa_terms)
-    again_parts = (
-        lax.all_gather(qkv_weight, "batch", axis=0, tiled=True),
-        lax.all_gather(proj_weight, "batch", axis=0, tiled=True),
-        lax.all_gather(up_weight, "batch", axis=0, tiled=True),
-        lax.all_gather(down_weight, "batch", axis=0, tiled=True),
-    )
-    w_qkv, w_proj, w_up, w_down = (
-        lax.all_gather(again_parts[0], "seq", axis=1, tiled=True),
-        lax.all_gather(again_parts[1], "seq", axis=1, tiled=True),
-        lax.all_gather(again_parts[2], "seq", axis=1, tiled=True),
-        lax.all_gather(again_parts[3], "seq", axis=1, tiled=True),
-    )
     dy_full = dwa_weights[HIST] * grad_out
     dmlp_low = dy_full.astype(jnp.bfloat16)
     down_local = jnp.einsum("nf,nd->fd", gelu_low, dmlp_low, preferred_element_type=jnp.float32)
@@ -421,9 +416,17 @@
             col_sums[3].astype(jnp.bfloat16), "batch", scatter_dimension=0, tiled=True
         ).astype(jnp.float32),
     )
-    gain1_grad, bias1_grad, gain2_grad, bias2_grad, dwa_grad = lax.psum(
-        (gain1_local, bias1_local, gain2_local, bias2_local, dwa_local), ("batch", "seq")
-    )
+    small_sums = lax.psum(
+        lax.psum(
+            jnp.concatenate([gain1_local, bias1_local, gain2_local, bias2_local, dwa_local]),
+            "seq",
+        ),
+        "batch",
+    )
+    gain1_grad, bias1_grad, gain2_grad, bias2_grad = (
+        small_sums[k * D : (k + 1) * D] for k in range(4)
+    )
+    dwa_grad = small_sums[4 * D :]
     row_lse = log_total.reshape(1, per_dev, SLOT)
     return (
         block_output,

time: 659 us -> 634 us (0.962)
  waiting for transfers between devices: 133 us -> 239 us
  Pallas kernels: 111 us -> 29.9 us
  blocking collectives: 125 us -> 62.2 us
  local copies, waits for them, and re-layouts: 136 us -> 151 us
    all_gather x4 -> x0, blocking collectives: 66.6 us -> none  [the longest x1 18.6 us: local(): lax.all_gather(qkv_weight, 'batch', axis=0, tiled=True)]
    pallas_call x1, Pallas kernels: 77 us -> 16.7 us  [attn_backward(): pl.pallas_call(functools.partial(bwd_kernel, bk=bk, bq=bq, scale=scale),...]
    all_gather x0 -> x1, waiting for transfers between devices: none -> 43.1 us  [local(): lax.all_gather(jnp.concatenate([w.reshape(-1) for w in shards]), 'batch',...]
    all_gather x1, waiting for transfers between devices: 0.63 us -> 26.2 us  [local(): lax.all_gather(row_parts[0], 'seq', axis=1, tiled=True)]
    pallas_call x1, Pallas kernels: 33.8 us -> 13.3 us  [attn_forward(): pl.pallas_call(functools.partial(fwd_kernel, bq=bq, bk=bk, scale=scale),...]
    unnamed x15 -> x16, waiting for transfers between devices: 15.8 us -> 29.9 us
    reshape x0 -> x11, local copies, waits for them, and re-layouts: none -> 12.2 us  [the longest x7 8.86 us: local(): gathered[:, offset:offset + w.size].reshape(-1, w.shape[1])]
    all_to_all x1, waiting for transfers between devices: 29.9 us -> 41.7 us  [local(): lax.all_to_all(to_pairs(stacked, order_row, n_seq, per_dev), 'seq', split...]
  transfers between devices with their start and end apart: 15 -> 16, of which waited for: 6 -> 8; matrix products, arithmetic and copies ran while one was open for 32% -> 35% of each run, Pallas kernels for 17% -> 5%
where the time goes in v3:
time: 634 us; the launch traced here: 624 us
  waiting for transfers between devices  239 us (38%)
  local copies, waits for them, and re-layouts  151 us (24%)
  matrix products  71.6 us (11%)
  blocking collectives  62.2 us (10%)
  other arithmetic  43.2 us (7%)
  Pallas kernels  29.9 us (5%)
  between operations  14.9 us (2%)
  starting transfers between devices  12.4 us (2%)
    all_gather x1, waiting for transfers between devices, local(): lax.all_gather(jnp.concatenate([w.reshape(-1) for w in shards]), 'batch',...  43.1 us
    all_to_all x1, waiting for transfers between devices, local(): lax.all_to_all(pairs_split(dpairs, n_seq), 'seq', split_axis=0, concat_ax...  42.3 us
    all_to_all x1, waiting for transfers between devices, local(): lax.all_to_all(to_pairs(stacked, order_row, n_seq, per_dev), 'seq', split...  41.7 us
    reduce_scatter x1, waiting for transfers between devices, local(): lax.psum_scatter(qkv_local.astype(jnp.bfloat16), 'seq', scatter_dimension...  41.6 us
    unnamed x16, waiting for transfers between devices  29.9 us
    all_gather x1, waiting for transfers between devices, local(): lax.all_gather(row_parts[0], 'seq', axis=1, tiled=True)  26.2 us
    psum x1, blocking collectives, local(): lax.psum(jnp.concatenate([gain1_local, bias1_local, gain2_local, bias2_lo...  23.5 us
    unnamed x63, local copies, waits for them, and re-layouts  20.2 us
  transfers between devices with their start and end apart: 16, of which 8 were waited for; matrix products, arithmetic and copies ran while one was open for 35% of the time, Pallas kernels for 5%

profile of v3, /device:TPU:0, one launch (start us, length us, event | category | flops | bytes accessed | tf_op | source)
XLA Modules:
  0.0 624.1 jit_solution(15297287596341695777)
XLA Ops:
  12.5 43.1 %all-gather.15.cloned.1.call-done = bf16[884736]{0:T(1024)(128)(2,1)} async-done(((bf16[221184]{0:T(1024)(128)(2,1)}), bf16[884736]{0:T(1024)(128)(2,1)}) %all-gather.15.cloned.1.call-update) | async-done | bytes 1769488 | tf_op jit(solution)/shard_map/all_gather | solution.py:298
  66.5 26.2 %all-gather.7.cloned.1.call-done = bf16[768,2304]{0,1:T(8,128)(2,1)} async-done(((bf16[768,288]{0,1:T(8,128)(2,1)}), bf16[768,2304]{0,1:T(8,128)(2,1)}) %all-gather.7.cloned.1.call-update) | async-done | bytes 3538960 | tf_op jit(solution)/shard_map/all_gather | solution.py:307
  117.9 5.2 copy.91
  123.1 8.2 %reshape.523 = bf16[24,3,16384]{2,1,0:T(4,128)(2,1)} reshape(bf16[2,12,3,256,64]{4,3,2,1,0:T(8,128)(2,1)} %copy.91) | data formatting | bytes 4718592 | tf_op jit(solution)/shard_map/reshape | solution.py:224
  131.3 6.9 %gather_fusion.1 = bf16[24,3,16384]{2,1,0:T(4,128)(2,1)S(1)} fusion(bf16[24,3,16384]{2,1,0:T(4,128)(2,1)} %reshape.523, s32[1024]{0:T(1024)S(1)} %get-tuple-element.133), kind=kCustom, calls=%fused_computation.clone | custom fusion | bytes 4718688 | tf_op jit(solution)/shard_map/jit(_take)/gather | solution.py:227
  153.5 41.7 %all-to-all-done = bf16[8,3,3,16384]{3,1,2,0:T(4,128)(2,1)S(1)} async-done(((bf16[8,3,3,16384]{3,1,2,0:T(4,128)(2,1)}), bf16[8,3,3,16384]{3,1,2,0:T(4,128)(2,1)S(1)}, u32[]{:S(2)}, u32[]{:S(2)}) %all-to-all-start) | async-done | bytes 2359328 | tf_op jit(solution)/shard_map/all_to_all | solution.py:322
  198.4 7.6 %reshape.426 = bf16[8,3,3,256,64]{4,3,0,2,1:T(8,128)(2,1)} reshape(bf16[8,3,3,16384]{3,0,2,1:T(8,128)(2,1)} %copy.75) | data formatting | bytes 4718592 | tf_op jit(solution)/shard_map/reshape | solution.py:236
  205.9 13.3 %attn_fwd.1 = (bf16[3,2048,64]{2,1,0:T(8,128)(2,1)}, f32[3,1,2048]{2,1,0:T(1,128)}) custom-call(s32[3]{0:T(128)} %and_select_fusion.1.seg_ref, bf16[3,3,2048,64]{3,2,1,0:T(8,128)(2,1)} %bitcast.186, bf16[3,3,2048,64]{3,2,1,0:T(8,128)(2,1)} %bitcast.187, bf16[3,3,2048,64]{3,2,1,0:T(8,128)(2,1)} %bitcast.188), custom_call_target="tpu_custom_call" | custom-call | flops 2013265920 | bytes 3170304 | tf_op jit(solution)/shard_map/attn_fwd/pallas_call | solution.py:88
  228.5 13.9 %all-to-all-done.1 = bf16[8,3,1,16384]{3,1,2,0:T(4,128)(2,1)S(1)} async-done(((bf16[8,3,1,16384]{3,1,2,0:T(4,128)(2,1)}), bf16[8,3,1,16384]{3,1,2,0:T(4,128)(2,1)S(1)}, u32[]{:S(2)}, u32[]{:S(2)}) %all-to-all-start.1) | async-done | bytes 786464 | tf_op jit(solution)/shard_map/all_to_all | solution.py:330
  250.3 7.0 %fusion.59 = f32[512,3072]{1,0:T(8,128)} fusion(bf16[768,3072]{1,0:T(8,128)(2,1)} %all-gather.11.cloned.1.call-done, f32[512,768]{1,0:T(8,128)S(1)} %get-tuple-element.128, f32[768]{0:T(1024)S(1)} %copy-done.18, f32[768]{0:T(1024)S(1)} %copy-done.13, f32[512]{0:T(512)S(1)} %add_rsqrt_fusion, f32[512]{0:T(512)S(1)} %broadcast_multiply_fusion.5), kind=kOutput, calls=%fused_computation.154 | convolution fusion | flops 2417885184 | bytes 12593152 | tf_op jit(solution)/shard_map/dot_general | solution.py:337
  257.3 10.1 %fusion.6 = bf16[512,3072]{1,0:T(8,128)(2,1)S(1)} fusion(f32[512,3072]{1,0:T(8,128)} %fusion.59, bf16[3072,768]{0,1:T(8,128)(2,1)} %all-gather.13.cloned.1.call-done, bf16[512,768]{1,0:T(8,128)(2,1)S(1)} %copy-done.8, f32[]{:T(128)} %bitcast), kind=kOutput, calls=%fused_computation.15 | convolution fusion | flops 2448556032 | bytes 14942212 | tf_op jit(solution)/shard_map/nd,fd->nf/dot_general | solution.py:355
  270.9 15.2 %fusion.32 = (bf16[512,768]{1,0:T(8,128)(2,1)}, f32[512,768]{1,0:T(8,128)S(1)}) fusion(f32[]{:T(128)} %bitcast.34, f32[]{:T(128)} %bitcast.32, f32[]{:T(128)} %bitcast.30, f32[]{:T(128)} %bitcast.28, f32[]{:T(128)} %bitcast.26, f32[]{:T(128)} %bitcast.24, f32[]{:T(128)} %bitcast.22, f32[]{:T(128)} %bitcast.20, f32[]{:T(128)} %bitcast, ...), kind=kOutput, calls=%fused_computation.70 | convolution fusion | flops 2440691712 | bytes 21233700 | tf_op jit(solution)/shard_map/dot_general | solution.py:340
  291.8 6.6 %convolution_convert_fusion.2 = bf16[768,3072]{1,0:T(8,128)(2,1)} fusion(bf16[512,3072]{1,0:T(8,128)(2,1)} %copy-done.21, f32[512,768]{1,0:T(8,128)S(1)} %get-tuple-element.128, f32[768]{0:T(1024)S(1)} %copy-done.18, f32[768]{0:T(1024)S(1)} %copy-done.13, f32[512]{0:T(512)S(1)} %add_rsqrt_fusion, f32[512]{0:T(512)S(1)} %broadcast_multiply_fusion.5), kind=kOutput, calls=%fused_computation.19 | convolution fusion | flops 2420244480 | bytes 9447424 | tf_op jit(solution)/shard_map/nd,nf->df/dot_general | solution.py:357
  298.4 6.6 %copy.101 = bf16[768,3072]{0,1:T(8,128)(2,1)} copy(bf16[768,3072]{1,0:T(8,128)(2,1)} %convolution_convert_fusion.2) | data formatting | bytes 9437184
  313.5 8.9 %convolution_convert_fusion.1 = bf16[3072,768]{0,1:T(8,128)(2,1)} fusion(bf16[512,768]{1,0:T(8,128)(2,1)} %param.20, f32[]{:T(128)} %bitcast, f32[512,3072]{1,0:T(8,128)} %fusion.59), kind=kOutput, calls=%fused_computation.18 | convolution fusion | flops 2433613824 | bytes 11796484 | tf_op jit(solution)/shard_map/nf,nd->fd/dot_general | solution.py:354
  325.0 19.8 %all_to_all.20 = bf16[8,3,1,16384]{3,1,2,0:T(4,128)(2,1)S(1)} all-to-all(bf16[8,3,1,16384]{3,1,2,0:T(4,128)(2,1)S(1)} %bitcast.201), channel_id=1, replica_groups=mesh['batch'=4,'seq'=8] {'seq'}, dimensions={0} | all-to-all | bytes 1572864 | tf_op jit(solution)/shard_map/all_to_all | solution.py:367
  352.5 16.7 %attn_bwd.1 = bf16[3,3,2048,64]{3,2,1,0:T(8,128)(2,1)} custom-call(s32[3]{0:T(128)} %and_select_fusion.1.seg_ref, bf16[3,3,2048,64]{3,2,1,0:T(8,128)(2,1)} %bitcast.189, bf16[3,3,2048,64]{3,2,1,0:T(8,128)(2,1)} %bitcast.190, bf16[3,3,2048,64]{3,2,1,0:T(8,128)(2,1)} %bitcast.191, bf16[3,2048,64]{2,1,0:T(8,128)(2,1)} %bitcast.194, ...), custom_call_target="tpu_custom_call" | custom-call | flops 5033164800 | bytes 5554176 | tf_op jit(solution)/shard_map/attn_bwd/pallas_call | solution.py:172
  369.2 6.8 %reshape.439 = bf16[3,3,8,16384]{3,2,1,0:T(8,128)(2,1)} reshape(bf16[3,3,2048,64]{3,2,1,0:T(8,128)(2,1)} %attn_bwd.1) | data formatting | bytes 4718592 | tf_op jit(solution)/shard_map/reshape | solution.py:244
  376.0 5.4 copy.84
  387.7 42.3 %all-to-all-done.3 = bf16[8,3,3,16384]{3,2,1,0:T(4,128)(2,1)} async-done(((bf16[8,3,3,16384]{3,2,1,0:T(4,128)(2,1)}), bf16[8,3,3,16384]{3,2,1,0:T(4,128)(2,1)}, u32[]{:S(2)}, u32[]{:S(2)}) %all-to-all-start.3) | async-done | bytes 2359328 | tf_op jit(solution)/shard_map/all_to_all | solution.py:379
  430.0 7.5 %gather_fusion.4 = bf16[24,3,16384]{2,1,0:T(4,128)(2,1)} fusion(bf16[24,3,16384]{2,1,0:T(4,128)(2,1)} %bitcast.44, s32[1024]{0:T(1024)S(1)} %pad_clamp_fusion), kind=kCustom, calls=%fused_computation.2.clone | custom fusion | bytes 4718688 | tf_op jit(solution)/shard_map/jit(_take)/gather | solution.py:251
  437.4 5.0 broadcast_select_fusion
  442.5 8.4 %reshape.526 = bf16[2,12,3,256,64]{4,3,2,1,0:T(8,128)(2,1)} reshape(bf16[24,3,16384]{2,1,0:T(4,128)(2,1)} %broadcast_select_fusion) | data formatting | bytes 4718592 | tf_op jit(solution)/shard_map/reshape | solution.py:254
  450.8 7.6 %copy.88 = bf16[2,12,3,256,64]{3,0,4,1,2:T(2,128)(2,1)} copy(bf16[2,12,3,256,64]{4,3,2,1,0:T(8,128)(2,1)} %reshape.526) | data formatting | bytes 4718592 | tf_op jit(solution)/shard_map/reshape | solution.py:254
  474.7 4.5 multiply_convert_fusion
  479.2 16.4 %reduce-scatter.27.cloned.1.call-done = bf16[192,96]{1,0:T(8,128)(2,1)} async-done(((bf16[768,96]{1,0:T(8,128)(2,1)}), bf16[192,96]{1,0:T(8,128)(2,1)}) %reduce-scatter.27.cloned.1.call-update) | async-done | bytes 36880
  497.3 6.2 fusion.22
  503.5 41.6 %reduce-scatter.15.cloned.1.call-done = bf16[768,288]{0,1:T(8,128)(2,1)} async-done(((bf16[768,2304]{0,1:T(8,128)(2,1)}), bf16[768,288]{0,1:T(8,128)(2,1)}) %reduce-scatter.15.cloned.1.call-update) | async-done | bytes 442384 | tf_op jit(solution)/shard_map/reduce_scatter | solution.py:392
  547.2 5.8 concatenate.32
  553.0 23.5 %psum.14 = f32[3081]{0:T(1024)S(1)} all-reduce(f32[3081]{0:T(1024)S(1)} %concatenate.32), channel_id=1, replica_groups=mesh['batch'=4,'seq'=8] {'seq'}, use_global_device_ids=true, to_apply=%region_31.34 | all-reduce | flops 3081 | bytes 24648 | tf_op jit(solution)/shard_map/psum | solution.py:420
  576.6 18.9 %psum.15 = f32[3081]{0:T(1024)S(1)} all-reduce(f32[3081]{0:T(1024)S(1)} %psum.14), channel_id=1, replica_groups=mesh['batch'=4,'seq'=8] {'batch'}, use_global_device_ids=true, to_apply=%region_32.35 | all-reduce | flops 3081 | bytes 24648 | tf_op jit(solution)/shard_map/psum | solution.py:419
  602.7 12.8 %reduce-scatter.25.cloned.1.call-done = bf16[192,288]{1,0:T(8,128)(2,1)} async-done(((bf16[768,288]{1,0:T(8,128)(2,1)}), bf16[192,288]{1,0:T(8,128)(2,1)}) %reduce-scatter.25.cloned.1.call-update) | async-done | bytes 110608
  (196 shorter events, 139.8 us)
Async XLA Ops:
  7.2 48.4 %all-gather.15.cloned.1.call-start = ((), (), s32[]{:S(2)}) async-start(), calls=%async_computation.21 | async-start | bytes 2211840 | tf_op jit(solution)/shard_map/all_gather | solution.py:298
  12.5 80.2 %all-gather.7.cloned.1.call-start = ((), (), s32[]{:S(2)}) async-start(), calls=%async_computation.12 | async-start | bytes 3981312 | tf_op jit(solution)/shard_map/all_gather | solution.py:307
  59.9 187.2 %all-gather.9.cloned.1.call-start = ((), (), s32[]{:S(2)}) async-start(), calls=%async_computation.13 | async-start | bytes 1327104 | tf_op jit(solution)/shard_map/all_gather | solution.py:308
  61.3 188.7 %all-gather.11.cloned.1.call-start = ((), (), s32[]{:S(2)}) async-start(), calls=%async_computation.14 | async-start | bytes 5308416 | tf_op jit(solution)/shard_map/all_gather | solution.py:309
  62.6 3.4 copy-start.1
  63.8 28.9 %copy-start.14 = (f32[768]{0:T(1024)S(1)}, f32[768]{0:T(1024)}, u32[]{:S(2)}) copy-start(f32[768]{0:T(1024)} %param.25) | copy-start | bytes 9220
  63.8 28.9 %copy-start.19 = (f32[768]{0:T(1024)S(1)}, f32[768]{0:T(1024)}, u32[]{:S(2)}) copy-start(f32[768]{0:T(1024)} %param.26) | copy-start | bytes 9220
  104.7 5.3 copy-start.4
  143.7 51.5 %all-to-all-start = ((bf16[8,3,3,16384]{3,1,2,0:T(4,128)(2,1)}), bf16[8,3,3,16384]{3,1,2,0:T(4,128)(2,1)S(1)}, u32[]{:S(2)}, u32[]{:S(2)}) async-start(bf16[8,3,3,16384]{3,1,2,0:T(4,128)(2,1)} %copy.74), calls=%async_computation | async-start | bytes 6291456 | tf_op jit(solution)/shard_map/all_to_all | solution.py:322
  147.4 110.0 %all-gather.13.cloned.1.call-start = ((), (), s32[]{:S(2)}) async-start(), calls=%async_computation.15 | async-start | bytes 5308416 | tf_op jit(solution)/shard_map/all_gather | solution.py:310
  221.8 6.0 copy-start.12
  223.4 18.9 %all-to-all-start.1 = ((bf16[8,3,1,16384]{3,1,2,0:T(4,128)(2,1)}), bf16[8,3,1,16384]{3,1,2,0:T(4,128)(2,1)S(1)}, u32[]{:S(2)}, u32[]{:S(2)}) async-start(bf16[8,3,1,16384]{3,1,2,0:T(4,128)(2,1)} %copy.76), calls=%async_computation.1 | async-start | bytes 2097152 | tf_op jit(solution)/shard_map/all_to_all | solution.py:330
  227.0 158.9 %reduce-scatter.17.cloned.1.call-start = ((), (), s32[]{:S(2)}) async-start(), calls=%async_computation.17 | async-start | bytes 1327104 | tf_op jit(solution)/shard_map/reduce_scatter | solution.py:395
  247.1 2.5 copy-start.5
  249.9 7.4 %copy-start.8 = (bf16[512,768]{1,0:T(8,128)(2,1)S(1)}, bf16[512,768]{1,0:T(8,128)(2,1)}, u32[]{:S(2)}) copy-start(bf16[512,768]{1,0:T(8,128)(2,1)} %param.20) | copy-start | bytes 2359300
  257.3 10.1 %copy-start.16 = (bf16[768,3072]{1,0:T(8,128)(2,1)S(1)}, bf16[768,3072]{1,0:T(8,128)(2,1)}, u32[]{:S(2)}) copy-start(bf16[768,3072]{1,0:T(8,128)(2,1)} %all-gather.11.cloned.1.call-done) | copy-start | bytes 14155780
  267.4 3.1 copy-start.21
  267.4 3.5 copy-start.17
  270.5 15.6 %slice-start = ((s8[6291456]{0:T(1024)(128)(4,1)}), s8[4194304]{0:T(1024)(128)(4,1)S(1)}, s32[]{:S(2)}) async-start(s8[6291456]{0:T(1024)(128)(4,1)} %bitcast.198), calls=%async_computation.25 | async-start | bytes 8388608
  270.9 15.2 %slice-start.1 = ((s8[6291456]{0:T(1024)(128)(4,1)}), s8[2097152]{0:T(1024)(128)(4,1)S(1)}, s32[]{:S(2)}) async-start(s8[6291456]{0:T(1024)(128)(4,1)} %bitcast.198), calls=%async_computation.26 | async-start | bytes 4194304
  270.9 15.2 %copy-start.9 = (bf16[512,768]{1,0:T(8,128)(2,1)S(1)}, bf16[512,768]{1,0:T(8,128)(2,1)}, u32[]{:S(2)}) copy-start(bf16[512,768]{1,0:T(8,128)(2,1)} %param.20) | copy-start | bytes 2359300
  286.1 3.8 copy-start.6
  291.8 179.6 %reduce-scatter.29.cloned.1.call-start = ((), (), s32[]{:S(2)}) async-start(), calls=%async_computation.24 | async-start | bytes 5308416
  305.0 168.7 %reduce-scatter.21.cloned.1.call-start = ((), (), s32[]{:S(2)}) async-start(), calls=%async_computation.19 | async-start | bytes 5308416 | tf_op jit(solution)/shard_map/reduce_scatter | solution.py:401
  348.8 3.1 copy-start
  381.3 48.7 %all-to-all-start.3 = ((bf16[8,3,3,16384]{3,2,1,0:T(4,128)(2,1)}), bf16[8,3,3,16384]{3,2,1,0:T(4,128)(2,1)}, u32[]{:S(2)}, u32[]{:S(2)}) async-start(bf16[8,3,3,16384]{3,2,1,0:T(4,128)(2,1)} %copy.84), calls=%async_computation.3 | async-start | bytes 6291456 | tf_op jit(solution)/shard_map/all_to_all | solution.py:379
  385.8 109.8 %reduce-scatter.27.cloned.1.call-start = ((), (), s32[]{:S(2)}) async-start(), calls=%async_computation.23 | async-start | bytes 245760
  387.6 157.5 %reduce-scatter.15.cloned.1.call-start = ((), (), s32[]{:S(2)}) async-start(), calls=%async_computation.16 | async-start | bytes 3981312 | tf_op jit(solution)/shard_map/reduce_scatter | solution.py:392
  471.3 3.2 copy-start.10
  471.3 128.1 %reduce-scatter.19.cloned.1.call-start = ((), (), s32[]{:S(2)}) async-start(), calls=%async_computation.18 | async-start | bytes 737280 | tf_op jit(solution)/shard_map/reduce_scatter | solution.py:412
  473.7 127.3 %reduce-scatter.23.cloned.1.call-start = ((), (), s32[]{:S(2)}) async-start(), calls=%async_computation.20 | async-start | bytes 737280 | tf_op jit(solution)/shard_map/reduce_scatter | solution.py:415
  474.3 141.2 %reduce-scatter.25.cloned.1.call-start = ((), (), s32[]{:S(2)}) async-start(), calls=%async_computation.22 | async-start | bytes 737280
  (8 other events, 12.2 us)
Sparse Core Ops, SparseCore 0:
  12.6 42.9 all-gather.14
  60.0 32.6 all-gather.6
  95.2 23.9 all-gather.8
  120.8 47.0 all-gather.10
  170.2 49.6 all-gather.12
  291.9 47.9 reduce-scatter.16
  343.3 59.7 reduce-scatter.28
  406.6 66.5 reduce-scatter.20
  476.0 19.6 reduce-scatter.26
  499.0 46.1 reduce-scatter.14
  547.4 22.2 reduce-scatter.18
  571.8 20.6 reduce-scatter.22
  594.8 20.6 reduce-scatter.24

commit v4 on v3

--- a/solution.py
+++ b/solution.py
@@ -24,14 +24,14 @@
     seg_len = seg_ref[pair]
     q_start = qi * bq
     seg_start = (q_start // seg_len) * seg_len
-    query = (q_ref[0, 0].astype(jnp.float32) * scale).astype(jnp.bfloat16)
+    query = (q_ref[0, 0].astype(jnp.float32).T * scale).astype(jnp.bfloat16)
 
     def step(j, carry, masked):
         m_old, l_old, acc = carry
         k_off = pl.multiple_of(j * bk, bk)
-        key = k_ref[0, 0, pl.ds(k_off, bk), :]
-        value = v_ref[0, 0, pl.ds(k_off, bk), :]
-        s = lax.dot_general(query, key, NT_DIMS, preferred_element_type=jnp.float32)
+        key_t = k_ref[0, 0, :, pl.ds(k_off, bk)]
+        value_t = v_ref[0, 0, :, pl.ds(k_off, bk)]
+        s = jnp.dot(query, key_t, preferred_element_type=jnp.float32)
         if masked:
             rows = q_start + lax.broadcasted_iota(jnp.int32, (bq, bk), 0)
             cols = k_off + lax.broadcasted_iota(jnp.int32, (bq, bk), 1)
@@ -40,8 +40,8 @@
         alpha = jnp.exp(m_old - m_new)
         weights = jnp.exp(s - m_new)
         l_new = alpha * l_old + jnp.sum(weights, axis=-1, keepdims=True)
-        acc = alpha * acc + jnp.dot(
-            weights.astype(jnp.bfloat16), value, preferred_element_type=jnp.float32
+        acc = alpha * acc + lax.dot_general(
+            weights.astype(jnp.bfloat16), value_t, NT_DIMS, preferred_element_type=jnp.float32
         )
         return m_new, l_new, acc
 
@@ -51,19 +51,17 @@
         jnp.zeros((bq, HD), jnp.float32),
     )
     j_diag = q_start // bk
-    carry = lax.fori_loop(
-        seg_start // bk, j_diag, lambda j, c: step(j, c, False), carry
-    )
+    carry = lax.fori_loop(seg_start // bk, j_diag, lambda j, c: step(j, c, False), carry)
     for r in range(bq // bk):
         carry = step(j_diag + r, carry, True)
     m_fin, l_fin, acc = carry
-    o_ref[0] = (acc / l_fin).astype(o_ref.dtype)
+    o_ref[0] = (acc / l_fin).T.astype(o_ref.dtype)
     lse = m_fin + jnp.log(l_fin)
     lse_ref[0] = jnp.transpose(jnp.broadcast_to(lse, (bq, 128)))[0:1, :]
 
 
-def attn_forward(qkv, seg_pairs, bq=512, bk=512):
-    pairs, _, seq_len, head_size = qkv.shape
+def attn_forward(qkv_t, seg_pairs, bq=512, bk=512):
+    pairs, _, head_size, seq_len = qkv_t.shape
     scale = head_size ** (-0.5)
     n_q = seq_len // bq
     blocks_done = pairs * (seq_len // bk) * (seq_len // bk + 1) // 2
@@ -76,12 +74,12 @@
         num_scalar_prefetch=1,
         grid=(pairs, n_q),
         in_specs=[
-            pl.BlockSpec((1, 1, bq, head_size), lambda p, i, seg: (p, 0, i, 0)),
-            pl.BlockSpec((1, 1, seq_len, head_size), lambda p, i, seg: (p, 1, 0, 0)),
-            pl.BlockSpec((1, 1, seq_len, head_size), lambda p, i, seg: (p, 2, 0, 0)),
+            pl.BlockSpec((1, 1, head_size, bq), lambda p, i, seg: (p, 0, 0, i)),
+            pl.BlockSpec((1, 1, head_size, seq_len), lambda p, i, seg: (p, 1, 0, 0)),
+            pl.BlockSpec((1, 1, head_size, seq_len), lambda p, i, seg: (p, 2, 0, 0)),
         ],
         out_specs=[
-            pl.BlockSpec((1, bq, head_size), lambda p, i, seg: (p, i, 0)),
+            pl.BlockSpec((1, head_size, bq), lambda p, i, seg: (p, 0, i)),
             pl.BlockSpec((1, 1, bq), lambda p, i, seg: (p, 0, i)),
         ],
     )
@@ -89,15 +87,15 @@
         functools.partial(fwd_kernel, bq=bq, bk=bk, scale=scale),
         grid_spec=grid_spec,
         out_shape=[
-            jax.ShapeDtypeStruct((pairs, seq_len, head_size), jnp.bfloat16),
+            jax.ShapeDtypeStruct((pairs, head_size, seq_len), jnp.bfloat16),
             jax.ShapeDtypeStruct((pairs, 1, seq_len), jnp.float32),
         ],
         cost_estimate=cost,
         name="attn_fwd",
-    )(seg_pairs, qkv, qkv, qkv)
-
-
-def bwd_kernel(seg_ref, q_ref, k_ref, v_ref, do_ref, lse_ref, dl_ref, out_ref, dq_acc, *, bk, bq, scale):
+    )(seg_pairs, qkv_t, qkv_t, qkv_t)
+
+
+def bwd_kernel(seg_ref, q_ref, k_ref, v_ref, do_ref, o_ref, lse_ref, out_ref, dq_acc, *, bk, bq, scale):
     pair = pl.program_id(0)
     kj = pl.program_id(1)
 
@@ -108,74 +106,78 @@
     seg_len = seg_ref[pair]
     k_start = kj * bk
     seg_end = (k_start // seg_len + 1) * seg_len
-    key = k_ref[0, 0]
-    value = (v_ref[0, 0].astype(jnp.float32) * scale).astype(jnp.bfloat16)
+    key_t = k_ref[0, 0]
+    key = key_t.astype(jnp.float32).T.astype(jnp.bfloat16)
+    value_s = (v_ref[0, 0].astype(jnp.float32).T * scale).astype(jnp.bfloat16)
 
     def step(i, carry, masked):
-        dk, dv = carry
+        dk_t, dv_t = carry
         q_off = pl.multiple_of(i * bq, bq)
-        query = q_ref[0, 0, pl.ds(q_off, bq), :]
-        query_s = (query.astype(jnp.float32) * scale).astype(jnp.bfloat16)
-        dout = do_ref[0, pl.ds(q_off, bq), :]
+        query_t = q_ref[0, 0, :, pl.ds(q_off, bq)]
+        query_ts = (query_t.astype(jnp.float32) * scale).astype(jnp.bfloat16)
+        dout_t = do_ref[0, :, pl.ds(q_off, bq)]
+        out_t = o_ref[0, :, pl.ds(q_off, bq)]
         lse = lse_ref[0, :, pl.ds(q_off, bq)]
-        delta = dl_ref[0, :, pl.ds(q_off, bq)] * scale
-        s_t = lax.dot_general(key, query_s, NT_DIMS, preferred_element_type=jnp.float32)
+        delta = jnp.sum(
+            dout_t.astype(jnp.float32) * out_t.astype(jnp.float32), axis=0, keepdims=True
+        ) * scale
+        s_t = jnp.dot(key, query_ts, preferred_element_type=jnp.float32)
         if masked:
             keys_at = k_start + lax.broadcasted_iota(jnp.int32, (bk, bq), 0)
             queries_at = q_off + lax.broadcasted_iota(jnp.int32, (bk, bq), 1)
             s_t = jnp.where(keys_at <= queries_at, s_t, MASKED)
         p_t = jnp.exp(s_t - lse)
-        dv = dv + jnp.dot(p_t.astype(jnp.bfloat16), dout, preferred_element_type=jnp.float32)
-        dp_t = lax.dot_general(value, dout, NT_DIMS, preferred_element_type=jnp.float32)
-        ds_t = p_t * (dp_t - delta)
-        dk = dk + jnp.dot(ds_t.astype(jnp.bfloat16), query, preferred_element_type=jnp.float32)
-        dq_acc[pl.ds(q_off, bq), :] += jnp.dot(
-            ds_t.T.astype(jnp.bfloat16), key, preferred_element_type=jnp.float32
+        dv_t = dv_t + lax.dot_general(
+            dout_t, p_t.astype(jnp.bfloat16), NT_DIMS, preferred_element_type=jnp.float32
         )
-        return dk, dv
-
-    carry = (jnp.zeros((bk, HD), jnp.float32), jnp.zeros((bk, HD), jnp.float32))
+        dp_t = jnp.dot(value_s, dout_t, preferred_element_type=jnp.float32)
+        ds_t = (p_t * (dp_t - delta)).astype(jnp.bfloat16)
+        dk_t = dk_t + lax.dot_general(query_t, ds_t, NT_DIMS, preferred_element_type=jnp.float32)
+        dq_acc[:, pl.ds(q_off, bq)] += jnp.dot(key_t, ds_t, preferred_element_type=jnp.float32)
+        return dk_t, dv_t
+
+    carry = (jnp.zeros((HD, bk), jnp.float32), jnp.zeros((HD, bk), jnp.float32))
     for r in range(bk // bq):
         carry = step(k_start // bq + r, carry, True)
-    dk, dv = lax.fori_loop(
+    dk_t, dv_t = lax.fori_loop(
         (k_start + bk) // bq, seg_end // bq, lambda i, c: step(i, c, False), carry
     )
-    out_ref[0, 0] = dq_acc[pl.ds(pl.multiple_of(k_start, bk), bk), :].astype(out_ref.dtype)
-    out_ref[0, 1] = dk.astype(out_ref.dtype)
-    out_ref[0, 2] = dv.astype(out_ref.dtype)
-
-
-def attn_backward(qkv, dout, lse, delta, seg_pairs, bk=512, bq=512):
-    pairs, _, seq_len, head_size = qkv.shape
+    out_ref[0, 0] = dq_acc[:, pl.ds(pl.multiple_of(k_start, bk), bk)].astype(out_ref.dtype)
+    out_ref[0, 1] = dk_t.astype(out_ref.dtype)
+    out_ref[0, 2] = dv_t.astype(out_ref.dtype)
+
+
+def attn_backward(qkv_t, dout_t, out_t, lse, seg_pairs, bk=512, bq=512):
+    pairs, _, head_size, seq_len = qkv_t.shape
     scale = head_size ** (-0.5)
     n_k = seq_len // bk
     blocks_done = pairs * (seq_len // bq) * (seq_len // bq + 1) // 2
     cost = pl.CostEstimate(
         flops=10 * blocks_done * bq * bq * head_size,
         transcendentals=blocks_done * bq * bq,
-        bytes_accessed=pairs * seq_len * head_size * 2 * 7 + pairs * seq_len * 8,
+        bytes_accessed=pairs * seq_len * head_size * 2 * 8 + pairs * seq_len * 4,
     )
     grid_spec = pltpu.PrefetchScalarGridSpec(
         num_scalar_prefetch=1,
         grid=(pairs, n_k),
         in_specs=[
-            pl.BlockSpec((1, 1, seq_len, head_size), lambda p, j, seg: (p, 0, 0, 0)),
-            pl.BlockSpec((1, 1, bk, head_size), lambda p, j, seg: (p, 1, j, 0)),
-            pl.BlockSpec((1, 1, bk, head_size), lambda p, j, seg: (p, 2, j, 0)),
-            pl.BlockSpec((1, seq_len, head_size), lambda p, j, seg: (p, 0, 0)),
-            pl.BlockSpec((1, 1, seq_len), lambda p, j, seg: (p, 0, 0)),
+            pl.BlockSpec((1, 1, head_size, seq_len), lambda p, j, seg: (p, 0, 0, 0)),
+            pl.BlockSpec((1, 1, head_size, bk), lambda p, j, seg: (p, 1, 0, j)),
+            pl.BlockSpec((1, 1, head_size, bk), lambda p, j, seg: (p, 2, 0, j)),
+            pl.BlockSpec((1, head_size, seq_len), lambda p, j, seg: (p, 0, 0)),
+            pl.BlockSpec((1, head_size, seq_len), lambda p, j, seg: (p, 0, 0)),
             pl.BlockSpec((1, 1, seq_len), lambda p, j, seg: (p, 0, 0)),
         ],
-        out_specs=pl.BlockSpec((1, 3, bk, head_size), lambda p, j, seg: (p, 0, j, 0)),
-        scratch_shapes=[pltpu.VMEM((seq_len, head_size), jnp.float32)],
+        out_specs=pl.BlockSpec((1, 3, head_size, bk), lambda p, j, seg: (p, 0, 0, j)),
+        scratch_shapes=[pltpu.VMEM((head_size, seq_len), jnp.float32)],
     )
     return pl.pallas_call(
         functools.partial(bwd_kernel, bk=bk, bq=bq, scale=scale),
         grid_spec=grid_spec,
-        out_shape=jax.ShapeDtypeStruct((pairs, 3, seq_len, head_size), jnp.bfloat16),
+        out_shape=jax.ShapeDtypeStruct((pairs, 3, head_size, seq_len), jnp.bfloat16),
         cost_estimate=cost,
         name="attn_bwd",
-    )(seg_pairs, qkv, qkv, qkv, dout, lse, delta)
+    )(seg_pairs, qkv_t, qkv_t, qkv_t, dout_t, out_t, lse)
 
 
 def norm_rows(values, gain, shift):
@@ -216,42 +218,6 @@
     sin_part = sine_tab[..., None, :]
     return jnp.concatenate(
         [front * cos_part + behind * sin_part, behind * cos_part - front * sin_part], axis=-1
-    )
-
-
-def to_pairs(stacked, order_row, n_seq, per_dev):
-    slot_count, piece_len, part_count, head_count, head_size = stacked.shape
-    reordered = jnp.transpose(stacked, (0, 3, 2, 1, 4)).reshape(
-        slot_count * head_count, part_count, piece_len * head_size
-    )
-    return jnp.take(reordered, order_row, axis=0).reshape(
-        n_seq, per_dev, part_count, piece_len * head_size
-    )
-
-
-def pairs_whole(incoming, head_size):
-    n_seq, per_dev, part_count, flat_len = incoming.shape
-    piece_len = flat_len // head_size
-    reordered = jnp.transpose(
-        incoming.reshape(n_seq, per_dev, part_count, piece_len, head_size), (1, 2, 0, 3, 4)
-    )
-    return reordered.reshape(per_dev, part_count, n_seq * piece_len, head_size)
-
-
-def pairs_split(whole_seq, n_seq):
-    per_dev, part_count, seq_len, head_size = whole_seq.shape
-    return jnp.transpose(
-        whole_seq.reshape(per_dev, part_count, n_seq, seq_len // n_seq * head_size), (2, 0, 1, 3)
-    )
-
-
-def tokens_back(incoming, inverse, slot_count, head_size):
-    n_seq, per_dev, part_count, flat_len = incoming.shape
-    piece_len = flat_len // head_size
-    ordered = jnp.take(incoming.reshape(n_seq * per_dev, part_count, flat_len), inverse, axis=0)
-    head_count = n_seq * per_dev // slot_count
-    return jnp.transpose(
-        ordered.reshape(slot_count, head_count, part_count, piece_len, head_size), (0, 3, 2, 1, 4)
     )
 
 
@@ -287,22 +253,17 @@
     my_start = my_index * piece_len
     cosine = lax.dynamic_slice_in_dim(jnp.cos(angles), my_start, piece_len, 1)
     sine_tab = lax.dynamic_slice_in_dim(jnp.sin(angles), my_start, piece_len, 1)
+    head_groups = HEADS // per_dev
     order_row = pair_order[0]
-    inverse = (
-        jnp.zeros((pair_count,), jnp.int32)
-        .at[order_row]
-        .set(jnp.arange(pair_count, dtype=jnp.int32))
-    )
     held_pairs = lax.dynamic_slice_in_dim(order_row, my_index * per_dev, per_dev, 0)
-    shards = (qkv_weight, proj_weight, up_weight, down_weight)
-    gathered = lax.all_gather(
-        jnp.concatenate([w.reshape(-1) for w in shards]), "batch", axis=0
-    )
-    row_parts = []
-    offset = 0
-    for w in shards:
-        row_parts.append(gathered[:, offset : offset + w.size].reshape(-1, w.shape[1]))
-        offset += w.size
+    my_pairs = my_index * per_dev + jnp.arange(per_dev, dtype=jnp.int32)
+    seg_pairs = jnp.take(seg_len, my_pairs // HEADS).astype(jnp.int32)
+    row_parts = (
+        lax.all_gather(qkv_weight, "batch", axis=0, tiled=True),
+        lax.all_gather(proj_weight, "batch", axis=0, tiled=True),
+        lax.all_gather(up_weight, "batch", axis=0, tiled=True),
+        lax.all_gather(down_weight, "batch", axis=0, tiled=True),
+    )
     w_qkv, w_proj, w_up, w_down = (
         lax.all_gather(row_parts[0], "seq", axis=1, tiled=True),
         lax.all_gather(row_parts[1], "seq", axis=1, tiled=True),
@@ -319,18 +280,17 @@
     )
     values_in = qkv_out[:, 2 * D :].reshape(slot_count, piece_len, HEADS, HD)
     stacked = jnp.stack([queries, keys_rot, values_in], axis=2).astype(jnp.bfloat16)
-    incoming = lax.all_to_all(
-        to_pairs(stacked, order_row, n_seq, per_dev), "seq", split_axis=0, concat_axis=0, tiled=True
-    )
-    sequences = pairs_whole(incoming, HD)
-    seg_pairs = jnp.take(seg_len, held_pairs // HEADS).astype(jnp.int32)
-    attn_out, lse_rows = attn_forward(sequences, seg_pairs)
-    attended_pairs = attn_out.reshape(per_dev, 1, SLOT, HD)
-    log_total = lse_rows.reshape(per_dev, SLOT)
-    returned = lax.all_to_all(
-        pairs_split(attended_pairs, n_seq), "seq", split_axis=0, concat_axis=0, tiled=True
-    )
-    attended = tokens_back(returned, inverse, slot_count, HD).reshape(row_count, D)
+    send = jnp.transpose(
+        stacked.reshape(slot_count, piece_len, 3, head_groups, per_dev, HD), (0, 3, 4, 2, 5, 1)
+    ).reshape(n_seq, per_dev, 3, HD, piece_len)
+    incoming = lax.all_to_all(send, "seq", split_axis=0, concat_axis=0, tiled=True)
+    qkv_t = jnp.transpose(incoming, (1, 2, 3, 0, 4)).reshape(per_dev, 3, HD, SLOT)
+    attn_t, lse_rows = attn_forward(qkv_t, seg_pairs)
+    back = jnp.transpose(attn_t.reshape(per_dev, HD, n_seq, piece_len), (2, 0, 1, 3))
+    returned = lax.all_to_all(back, "seq", split_axis=0, concat_axis=0, tiled=True)
+    attended = jnp.transpose(
+        returned.reshape(slot_count, head_groups, per_dev, HD, piece_len), (0, 4, 1, 2, 3)
+    ).reshape(row_count, D)
     middle = inputs32 + jnp.dot(attended, w_proj, preferred_element_type=jnp.float32)
     norm2_out, normed2, inv_std2 = norm_rows(middle, norm2_gain, norm2_bias)
     norm2_low = norm2_out.astype(jnp.bfloat16)
@@ -363,23 +323,19 @@
     dattended = jnp.einsum(
         "ne,de->nd", dmiddle_low, w_proj, preferred_element_type=jnp.float32
     ).astype(jnp.bfloat16)
-    dattn_tokens = dattended.reshape(slot_count, piece_len, 1, HEADS, HD)
-    dattn_in = lax.all_to_all(
-        to_pairs(dattn_tokens, order_row, n_seq, per_dev),
-        "seq",
-        split_axis=0,
-        concat_axis=0,
-        tiled=True,
-    )
-    dout_pairs = pairs_whole(dattn_in, HD)[:, 0]
-    delta = jnp.sum(
-        dout_pairs.astype(jnp.float32) * attn_out.astype(jnp.float32), axis=-1
-    ).reshape(per_dev, 1, SLOT)
-    dpairs = attn_backward(sequences, dout_pairs, lse_rows, delta, seg_pairs)
-    dreturned = lax.all_to_all(
-        pairs_split(dpairs, n_seq), "seq", split_axis=0, concat_axis=0, tiled=True
-    )
-    dtokens = tokens_back(dreturned, inverse, slot_count, HD)
+    dsend = jnp.transpose(
+        dattended.reshape(slot_count, piece_len, head_groups, per_dev, HD), (0, 2, 3, 4, 1)
+    ).reshape(n_seq, per_dev, HD, piece_len)
+    dattn_in = lax.all_to_all(dsend, "seq", split_axis=0, concat_axis=0, tiled=True)
+    dout_t = jnp.transpose(dattn_in, (1, 2, 0, 3)).reshape(per_dev, HD, SLOT)
+    dpairs = attn_backward(qkv_t, dout_t, attn_t, lse_rows, seg_pairs)
+    dback = jnp.transpose(
+        dpairs.reshape(per_dev, 3, HD, n_seq, piece_len), (3, 0, 1, 2, 4)
+    )
+    dreturned = lax.all_to_all(dback, "seq", split_axis=0, concat_axis=0, tiled=True)
+    dtokens = jnp.transpose(
+        dreturned.reshape(slot_count, head_groups, per_dev, 3, HD, piece_len), (0, 5, 3, 1, 2, 4)
+    ).reshape(slot_count, piece_len, 3, HEADS, HD)
     dq_rows = unrotate(dtokens[:, :, 0].astype(jnp.float32), cosine, sine_tab).reshape(row_count, D)
     dk_rows = unrotate(dtokens[:, :, 1].astype(jnp.float32), cosine, sine_tab).reshape(row_count, D)
     dv_rows = dtokens[:, :, 2].astype(jnp.float32).reshape(row_count, D)
@@ -427,7 +383,8 @@
         small_sums[k * D : (k + 1) * D] for k in range(4)
     )
     dwa_grad = small_sums[4 * D :]
-    row_lse = log_total.reshape(1, per_dev, SLOT)
+    lse_all = lax.all_gather(lse_rows.reshape(per_dev, SLOT), "seq", axis=0, tiled=True)
+    row_lse = jnp.take(lse_all, held_pairs, axis=0).reshape(1, per_dev, SLOT)
     return (
         block_output,
         input_grad,

time: 634 us -> 583 us (0.920)
  local copies, waits for them, and re-layouts: 151 us -> 59.4 us
  blocking collectives: 62.2 us -> 133 us
  waiting for transfers between devices: 239 us -> 219 us
  other arithmetic: 43.2 us -> 29.3 us
    all_gather x0 -> x5, blocking collectives: none -> 75 us  [the longest x1 18.6 us: local(): lax.all_gather(qkv_weight, 'batch', axis=0, tiled=True)]
    reshape x23 -> x6, local copies, waits for them, and re-layouts: 66.7 us -> 10.2 us  [the longest x1 3.68 us: local(): dpairs.reshape(per_dev, 3, HD, n_seq, piece_len)]
    reduce_scatter x1, waiting for transfers between devices: 0.02 us -> 49.8 us  [local(): lax.psum_scatter(down_local.astype(jnp.bfloat16), 'seq', scatter_dimensio...]
    all_gather x1 -> x0, waiting for transfers between devices: 43.1 us -> none  [local(): lax.all_gather(jnp.concatenate([w.reshape(-1) for w in shards]), 'batch',...]
    all_gather x1, waiting for transfers between devices: 26.2 us -> 0.02 us  [local(): lax.all_gather(row_parts[0], 'seq', axis=1, tiled=True)]
    gather x5 -> x2, local copies, waits for them, and re-layouts: 17.1 us -> 1.21 us  [the longest x1 0.64 us: local(): seg_pairs = jnp.take(seg_len, my_pairs // HEADS).astype(jnp.int32)]
    transpose x4 -> x3, local copies, waits for them, and re-layouts: 10.2 us -> 1.23 us  [the longest x1 0.81 us: local(): jnp.transpose(returned.reshape(slot_count, head_groups, per_dev, HD, piec...]
    select_n x9 -> x4, other arithmetic: 8.4 us -> 0.7 us  [the longest x2 0.55 us: local(): seg_pairs = jnp.take(seg_len, my_pairs // HEADS).astype(jnp.int32)]
  transfers between devices with their start and end apart: 16 -> 15, of which waited for: 8 -> 8; matrix products, arithmetic and copies ran while one was open for 35% -> 21% of each run, Pallas kernels for 5% -> 5%
where the time goes in v4:
time: 583 us; the launch traced here: 574 us
  waiting for transfers between devices  219 us (38%)
  blocking collectives  133 us (23%)
  matrix products  71.5 us (12%)
  local copies, waits for them, and re-layouts  59.4 us (10%)
  other arithmetic  29.3 us (5%)
  Pallas kernels  28.7 us (5%)
  starting transfers between devices  17.9 us (3%)
  between operations  15.3 us (3%)
    reduce_scatter x1, waiting for transfers between devices, local(): lax.psum_scatter(down_local.astype(jnp.bfloat16), 'seq', scatter_dimensio...  49.8 us
    reduce_scatter x1, waiting for transfers between devices, local(): lax.psum_scatter(qkv_local.astype(jnp.bfloat16), 'seq', scatter_dimension...  41.9 us
    all_to_all x1, waiting for transfers between devices, local(): lax.all_to_all(send, 'seq', split_axis=0, concat_axis=0, tiled=True)  40.8 us
    all_to_all x1, waiting for transfers between devices, local(): lax.all_to_all(dback, 'seq', split_axis=0, concat_axis=0, tiled=True)  39.9 us
    unnamed x15, waiting for transfers between devices  27.9 us
    psum x1, blocking collectives, local(): lax.psum(jnp.concatenate([gain1_local, bias1_local, gain2_local, bias2_lo...  23.5 us
    unnamed x64, local copies, waits for them, and re-layouts  21.3 us
    psum x1, blocking collectives, local(): lax.psum(lax.psum(jnp.concatenate([gain1_local, bias1_local, gain2_local,...  18.7 us
  transfers between devices with their start and end apart: 15, of which 8 were waited for; matrix products, arithmetic and copies ran while one was open for 21% of the time, Pallas kernels for 5%

profile of v4, /device:TPU:0, one launch (start us, length us, event | category | flops | bytes accessed | tf_op | source)
XLA Modules:
  0.0 573.7 jit_solution(888069531107403374)
XLA Ops:
  7.2 18.6 %all_gather.27 = bf16[768,288]{1,0:T(8,128)(2,1)S(1)} all-gather(bf16[192,288]{1,0:T(8,128)(2,1)} %param.17), channel_id=1, replica_groups=mesh['batch'=4,'seq'=8] {'batch'}, dimensions={0}, use_global_device_ids=true | all-gather | bytes 552960 | tf_op jit(solution)/shard_map/all_gather | solution.py:262
  26.9 13.6 %all_gather.29 = bf16[768,96]{1,0:T(8,128)(2,1)S(1)} all-gather(bf16[192,96]{1,0:T(8,128)(2,1)S(1)} %copy-done.11), channel_id=1, replica_groups=mesh['batch'=4,'seq'=8] {'batch'}, dimensions={0}, use_global_device_ids=true | all-gather | bytes 184320 | tf_op jit(solution)/shard_map/all_gather | solution.py:263
  41.4 17.5 %all_gather.31 = bf16[768,384]{1,0:T(8,128)(2,1)} all-gather(bf16[192,384]{1,0:T(8,128)(2,1)S(1)} %copy-done.8), channel_id=1, replica_groups=mesh['batch'=4,'seq'=8] {'batch'}, dimensions={0}, use_global_device_ids=true | all-gather | bytes 737280 | tf_op jit(solution)/shard_map/all_gather | solution.py:264
  59.0 15.8 %all_gather.33 = bf16[3072,96]{0,1:T(8,128)(2,1)} all-gather(bf16[768,96]{0,1:T(8,128)(2,1)S(1)} %copy-done.9), channel_id=1, replica_groups=mesh['batch'=4,'seq'=8] {'batch'}, dimensions={0}, use_global_device_ids=true | all-gather | bytes 737280 | tf_op jit(solution)/shard_map/all_gather | solution.py:265
  77.6 4.2 fusion.55
  102.6 4.1 all-to-all-start
  107.9 40.8 %all-to-all-done = bf16[8,3,3,64,256]{4,3,2,1,0:T(8,128)(2,1)S(1)} async-done(((bf16[8,3,3,64,256]{4,3,2,1,0:T(8,128)(2,1)}), bf16[8,3,3,64,256]{4,3,2,1,0:T(8,128)(2,1)S(1)}, u32[]{:S(2)}, u32[]{:S(2)}) %all-to-all-start) | async-done | bytes 2359328 | tf_op jit(solution)/shard_map/all_to_all | solution.py:286
  150.4 13.3 %attn_fwd.1 = (bf16[3,64,2048]{2,1,0:T(8,128)(2,1)}, f32[3,1,2048]{2,1,0:T(1,128)}) custom-call(s32[3]{0:T(128)} %and_select_fusion.2.seg_ref, bf16[3,3,64,2048]{3,2,1,0:T(8,128)(2,1)} %bitcast.187, bf16[3,3,64,2048]{3,2,1,0:T(8,128)(2,1)} %bitcast.188, bf16[3,3,64,2048]{3,2,1,0:T(8,128)(2,1)} %bitcast.189), custom_call_target="tpu_custom_call" | custom-call | flops 2013265920 | bytes 3170304 | tf_op jit(solution)/shard_map/attn_fwd/pallas_call | solution.py:86
  165.8 5.7 %all-to-all-start.1 = ((bf16[8,3,64,256]{3,2,1,0:T(8,128)(2,1)}), bf16[8,3,64,256]{3,2,1,0:T(8,128)(2,1)S(1)}, u32[]{:S(2)}, u32[]{:S(2)}) async-start(bf16[8,3,64,256]{3,2,1,0:T(8,128)(2,1)} %bitcast.160), calls=%async_computation.1 | async-start | bytes 1572864 | tf_op jit(solution)/shard_map/all_to_all | solution.py:290
  172.3 18.2 %all-to-all-done.1 = bf16[8,3,64,256]{3,2,1,0:T(8,128)(2,1)S(1)} async-done(((bf16[8,3,64,256]{3,2,1,0:T(8,128)(2,1)}), bf16[8,3,64,256]{3,2,1,0:T(8,128)(2,1)S(1)}, u32[]{:S(2)}, u32[]{:S(2)}) %all-to-all-start.1) | async-done | bytes 786464 | tf_op jit(solution)/shard_map/all_to_all | solution.py:290
  194.4 7.0 %fusion.57 = f32[512,3072]{1,0:T(8,128)} fusion(bf16[768,3072]{1,0:T(8,128)(2,1)} %all-gather.10.cloned.1.call-done, f32[512,768]{1,0:T(8,128)S(1)} %get-tuple-element.134, f32[768]{0:T(1024)S(1)} %copy-done.17, f32[768]{0:T(1024)S(1)} %copy-done.13, f32[512]{0:T(512)S(1)} %add_rsqrt_fusion, f32[512]{0:T(512)S(1)} %broadcast_multiply_fusion.5), kind=kOutput, calls=%fused_computation.141 | convolution fusion | flops 2417885184 | bytes 12593152 | tf_op jit(solution)/shard_map/dot_general | solution.py:297
  201.5 9.5 %fusion.6 = bf16[512,3072]{1,0:T(8,128)(2,1)S(1)} fusion(f32[512,3072]{1,0:T(8,128)} %fusion.57, bf16[3072,768]{0,1:T(8,128)(2,1)} %all-gather.12.cloned.1.call-done, bf16[512,768]{1,0:T(8,128)(2,1)} %param.16, f32[]{:T(128)} %bitcast), kind=kOutput, calls=%fused_computation.11 | convolution fusion | flops 2448556032 | bytes 14942212 | tf_op jit(solution)/shard_map/nd,fd->nf/dot_general | solution.py:315
  214.5 15.2 %fusion.32 = (bf16[512,768]{1,0:T(8,128)(2,1)}, f32[512,768]{1,0:T(8,128)S(1)}) fusion(f32[]{:T(128)} %bitcast.26, f32[]{:T(128)} %bitcast.24, f32[]{:T(128)} %bitcast.22, f32[]{:T(128)} %bitcast.20, f32[]{:T(128)} %bitcast.18, f32[]{:T(128)} %bitcast.16, f32[]{:T(128)} %bitcast.14, f32[]{:T(128)} %bitcast.12, f32[]{:T(128)} %bitcast, ...), kind=kOutput, calls=%fused_computation.64 | convolution fusion | flops 2440691712 | bytes 21233700 | tf_op jit(solution)/shard_map/dot_general | solution.py:300
  229.7 5.0 fusion.40
  236.8 7.4 %convolution_convert_fusion.2 = bf16[768,3072]{1,0:T(8,128)(2,1)} fusion(bf16[512,3072]{1,0:T(8,128)(2,1)} %copy-done.21, f32[512,768]{1,0:T(8,128)} %copy-done.3, f32[768]{0:T(1024)S(1)} %copy-done.17, f32[768]{0:T(1024)S(1)} %copy-done.13, f32[512]{0:T(512)S(1)} %add_rsqrt_fusion, f32[512]{0:T(512)S(1)} %broadcast_multiply_fusion.5), kind=kOutput, calls=%fused_computation.15 | convolution fusion | flops 2420244480 | bytes 9447424 | tf_op jit(solution)/shard_map/nd,nf->df/dot_general | solution.py:317
  244.1 6.7 %copy.119 = bf16[768,3072]{0,1:T(8,128)(2,1)} copy(bf16[768,3072]{1,0:T(8,128)(2,1)} %convolution_convert_fusion.2) | data formatting | bytes 9437184
  252.0 8.8 %convolution_convert_fusion.1 = bf16[3072,768]{0,1:T(8,128)(2,1)} fusion(bf16[512,768]{1,0:T(8,128)(2,1)S(1)} %copy-done.5, f32[]{:T(128)} %bitcast, f32[512,3072]{1,0:T(8,128)} %fusion.57), kind=kOutput, calls=%fused_computation.14 | convolution fusion | flops 2433613824 | bytes 11796484 | tf_op jit(solution)/shard_map/nf,nd->fd/dot_general | solution.py:314
  263.5 15.8 %all_to_all.20 = bf16[8,3,64,256]{3,2,1,0:T(8,128)(2,1)S(1)} all-to-all(bf16[8,3,64,256]{3,2,1,0:T(8,128)(2,1)S(1)} %bitcast.183), channel_id=1, replica_groups=mesh['batch'=4,'seq'=8] {'seq'}, dimensions={0} | all-to-all | bytes 1572864 | tf_op jit(solution)/shard_map/all_to_all | solution.py:329
  280.3 15.4 %attn_bwd.1 = bf16[3,3,64,2048]{3,2,1,0:T(8,128)(2,1)} custom-call(s32[3]{0:T(128)} %and_select_fusion.2.seg_ref, bf16[3,3,64,2048]{3,2,1,0:T(8,128)(2,1)} %bitcast.190, bf16[3,3,64,2048]{3,2,1,0:T(8,128)(2,1)} %bitcast.191, bf16[3,3,64,2048]{3,2,1,0:T(8,128)(2,1)} %bitcast.192, bf16[3,64,2048]{2,1,0:T(8,128)(2,1)} %bitcast.196, ...), custom_call_target="tpu_custom_call" | custom-call | flops 5033164800 | bytes 6316032 | tf_op jit(solution)/shard_map/attn_bwd/pallas_call | solution.py:174
  299.4 7.2 %all-to-all-start.3 = ((bf16[8,3,3,64,256]{4,3,2,1,0:T(8,128)(2,1)}), bf16[8,3,3,64,256]{4,3,2,1,0:T(8,128)(2,1)S(1)}, u32[]{:S(2)}, u32[]{:S(2)}) async-start(bf16[8,3,3,64,256]{4,3,2,1,0:T(8,128)(2,1)} %bitcast.166), calls=%async_computation.3 | async-start | bytes 4718592 | tf_op jit(solution)/shard_map/all_to_all | solution.py:335
  308.7 39.9 %all-to-all-done.3 = bf16[8,3,3,64,256]{4,3,2,1,0:T(8,128)(2,1)S(1)} async-done(((bf16[8,3,3,64,256]{4,3,2,1,0:T(8,128)(2,1)}), bf16[8,3,3,64,256]{4,3,2,1,0:T(8,128)(2,1)S(1)}, u32[]{:S(2)}, u32[]{:S(2)}) %all-to-all-start.3) | async-done | bytes 2359328 | tf_op jit(solution)/shard_map/all_to_all | solution.py:335
  357.5 4.0 convolution_convert_fusion
  367.9 4.5 multiply_convert_fusion
  372.4 49.8 %reduce-scatter.21.cloned.1.call-done = bf16[3072,96]{0,1:T(8,128)(2,1)} async-done(((bf16[3072,768]{0,1:T(8,128)(2,1)}), bf16[3072,96]{0,1:T(8,128)(2,1)}) %reduce-scatter.21.cloned.1.call-update) | async-done | bytes 589840 | tf_op jit(solution)/shard_map/reduce_scatter | solution.py:357
  422.4 9.5 %all-gather = f32[24,1,2048]{2,1,0:T(1,128)S(1)} all-gather(f32[3,1,2048]{2,1,0:T(1,128)S(1)} %copy-done.12), channel_id=2, replica_groups=mesh['batch'=4,'seq'=8] {'seq'}, dimensions={0}, use_global_device_ids=true | all-gather | bytes 221184 | tf_op jit(solution)/shard_map/all_gather | solution.py:386
  433.2 11.5 %reduce-scatter.27.cloned.1.call-done = bf16[192,96]{1,0:T(8,128)(2,1)} async-done(((bf16[768,96]{1,0:T(8,128)(2,1)}), bf16[192,96]{1,0:T(8,128)(2,1)}) %reduce-scatter.27.cloned.1.call-update) | async-done | bytes 36880
  446.3 6.2 %fusion.22 = (f32[768]{0:T(1024)S(1)}, f32[512]{0:T(512)S(1)}, f32[512]{0:T(512)S(1)}, f32[768]{0:T(1024)S(1)}, f32[512,768]{1,0:T(8,128)}) fusion(bf16[512,768]{1,0:T(8,128)(2,1)S(1)} %copy-done.2, f32[512]{0:T(512)S(1)} %add_rsqrt_fusion.1, f32[512]{0:T(512)S(1)} %broadcast_multiply_fusion.6, f32[768]{0:T(1024)S(1)} %copy-done.14, ...), kind=kOutput, calls=%fused_computation.54 | convolution fusion | flops 1815868928 | bytes 8274944 | tf_op jit(solution)/shard_map/nf,df->nd/dot_general | solution.py:344
  452.6 41.9 %reduce-scatter.15.cloned.1.call-done = bf16[768,288]{0,1:T(8,128)(2,1)} async-done(((bf16[768,2304]{0,1:T(8,128)(2,1)}), bf16[768,288]{0,1:T(8,128)(2,1)}) %reduce-scatter.15.cloned.1.call-update) | async-done | bytes 442384 | tf_op jit(solution)/shard_map/reduce_scatter | solution.py:348
  496.6 5.7 concatenate.30
  502.2 23.5 %psum.14 = f32[3081]{0:T(1024)S(1)} all-reduce(f32[3081]{0:T(1024)S(1)} %concatenate.30), channel_id=1, replica_groups=mesh['batch'=4,'seq'=8] {'seq'}, use_global_device_ids=true, to_apply=%region_29.30 | all-reduce | flops 3081 | bytes 24648 | tf_op jit(solution)/shard_map/psum | solution.py:376
  525.7 18.7 %psum.15 = f32[3081]{0:T(1024)S(1)} all-reduce(f32[3081]{0:T(1024)S(1)} %psum.14), channel_id=1, replica_groups=mesh['batch'=4,'seq'=8] {'batch'}, use_global_device_ids=true, to_apply=%region_30.31 | all-reduce | flops 3081 | bytes 24648 | tf_op jit(solution)/shard_map/psum | solution.py:375
  551.7 12.8 %reduce-scatter.25.cloned.1.call-done = bf16[192,288]{1,0:T(8,128)(2,1)} async-done(((bf16[768,288]{1,0:T(8,128)(2,1)}), bf16[192,288]{1,0:T(8,128)(2,1)}) %reduce-scatter.25.cloned.1.call-update) | async-done | bytes 110608
  (168 shorter events, 80.5 us)
Async XLA Ops:
  7.2 19.7 %copy-start.11 = (bf16[192,96]{1,0:T(8,128)(2,1)S(1)}, bf16[192,96]{1,0:T(8,128)(2,1)}, u32[]{:S(2)}) copy-start(bf16[192,96]{1,0:T(8,128)(2,1)} %param.18) | copy-start | bytes 110596
  7.2 34.2 %copy-start.8 = (bf16[192,384]{1,0:T(8,128)(2,1)S(1)}, bf16[192,384]{1,0:T(8,128)(2,1)}, u32[]{:S(2)}) copy-start(bf16[192,384]{1,0:T(8,128)(2,1)} %param.19) | copy-start | bytes 442372
  7.2 70.4 %all-gather.6.cloned.1.call-start = ((), (), s32[]{:S(2)}) async-start(), calls=%async_computation.12 | async-start | bytes 3981312 | tf_op jit(solution)/shard_map/all_gather | solution.py:268
  25.8 33.2 %copy-start.9 = (bf16[768,96]{0,1:T(8,128)(2,1)S(1)}, bf16[768,96]{0,1:T(8,128)(2,1)}, u32[]{:S(2)}) copy-start(bf16[768,96]{0,1:T(8,128)(2,1)} %param.20) | copy-start | bytes 442372
  26.9 164.6 %all-gather.8.cloned.1.call-start = ((), (), s32[]{:S(2)}) async-start(), calls=%async_computation.13 | async-start | bytes 1327104 | tf_op jit(solution)/shard_map/all_gather | solution.py:269
  40.5 34.4 %copy-start.19 = (s32[1,2]{1,0:T(1,128)S(1)}, s32[1,2]{1,0:T(1,128)}, u32[]{:S(2)}) copy-start(s32[1,2]{1,0:T(1,128)} %param.27) | copy-start | bytes 28
  41.3 35.6 %copy-start.2 = (bf16[512,768]{1,0:T(8,128)(2,1)S(1)}, bf16[512,768]{1,0:T(8,128)(2,1)}, u32[]{:S(2)}) copy-start(bf16[512,768]{1,0:T(8,128)(2,1)} %param.14) | copy-start | bytes 2359300
  41.4 152.7 %all-gather.10.cloned.1.call-start = ((), (), s32[]{:S(2)}) async-start(), calls=%async_computation.14 | async-start | bytes 5308416 | tf_op jit(solution)/shard_map/all_gather | solution.py:270
  59.0 142.5 %all-gather.12.cloned.1.call-start = ((), (), s32[]{:S(2)}) async-start(), calls=%async_computation.15 | async-start | bytes 5308416 | tf_op jit(solution)/shard_map/all_gather | solution.py:271
  102.6 46.1 %all-to-all-start = ((bf16[8,3,3,64,256]{4,3,2,1,0:T(8,128)(2,1)}), bf16[8,3,3,64,256]{4,3,2,1,0:T(8,128)(2,1)S(1)}, u32[]{:S(2)}, u32[]{:S(2)}) async-start(bf16[8,3,3,64,256]{4,3,2,1,0:T(8,128)(2,1)} %copy.97), calls=%async_computation | async-start | bytes 4718592 | tf_op jit(solution)/shard_map/all_to_all | solution.py:286
  163.7 7.9 %copy-start.10 = (f32[9]{0:T(128)S(1)}, f32[9]{0:T(128)}, u32[]{:S(2)}) copy-start(f32[9]{0:T(128)} %param.25) | copy-start | bytes 112
  165.8 24.6 %all-to-all-start.1 = ((bf16[8,3,64,256]{3,2,1,0:T(8,128)(2,1)}), bf16[8,3,64,256]{3,2,1,0:T(8,128)(2,1)S(1)}, u32[]{:S(2)}, u32[]{:S(2)}) async-start(bf16[8,3,64,256]{3,2,1,0:T(8,128)(2,1)} %bitcast.160), calls=%async_computation.1 | async-start | bytes 1572864 | tf_op jit(solution)/shard_map/all_to_all | solution.py:290
  171.5 135.2 %reduce-scatter.17.cloned.1.call-start = ((), (), s32[]{:S(2)}) async-start(), calls=%async_computation.17 | async-start | bytes 1327104 | tf_op jit(solution)/shard_map/reduce_scatter | solution.py:351
  193.7 20.5 %copy-start.3 = (f32[512,768]{1,0:T(8,128)}, f32[512,768]{1,0:T(8,128)S(1)}, u32[]{:S(2)}) copy-start(f32[512,768]{1,0:T(8,128)S(1)} %get-tuple-element.134) | copy-start | bytes 4718596
  201.5 9.5 %copy-start.15 = (bf16[768,3072]{1,0:T(8,128)(2,1)S(1)}, bf16[768,3072]{1,0:T(8,128)(2,1)}, u32[]{:S(2)}) copy-start(bf16[768,3072]{1,0:T(8,128)(2,1)} %all-gather.10.cloned.1.call-done) | copy-start | bytes 14155780
  211.0 3.1 copy-start.21
  211.0 3.5 copy-start.16
  214.1 15.5 %slice-start = ((s8[6291456]{0:T(1024)(128)(4,1)}), s8[4194304]{0:T(1024)(128)(4,1)S(1)}, s32[]{:S(2)}) async-start(s8[6291456]{0:T(1024)(128)(4,1)} %bitcast.169), calls=%async_computation.24 | async-start | bytes 8388608
  214.5 15.2 %slice-start.1 = ((s8[6291456]{0:T(1024)(128)(4,1)}), s8[2097152]{0:T(1024)(128)(4,1)S(1)}, s32[]{:S(2)}) async-start(s8[6291456]{0:T(1024)(128)(4,1)} %bitcast.169), calls=%async_computation.25 | async-start | bytes 4194304
  214.5 15.2 %copy-start.4 = (bf16[512,768]{1,0:T(8,128)(2,1)S(1)}, bf16[512,768]{1,0:T(8,128)(2,1)}, u32[]{:S(2)}) copy-start(bf16[512,768]{1,0:T(8,128)(2,1)} %param.16) | copy-start | bytes 2359300
  234.6 26.2 %copy-start = (f32[512,768]{1,0:T(8,128)}, f32[512,768]{1,0:T(8,128)S(1)}, u32[]{:S(2)}) copy-start(f32[512,768]{1,0:T(8,128)S(1)} %get-tuple-element.113) | copy-start | bytes 4718596
  236.5 128.5 %reduce-scatter.29.cloned.1.call-start = ((), (), s32[]{:S(2)}) async-start(), calls=%async_computation.23 | async-start | bytes 5308416
  250.9 171.4 %reduce-scatter.21.cloned.1.call-start = ((), (), s32[]{:S(2)}) async-start(), calls=%async_computation.19 | async-start | bytes 5308416 | tf_op jit(solution)/shard_map/reduce_scatter | solution.py:357
  299.4 49.2 %all-to-all-start.3 = ((bf16[8,3,3,64,256]{4,3,2,1,0:T(8,128)(2,1)}), bf16[8,3,3,64,256]{4,3,2,1,0:T(8,128)(2,1)S(1)}, u32[]{:S(2)}, u32[]{:S(2)}) async-start(bf16[8,3,3,64,256]{4,3,2,1,0:T(8,128)(2,1)} %bitcast.166), calls=%async_computation.3 | async-start | bytes 4718592 | tf_op jit(solution)/shard_map/all_to_all | solution.py:335
  306.6 138.1 %reduce-scatter.27.cloned.1.call-start = ((), (), s32[]{:S(2)}) async-start(), calls=%async_computation.22 | async-start | bytes 245760
  308.5 186.0 %reduce-scatter.15.cloned.1.call-start = ((), (), s32[]{:S(2)}) async-start(), calls=%async_computation.16 | async-start | bytes 3981312 | tf_op jit(solution)/shard_map/reduce_scatter | solution.py:348
  361.5 5.7 copy-start.6
  361.6 186.9 %reduce-scatter.19.cloned.1.call-start = ((), (), s32[]{:S(2)}) async-start(), calls=%async_computation.18 | async-start | bytes 737280 | tf_op jit(solution)/shard_map/reduce_scatter | solution.py:368
  367.1 182.9 %reduce-scatter.23.cloned.1.call-start = ((), (), s32[]{:S(2)}) async-start(), calls=%async_computation.20 | async-start | bytes 737280 | tf_op jit(solution)/shard_map/reduce_scatter | solution.py:371
  367.9 54.6 %copy-start.12 = (f32[3,1,2048]{2,1,0:T(1,128)S(1)}, f32[3,1,2048]{2,1,0:T(1,128)}, u32[]{:S(2)}) copy-start(f32[3,1,2048]{2,1,0:T(1,128)} %get-tuple-element.16.lse_ref) | copy-start | bytes 73732
  422.3 142.3 %reduce-scatter.25.cloned.1.call-start = ((), (), s32[]{:S(2)}) async-start(), calls=%async_computation.21 | async-start | bytes 737280
  452.6 93.0 %copy-start.1 = (f32[512,768]{1,0:T(8,128)S(1)}, f32[512,768]{1,0:T(8,128)}, u32[]{:S(2)}) copy-start(f32[512,768]{1,0:T(8,128)} %copy-done) | copy-start | bytes 4718596
  (7 other events, 10.1 us)
Sparse Core Ops, SparseCore 0:
  27.0 35.0 all-gather.5
  64.5 23.9 all-gather.7
  90.4 53.7 all-gather.9
  145.9 51.6 all-gather.11
  236.7 46.1 reduce-scatter.16
  286.1 78.8 reduce-scatter.28
  368.4 53.7 reduce-scatter.20
  425.1 19.5 reduce-scatter.26
  448.2 46.2 reduce-scatter.14
  496.6 22.1 reduce-scatter.18
  521.0 20.7 reduce-scatter.22
  544.0 20.5 reduce-scatter.24

commit v5 on v4

--- a/solution.py
+++ b/solution.py
@@ -258,18 +258,10 @@
     held_pairs = lax.dynamic_slice_in_dim(order_row, my_index * per_dev, per_dev, 0)
     my_pairs = my_index * per_dev + jnp.arange(per_dev, dtype=jnp.int32)
     seg_pairs = jnp.take(seg_len, my_pairs // HEADS).astype(jnp.int32)
-    row_parts = (
-        lax.all_gather(qkv_weight, "batch", axis=0, tiled=True),
-        lax.all_gather(proj_weight, "batch", axis=0, tiled=True),
-        lax.all_gather(up_weight, "batch", axis=0, tiled=True),
-        lax.all_gather(down_weight, "batch", axis=0, tiled=True),
-    )
-    w_qkv, w_proj, w_up, w_down = (
-        lax.all_gather(row_parts[0], "seq", axis=1, tiled=True),
-        lax.all_gather(row_parts[1], "seq", axis=1, tiled=True),
-        lax.all_gather(row_parts[2], "seq", axis=1, tiled=True),
-        lax.all_gather(row_parts[3], "seq", axis=1, tiled=True),
-    )
+    w_qkv = lax.all_gather(
+        lax.all_gather(qkv_weight, "batch", axis=0, tiled=True), "seq", axis=1, tiled=True
+    )
+    later = (proj_weight, up_weight, down_weight)
     inputs32 = block_input.astype(jnp.float32)
     norm1_out, normed1, inv_std1 = norm_rows(inputs32, norm1_gain, norm1_bias)
     norm1_low = norm1_out.astype(jnp.bfloat16)
@@ -284,10 +276,20 @@
         stacked.reshape(slot_count, piece_len, 3, head_groups, per_dev, HD), (0, 3, 4, 2, 5, 1)
     ).reshape(n_seq, per_dev, 3, HD, piece_len)
     incoming = lax.all_to_all(send, "seq", split_axis=0, concat_axis=0, tiled=True)
+    later_rows = lax.all_gather(jnp.concatenate([w.reshape(-1) for w in later]), "batch", axis=0)
+    offset = 0
+    later_full = []
+    for w in later:
+        rows = later_rows[:, offset : offset + w.size].reshape(-1, w.shape[1])
+        later_full.append(lax.all_gather(rows, "seq", axis=1, tiled=True))
+        offset += w.size
+    w_proj, w_up, w_down = later_full
     qkv_t = jnp.transpose(incoming, (1, 2, 3, 0, 4)).reshape(per_dev, 3, HD, SLOT)
     attn_t, lse_rows = attn_forward(qkv_t, seg_pairs)
     back = jnp.transpose(attn_t.reshape(per_dev, HD, n_seq, piece_len), (2, 0, 1, 3))
     returned = lax.all_to_all(back, "seq", split_axis=0, concat_axis=0, tiled=True)
+    lse_all = lax.all_gather(lse_rows.reshape(per_dev, SLOT), "seq", axis=0, tiled=True)
+    lse_all, returned = lax.optimization_barrier((lse_all, returned))
     attended = jnp.transpose(
         returned.reshape(slot_count, head_groups, per_dev, HD, piece_len), (0, 4, 1, 2, 3)
     ).reshape(row_count, D)
@@ -383,7 +385,6 @@
         small_sums[k * D : (k + 1) * D] for k in range(4)
     )
     dwa_grad = small_sums[4 * D :]
-    lse_all = lax.all_gather(lse_rows.reshape(per_dev, SLOT), "seq", axis=0, tiled=True)
     row_lse = jnp.take(lse_all, held_pairs, axis=0).reshape(1, per_dev, SLOT)
     return (
         block_output,
@@ -419,6 +420,7 @@
         P("batch", None),
         P("batch", None),
     )
+
     return jax.shard_map(
         local,
         mesh=mesh,

time: 583 us -> 581 us (level)
  blocking collectives: 133 us -> 103 us
  waiting for transfers between devices: 219 us -> 237 us
  Pallas kernels: 28.7 us -> 38.1 us
  local copies, waits for them, and re-layouts: 59.4 us -> 68.7 us
    all_gather x4 -> x5, waiting for transfers between devices: 0.06 us -> 47.3 us  [the longest x1 26.8 us: local(): lax.all_gather(lax.all_gather(qkv_weight, 'batch', axis=0, tiled=True), '...]
    all_gather x3 -> x0, blocking collectives: 46.9 us -> none  [the longest x1 17.5 us: local(): lax.all_gather(up_weight, 'batch', axis=0, tiled=True)]
    all_to_all x1, waiting for transfers between devices: 18.2 us -> 0.01 us  [local(): lax.all_to_all(back, 'seq', split_axis=0, concat_axis=0, tiled=True)]
    all_gather x1, blocking collectives: 9.45 us -> 21.6 us  [local(): lax.all_gather(lse_rows.reshape(per_dev, SLOT), 'seq', axis=0, tiled=True)]
    all_to_all x1, waiting for transfers between devices: 39.9 us -> 31.9 us  [local(): lax.all_to_all(dback, 'seq', split_axis=0, concat_axis=0, tiled=True)]
    all_to_all x1, waiting for transfers between devices: 40.8 us -> 34.4 us  [local(): lax.all_to_all(send, 'seq', split_axis=0, concat_axis=0, tiled=True)]
    reshape x0 -> x8, local copies, waits for them, and re-layouts: none -> 6.1 us  [the longest x5 3.9 us: local(): rows = later_rows[:, offset:offset + w.size].reshape(-1, w.shape[1])]
    unnamed x15 -> x16, waiting for transfers between devices: 27.9 us -> 33.8 us
  transfers between devices with their start and end apart: 15 -> 16, of which waited for: 8 -> 9; matrix products, arithmetic and copies ran while one was open for 21% -> 22% of each run, Pallas kernels for 5% -> 7%
where the time goes in v5:
time: 581 us; the launch traced here: 575 us
  waiting for transfers between devices  237 us (41%)
  blocking collectives  103 us (18%)
  matrix products  71.2 us (12%)
  local copies, waits for them, and re-layouts  68.7 us (12%)
  Pallas kernels  38.1 us (7%)
  other arithmetic  30 us (5%)
  between operations  14.9 us (3%)
  starting transfers between devices  12.4 us (2%)
    reduce_scatter x1, waiting for transfers between devices, local(): lax.psum_scatter(down_local.astype(jnp.bfloat16), 'seq', scatter_dimensio...  48 us
    reduce_scatter x1, waiting for transfers between devices, local(): lax.psum_scatter(qkv_local.astype(jnp.bfloat16), 'seq', scatter_dimension...  41.7 us
    all_to_all x1, waiting for transfers between devices, local(): lax.all_to_all(send, 'seq', split_axis=0, concat_axis=0, tiled=True)  34.4 us
    unnamed x16, waiting for transfers between devices  33.8 us
    all_to_all x1, waiting for transfers between devices, local(): lax.all_to_all(dback, 'seq', split_axis=0, concat_axis=0, tiled=True)  31.9 us
    all_gather x1, waiting for transfers between devices, local(): lax.all_gather(lax.all_gather(qkv_weight, 'batch', axis=0, tiled=True), '...  26.8 us
    psum x1, blocking collectives, local(): lax.psum(jnp.concatenate([gain1_local, bias1_local, gain2_local, bias2_lo...  23.6 us
    unnamed x61, local copies, waits for them, and re-layouts  22.6 us
  transfers between devices with their start and end apart: 16, of which 9 were waited for; matrix products, arithmetic and copies ran while one was open for 22% of the time, Pallas kernels for 7%

profile of v5, /device:TPU:0, one launch (start us, length us, event | category | flops | bytes accessed | tf_op | source)
XLA Modules:
  0.0 575.3 jit_solution(15148333182428720596)
XLA Ops:
  11.4 22.3 %all_gather.24 = bf16[768,288]{1,0:T(8,128)(2,1)S(1)} all-gather(bf16[192,288]{1,0:T(8,128)(2,1)S(1)} %copy-done.8), channel_id=1, replica_groups=mesh['batch'=4,'seq'=8] {'batch'}, dimensions={0}, use_global_device_ids=true | all-gather | bytes 552960 | tf_op jit(solution)/shard_map/all_gather | solution.py:262
  34.7 15.3 %all-gather.16.cloned.1.call-done = bf16[663552]{0:T(1024)(128)(2,1)} async-done(((bf16[165888]{0:T(1024)(128)(2,1)}), bf16[663552]{0:T(1024)(128)(2,1)}) %all-gather.16.cloned.1.call-update) | async-done | bytes 1327120 | tf_op jit(solution)/shard_map/all_gather | solution.py:279
  59.3 26.8 %all-gather.8.cloned.1.call-done = bf16[768,2304]{0,1:T(8,128)(2,1)} async-done(((bf16[768,288]{0,1:T(8,128)(2,1)}), bf16[768,2304]{0,1:T(8,128)(2,1)}) %all-gather.8.cloned.1.call-update) | async-done | bytes 3538960 | tf_op jit(solution)/shard_map/all_gather | solution.py:261
  86.0 4.2 fusion.55
  111.0 4.0 all-to-all-start
  116.3 34.4 %all-to-all-done = bf16[8,3,3,64,256]{4,3,2,1,0:T(8,128)(2,1)S(1)} async-done(((bf16[8,3,3,64,256]{4,3,2,1,0:T(8,128)(2,1)}), bf16[8,3,3,64,256]{4,3,2,1,0:T(8,128)(2,1)S(1)}, u32[]{:S(2)}, u32[]{:S(2)}) %all-to-all-start) | async-done | bytes 2359328 | tf_op jit(solution)/shard_map/all_to_all | solution.py:278
  152.4 17.1 %attn_fwd.1 = (bf16[3,64,2048]{2,1,0:T(8,128)(2,1)}, f32[3,1,2048]{2,1,0:T(1,128)}) custom-call(s32[3]{0:T(128)} %and_select_fusion.2.seg_ref, bf16[3,3,64,2048]{3,2,1,0:T(8,128)(2,1)} %bitcast.187, bf16[3,3,64,2048]{3,2,1,0:T(8,128)(2,1)} %bitcast.188, bf16[3,3,64,2048]{3,2,1,0:T(8,128)(2,1)} %bitcast.189), custom_call_target="tpu_custom_call" | custom-call | flops 2013265920 | bytes 3170304 | tf_op jit(solution)/shard_map/attn_fwd/pallas_call | solution.py:86
  171.7 3.5 all-to-all-start.1
  175.9 21.6 %all-gather = f32[24,1,2048]{2,1,0:T(1,128)S(1)} all-gather(f32[3,1,2048]{2,1,0:T(1,128)S(1)} %copy-done.10), channel_id=2, replica_groups=mesh['batch'=4,'seq'=8] {'seq'}, dimensions={0}, use_global_device_ids=true | all-gather | bytes 221184 | tf_op jit(solution)/shard_map/all_gather | solution.py:291
  201.6 7.0 %fusion.57 = f32[512,3072]{1,0:T(8,128)} fusion(bf16[768,3072]{1,0:T(8,128)(2,1)} %all-gather.12.cloned.1.call-done, f32[512,768]{1,0:T(8,128)S(1)} %get-tuple-element.140, f32[768]{0:T(1024)S(1)} %copy-done.15, f32[768]{0:T(1024)S(1)} %copy-done.11, f32[512]{0:T(512)S(1)} %add_rsqrt_fusion, f32[512]{0:T(512)S(1)} %broadcast_multiply_fusion.5), kind=kOutput, calls=%fused_computation.142 | convolution fusion | flops 2417885184 | bytes 12593152 | tf_op jit(solution)/shard_map/dot_general | solution.py:299
  208.6 5.2 all-gather.14.cloned.1.call-done
  213.8 9.5 %fusion.6 = bf16[512,3072]{1,0:T(8,128)(2,1)S(1)} fusion(f32[512,3072]{1,0:T(8,128)} %fusion.57, bf16[3072,768]{0,1:T(8,128)(2,1)} %all-gather.14.cloned.1.call-done, bf16[512,768]{1,0:T(8,128)(2,1)} %param.16, f32[]{:T(128)} %bitcast), kind=kOutput, calls=%fused_computation.11 | convolution fusion | flops 2448556032 | bytes 14942212 | tf_op jit(solution)/shard_map/nd,fd->nf/dot_general | solution.py:317
  226.8 15.2 %fusion.32 = (bf16[512,768]{1,0:T(8,128)(2,1)}, f32[512,768]{1,0:T(8,128)S(1)}) fusion(f32[]{:T(128)} %bitcast.26, f32[]{:T(128)} %bitcast.24, f32[]{:T(128)} %bitcast.22, f32[]{:T(128)} %bitcast.20, f32[]{:T(128)} %bitcast.18, f32[]{:T(128)} %bitcast.16, f32[]{:T(128)} %bitcast.14, f32[]{:T(128)} %bitcast.12, f32[]{:T(128)} %bitcast, ...), kind=kOutput, calls=%fused_computation.64 | convolution fusion | flops 2440691712 | bytes 21233700 | tf_op jit(solution)/shard_map/dot_general | solution.py:302
  242.0 5.0 fusion.40
  249.1 7.4 %convolution_convert_fusion.2 = bf16[768,3072]{1,0:T(8,128)(2,1)} fusion(bf16[512,3072]{1,0:T(8,128)(2,1)} %copy-done.19, f32[512,768]{1,0:T(8,128)} %copy-done.3, f32[768]{0:T(1024)S(1)} %copy-done.15, f32[768]{0:T(1024)S(1)} %copy-done.11, f32[512]{0:T(512)S(1)} %add_rsqrt_fusion, f32[512]{0:T(512)S(1)} %broadcast_multiply_fusion.5), kind=kOutput, calls=%fused_computation.15 | convolution fusion | flops 2420244480 | bytes 9447424 | tf_op jit(solution)/shard_map/nd,nf->df/dot_general | solution.py:319
  256.4 6.8 %copy.125 = bf16[768,3072]{0,1:T(8,128)(2,1)} copy(bf16[768,3072]{1,0:T(8,128)(2,1)} %convolution_convert_fusion.2) | data formatting | bytes 9437184
  264.3 8.6 %convolution_convert_fusion.1 = bf16[3072,768]{0,1:T(8,128)(2,1)} fusion(bf16[512,768]{1,0:T(8,128)(2,1)S(1)} %copy-done.5, f32[]{:T(128)} %bitcast, f32[512,3072]{1,0:T(8,128)} %fusion.57), kind=kOutput, calls=%fused_computation.14 | convolution fusion | flops 2433613824 | bytes 11796484 | tf_op jit(solution)/shard_map/nf,nd->fd/dot_general | solution.py:316
  275.7 16.7 %all_to_all.20 = bf16[8,3,64,256]{3,2,1,0:T(8,128)(2,1)S(1)} all-to-all(bf16[8,3,64,256]{3,2,1,0:T(8,128)(2,1)S(1)} %bitcast.183), channel_id=1, replica_groups=mesh['batch'=4,'seq'=8] {'seq'}, dimensions={0} | all-to-all | bytes 1572864 | tf_op jit(solution)/shard_map/all_to_all | solution.py:331
  293.3 21.0 %attn_bwd.1 = bf16[3,3,64,2048]{3,2,1,0:T(8,128)(2,1)} custom-call(s32[3]{0:T(128)} %and_select_fusion.2.seg_ref, bf16[3,3,64,2048]{3,2,1,0:T(8,128)(2,1)} %bitcast.190, bf16[3,3,64,2048]{3,2,1,0:T(8,128)(2,1)} %bitcast.191, bf16[3,3,64,2048]{3,2,1,0:T(8,128)(2,1)} %bitcast.192, bf16[3,64,2048]{2,1,0:T(8,128)(2,1)} %bitcast.196, ...), custom_call_target="tpu_custom_call" | custom-call | flops 5033164800 | bytes 6316032 | tf_op jit(solution)/shard_map/attn_bwd/pallas_call | solution.py:174
  314.3 4.0 copy.147
  318.3 3.6 all-to-all-start.3
  324.0 31.9 %all-to-all-done.3 = bf16[8,3,3,64,256]{4,3,2,1,0:T(8,128)(2,1)S(1)} async-done(((bf16[8,3,3,64,256]{4,3,2,1,0:T(8,128)(2,1)}), bf16[8,3,3,64,256]{4,3,2,1,0:T(8,128)(2,1)S(1)}, u32[]{:S(2)}, u32[]{:S(2)}) %all-to-all-start.3) | async-done | bytes 2359328 | tf_op jit(solution)/shard_map/all_to_all | solution.py:337
  364.7 4.0 convolution_convert_fusion
  371.8 4.5 multiply_convert_fusion
  376.3 48.0 %reduce-scatter.21.cloned.1.call-done = bf16[3072,96]{0,1:T(8,128)(2,1)} async-done(((bf16[3072,768]{0,1:T(8,128)(2,1)}), bf16[3072,96]{0,1:T(8,128)(2,1)}) %reduce-scatter.21.cloned.1.call-update) | async-done | bytes 589840 | tf_op jit(solution)/shard_map/reduce_scatter | solution.py:359
  426.0 20.8 %reduce-scatter.27.cloned.1.call-done = bf16[192,96]{1,0:T(8,128)(2,1)} async-done(((bf16[768,96]{1,0:T(8,128)(2,1)}), bf16[192,96]{1,0:T(8,128)(2,1)}) %reduce-scatter.27.cloned.1.call-update) | async-done | bytes 36880
  448.4 6.2 %fusion.22 = (f32[768]{0:T(1024)S(1)}, f32[512]{0:T(512)S(1)}, f32[512]{0:T(512)S(1)}, f32[768]{0:T(1024)S(1)}, f32[512,768]{1,0:T(8,128)}) fusion(bf16[512,768]{1,0:T(8,128)(2,1)S(1)} %copy-done.2, f32[512]{0:T(512)S(1)} %add_rsqrt_fusion.1, f32[512]{0:T(512)S(1)} %broadcast_multiply_fusion.6, f32[768]{0:T(1024)S(1)} %copy-done.12, ...), kind=kOutput, calls=%fused_computation.54 | convolution fusion | flops 1815868928 | bytes 8274944 | tf_op jit(solution)/shard_map/nf,df->nd/dot_general | solution.py:346
  454.6 41.7 %reduce-scatter.15.cloned.1.call-done = bf16[768,288]{0,1:T(8,128)(2,1)} async-done(((bf16[768,2304]{0,1:T(8,128)(2,1)}), bf16[768,288]{0,1:T(8,128)(2,1)}) %reduce-scatter.15.cloned.1.call-update) | async-done | bytes 442384 | tf_op jit(solution)/shard_map/reduce_scatter | solution.py:350
  498.4 5.7 concatenate.34
  504.1 23.6 %psum.14 = f32[3081]{0:T(1024)S(1)} all-reduce(f32[3081]{0:T(1024)S(1)} %concatenate.34), channel_id=1, replica_groups=mesh['batch'=4,'seq'=8] {'seq'}, use_global_device_ids=true, to_apply=%region_29.30 | all-reduce | flops 3081 | bytes 24648 | tf_op jit(solution)/shard_map/psum | solution.py:378
  527.7 18.9 %psum.15 = f32[3081]{0:T(1024)S(1)} all-reduce(f32[3081]{0:T(1024)S(1)} %psum.14), channel_id=1, replica_groups=mesh['batch'=4,'seq'=8] {'batch'}, use_global_device_ids=true, to_apply=%region_30.31 | all-reduce | flops 3081 | bytes 24648 | tf_op jit(solution)/shard_map/psum | solution.py:377
  553.9 12.8 %reduce-scatter.25.cloned.1.call-done = bf16[192,288]{1,0:T(8,128)(2,1)} async-done(((bf16[768,288]{1,0:T(8,128)(2,1)}), bf16[192,288]{1,0:T(8,128)(2,1)}) %reduce-scatter.25.cloned.1.call-update) | async-done | bytes 110608
  (176 shorter events, 83.3 us)
Async XLA Ops:
  7.2 4.2 copy-start.8
  7.2 42.8 %all-gather.16.cloned.1.call-start = ((), (), s32[]{:S(2)}) async-start(), calls=%async_computation.21 | async-start | bytes 1658880 | tf_op jit(solution)/shard_map/all_gather | solution.py:279
  11.3 74.7 %all-gather.8.cloned.1.call-start = ((), (), s32[]{:S(2)}) async-start(), calls=%async_computation.12 | async-start | bytes 3981312 | tf_op jit(solution)/shard_map/all_gather | solution.py:261
  34.7 163.9 %all-gather.10.cloned.1.call-start = ((), (), s32[]{:S(2)}) async-start(), calls=%async_computation.13 | async-start | bytes 1327104 | tf_op jit(solution)/shard_map/all_gather | solution.py:284
  52.9 148.3 %all-gather.12.cloned.1.call-start = ((), (), s32[]{:S(2)}) async-start(), calls=%async_computation.14 | async-start | bytes 5308416 | tf_op jit(solution)/shard_map/all_gather | solution.py:284
  54.6 159.2 %all-gather.14.cloned.1.call-start = ((), (), s32[]{:S(2)}) async-start(), calls=%async_computation.15 | async-start | bytes 5308416 | tf_op jit(solution)/shard_map/all_gather | solution.py:284
  55.4 3.3 copy-start.2
  56.5 29.5 %copy-start.12 = (f32[768]{0:T(1024)S(1)}, f32[768]{0:T(1024)}, u32[]{:S(2)}) copy-start(f32[768]{0:T(1024)} %param.21) | copy-start | bytes 9220
  56.5 29.5 %copy-start.16 = (f32[768]{0:T(1024)S(1)}, f32[768]{0:T(1024)}, u32[]{:S(2)}) copy-start(f32[768]{0:T(1024)} %param.22) | copy-start | bytes 9220
  111.0 39.7 %all-to-all-start = ((bf16[8,3,3,64,256]{4,3,2,1,0:T(8,128)(2,1)}), bf16[8,3,3,64,256]{4,3,2,1,0:T(8,128)(2,1)S(1)}, u32[]{:S(2)}, u32[]{:S(2)}) async-start(bf16[8,3,3,64,256]{4,3,2,1,0:T(8,128)(2,1)} %copy.101), calls=%async_computation | async-start | bytes 4718592 | tf_op jit(solution)/shard_map/all_to_all | solution.py:278
  169.5 5.7 copy-start.9
  169.5 6.4 %copy-start.10 = (f32[3,1,2048]{2,1,0:T(1,128)S(1)}, f32[3,1,2048]{2,1,0:T(1,128)}, u32[]{:S(2)}) copy-start(f32[3,1,2048]{2,1,0:T(1,128)} %get-tuple-element.17.lse_ref) | copy-start | bytes 73732
  171.7 25.9 %all-to-all-start.1 = ((bf16[8,3,64,256]{3,2,1,0:T(8,128)(2,1)}), bf16[8,3,64,256]{3,2,1,0:T(8,128)(2,1)S(1)}, u32[]{:S(2)}, u32[]{:S(2)}) async-start(bf16[8,3,64,256]{3,2,1,0:T(8,128)(2,1)} %bitcast.160), calls=%async_computation.1 | async-start | bytes 1572864 | tf_op jit(solution)/shard_map/all_to_all | solution.py:290
  175.2 146.8 %reduce-scatter.17.cloned.1.call-start = ((), (), s32[]{:S(2)}) async-start(), calls=%async_computation.17 | async-start | bytes 1327104 | tf_op jit(solution)/shard_map/reduce_scatter | solution.py:353
  200.8 25.6 %copy-start.3 = (f32[512,768]{1,0:T(8,128)}, f32[512,768]{1,0:T(8,128)S(1)}, u32[]{:S(2)}) copy-start(f32[512,768]{1,0:T(8,128)S(1)} %get-tuple-element.140) | copy-start | bytes 4718596
  213.8 9.5 %copy-start.13 = (bf16[768,3072]{1,0:T(8,128)(2,1)S(1)}, bf16[768,3072]{1,0:T(8,128)(2,1)}, u32[]{:S(2)}) copy-start(bf16[768,3072]{1,0:T(8,128)(2,1)} %all-gather.12.cloned.1.call-done) | copy-start | bytes 14155780
  223.3 3.0 copy-start.19
  223.3 3.5 copy-start.14
  226.4 15.6 %slice-start = ((s8[6291456]{0:T(1024)(128)(4,1)}), s8[4194304]{0:T(1024)(128)(4,1)S(1)}, s32[]{:S(2)}) async-start(s8[6291456]{0:T(1024)(128)(4,1)} %bitcast.169), calls=%async_computation.25 | async-start | bytes 8388608
  226.8 15.2 %slice-start.1 = ((s8[6291456]{0:T(1024)(128)(4,1)}), s8[2097152]{0:T(1024)(128)(4,1)S(1)}, s32[]{:S(2)}) async-start(s8[6291456]{0:T(1024)(128)(4,1)} %bitcast.169), calls=%async_computation.26 | async-start | bytes 4194304
  226.8 15.2 %copy-start.4 = (bf16[512,768]{1,0:T(8,128)(2,1)S(1)}, bf16[512,768]{1,0:T(8,128)(2,1)}, u32[]{:S(2)}) copy-start(bf16[512,768]{1,0:T(8,128)(2,1)} %param.16) | copy-start | bytes 2359300
  246.9 26.0 %copy-start = (f32[512,768]{1,0:T(8,128)}, f32[512,768]{1,0:T(8,128)S(1)}, u32[]{:S(2)}) copy-start(f32[512,768]{1,0:T(8,128)S(1)} %get-tuple-element.119) | copy-start | bytes 4718596
  248.9 120.0 %reduce-scatter.29.cloned.1.call-start = ((), (), s32[]{:S(2)}) async-start(), calls=%async_computation.24 | async-start | bytes 5308416
  263.2 161.1 %reduce-scatter.21.cloned.1.call-start = ((), (), s32[]{:S(2)}) async-start(), calls=%async_computation.19 | async-start | bytes 5308416 | tf_op jit(solution)/shard_map/reduce_scatter | solution.py:359
  318.3 37.6 %all-to-all-start.3 = ((bf16[8,3,3,64,256]{4,3,2,1,0:T(8,128)(2,1)}), bf16[8,3,3,64,256]{4,3,2,1,0:T(8,128)(2,1)S(1)}, u32[]{:S(2)}, u32[]{:S(2)}) async-start(bf16[8,3,3,64,256]{4,3,2,1,0:T(8,128)(2,1)} %bitcast.166), calls=%async_computation.3 | async-start | bytes 4718592 | tf_op jit(solution)/shard_map/all_to_all | solution.py:337
  321.9 124.8 %reduce-scatter.27.cloned.1.call-start = ((), (), s32[]{:S(2)}) async-start(), calls=%async_computation.23 | async-start | bytes 245760
  323.8 172.5 %reduce-scatter.15.cloned.1.call-start = ((), (), s32[]{:S(2)}) async-start(), calls=%async_computation.16 | async-start | bytes 3981312 | tf_op jit(solution)/shard_map/reduce_scatter | solution.py:350
  368.8 2.3 copy-start.6
  368.8 181.8 %reduce-scatter.19.cloned.1.call-start = ((), (), s32[]{:S(2)}) async-start(), calls=%async_computation.18 | async-start | bytes 737280 | tf_op jit(solution)/shard_map/reduce_scatter | solution.py:370
  371.1 181.1 %reduce-scatter.23.cloned.1.call-start = ((), (), s32[]{:S(2)}) async-start(), calls=%async_computation.20 | async-start | bytes 737280 | tf_op jit(solution)/shard_map/reduce_scatter | solution.py:373
  424.3 142.3 %reduce-scatter.25.cloned.1.call-start = ((), (), s32[]{:S(2)}) async-start(), calls=%async_computation.22 | async-start | bytes 737280
  454.6 93.1 %copy-start.1 = (f32[512,768]{1,0:T(8,128)S(1)}, f32[512,768]{1,0:T(8,128)}, u32[]{:S(2)}) copy-start(f32[512,768]{1,0:T(8,128)} %copy-done) | copy-start | bytes 4718596
  (6 other events, 6.4 us)
Sparse Core Ops, SparseCore 0:
  11.4 38.5 all-gather.15
  52.5 33.5 all-gather.7
  88.5 23.9 all-gather.9
  114.2 52.4 all-gather.11
  168.4 45.3 all-gather.13
  249.0 39.7 reduce-scatter.16
  292.2 73.6 reduce-scatter.28
  369.4 54.9 reduce-scatter.20
  427.2 19.5 reduce-scatter.26
  450.1 46.1 reduce-scatter.14
  498.6 22.2 reduce-scatter.18
  523.0 20.6 reduce-scatter.22
  546.0 20.5 reduce-scatter.24

commit v6 on v4

--- a/solution.py
+++ b/solution.py
@@ -288,6 +288,8 @@
     attn_t, lse_rows = attn_forward(qkv_t, seg_pairs)
     back = jnp.transpose(attn_t.reshape(per_dev, HD, n_seq, piece_len), (2, 0, 1, 3))
     returned = lax.all_to_all(back, "seq", split_axis=0, concat_axis=0, tiled=True)
+    lse_all = lax.all_gather(lse_rows.reshape(per_dev, SLOT), "seq", axis=0, tiled=True)
+    lse_all, returned = lax.optimization_barrier((lse_all, returned))
     attended = jnp.transpose(
         returned.reshape(slot_count, head_groups, per_dev, HD, piece_len), (0, 4, 1, 2, 3)
     ).reshape(row_count, D)
@@ -344,33 +346,19 @@
     dnorm1 = jnp.einsum("nf,df->nd", dqkv_low, w_qkv, preferred_element_type=jnp.float32)
     dinput_norm, gain1_local, bias1_local = norm_back(dnorm1, normed1, inv_std1, norm1_gain)
     input_grad = (dmiddle + dinput_norm).astype(jnp.bfloat16)
-    col_sums = (
-        lax.psum_scatter(
-            qkv_local.astype(jnp.bfloat16), "seq", scatter_dimension=1, tiled=True
-        ).astype(jnp.float32),
-        lax.psum_scatter(
-            proj_local.astype(jnp.bfloat16), "seq", scatter_dimension=1, tiled=True
-        ).astype(jnp.float32),
-        lax.psum_scatter(
-            up_local.astype(jnp.bfloat16), "seq", scatter_dimension=1, tiled=True
-        ).astype(jnp.float32),
-        lax.psum_scatter(
-            down_local.astype(jnp.bfloat16), "seq", scatter_dimension=1, tiled=True
-        ).astype(jnp.float32),
-    )
+    def scatter_grad(partial):
+        by_rows = lax.psum_scatter(
+            partial.astype(jnp.bfloat16), "batch", scatter_dimension=0, tiled=True
+        )
+        return lax.psum_scatter(by_rows, "seq", scatter_dimension=1, tiled=True).astype(
+            jnp.float32
+        )
+
     qkv_grad, proj_grad, up_grad, down_grad = (
-        lax.psum_scatter(
-            col_sums[0].astype(jnp.bfloat16), "batch", scatter_dimension=0, tiled=True
-        ).astype(jnp.float32),
-        lax.psum_scatter(
-            col_sums[1].astype(jnp.bfloat16), "batch", scatter_dimension=0, tiled=True
-        ).astype(jnp.float32),
-        lax.psum_scatter(
-            col_sums[2].astype(jnp.bfloat16), "batch", scatter_dimension=0, tiled=True
-        ).astype(jnp.float32),
-        lax.psum_scatter(
-            col_sums[3].astype(jnp.bfloat16), "batch", scatter_dimension=0, tiled=True
-        ).astype(jnp.float32),
+        scatter_grad(qkv_local),
+        scatter_grad(proj_local),
+        scatter_grad(up_local),
+        scatter_grad(down_local),
     )
     small_sums = lax.psum(
         lax.psum(
@@ -383,7 +371,6 @@
         small_sums[k * D : (k + 1) * D] for k in range(4)
     )
     dwa_grad = small_sums[4 * D :]
-    lse_all = lax.all_gather(lse_rows.reshape(per_dev, SLOT), "seq", axis=0, tiled=True)
     row_lse = jnp.take(lse_all, held_pairs, axis=0).reshape(1, per_dev, SLOT)
     return (
         block_output,

time: 583 us -> 766 us (1.31)
  waiting for transfers between devices: 219 us -> 383 us
  blocking collectives: 133 us -> 147 us
  Pallas kernels: 28.7 us -> 38 us
    reduce_scatter x5 -> x4, waiting for transfers between devices: 91.8 us -> 224 us  [scatter_grad(): lax.psum_scatter(partial.astype(jnp.bfloat16), 'batch', scatter_dimension...]
    unnamed x15 -> x16, waiting for transfers between devices: 27.9 us -> 92.3 us
    all_to_all x1, waiting for transfers between devices: 18.2 us -> 0.01 us  [local(): lax.all_to_all(back, 'seq', split_axis=0, concat_axis=0, tiled=True)]
    all_gather x1, blocking collectives: 9.45 us -> 24.2 us  [local(): lax.all_gather(lse_rows.reshape(per_dev, SLOT), 'seq', axis=0, tiled=True)]
    all_to_all x1, waiting for transfers between devices: 39.9 us -> 25.8 us  [local(): lax.all_to_all(dback, 'seq', split_axis=0, concat_axis=0, tiled=True)]
    unnamed x64 -> x71, local copies, waits for them, and re-layouts: 21.3 us -> 22.6 us
  transfers between devices with their start and end apart: 15 -> 15, of which waited for: 8 -> 8; matrix products, arithmetic and copies ran while one was open for 21% -> 15% of each run, Pallas kernels for 5% -> 2%
where the time goes in v6:
time: 766 us; the launch traced here: 755 us
  waiting for transfers between devices  383 us (50%)
  blocking collectives  147 us (19%)
  matrix products  72.4 us (9%)
  local copies, waits for them, and re-layouts  60.6 us (8%)
  Pallas kernels  38 us (5%)
  other arithmetic  26.8 us (3%)
  between operations  15.3 us (2%)
  starting transfers between devices  11.9 us (2%)
    reduce_scatter x4, waiting for transfers between devices, scatter_grad(): lax.psum_scatter(partial.astype(jnp.bfloat16), 'batch', scatter_dimension...  224 us
    unnamed x16, waiting for transfers between devices  92.3 us
    all_to_all x1, waiting for transfers between devices, local(): lax.all_to_all(send, 'seq', split_axis=0, concat_axis=0, tiled=True)  40.7 us
    all_to_all x1, waiting for transfers between devices, local(): lax.all_to_all(dback, 'seq', split_axis=0, concat_axis=0, tiled=True)  25.8 us
    all_gather x1, blocking collectives, local(): lax.all_gather(lse_rows.reshape(per_dev, SLOT), 'seq', axis=0, tiled=True)  24.2 us
    psum x1, blocking collectives, local(): lax.psum(jnp.concatenate([gain1_local, bias1_local, gain2_local, bias2_lo...  24 us
    unnamed x71, local copies, waits for them, and re-layouts  22.6 us
    pallas_call x1, Pallas kernels, attn_backward(): pl.pallas_call(functools.partial(bwd_kernel, bk=bk, bq=bq, scale=scale),...  20.8 us
  transfers between devices with their start and end apart: 15, of which 8 were waited for; matrix products, arithmetic and copies ran while one was open for 15% of the time, Pallas kernels for 2%

profile of v6, /device:TPU:0, one launch (start us, length us, event | category | flops | bytes accessed | tf_op | source)
XLA Modules:
  0.0 755.0 jit_solution(2106155029593865411)
XLA Ops:
  7.2 18.6 %all_gather.27 = bf16[768,288]{1,0:T(8,128)(2,1)S(1)} all-gather(bf16[192,288]{1,0:T(8,128)(2,1)} %param.17), channel_id=1, replica_groups=mesh['batch'=4,'seq'=8] {'batch'}, dimensions={0}, use_global_device_ids=true | all-gather | bytes 552960 | tf_op jit(solution)/shard_map/all_gather | solution.py:262
  26.9 13.6 %all_gather.30 = bf16[768,96]{1,0:T(8,128)(2,1)S(1)} all-gather(bf16[192,96]{1,0:T(8,128)(2,1)S(1)} %copy-done.13), channel_id=1, replica_groups=mesh['batch'=4,'seq'=8] {'batch'}, dimensions={0}, use_global_device_ids=true | all-gather | bytes 184320 | tf_op jit(solution)/shard_map/all_gather | solution.py:263
  41.4 17.5 %all_gather.32 = bf16[768,384]{1,0:T(8,128)(2,1)} all-gather(bf16[192,384]{1,0:T(8,128)(2,1)S(1)} %copy-done.10), channel_id=1, replica_groups=mesh['batch'=4,'seq'=8] {'batch'}, dimensions={0}, use_global_device_ids=true | all-gather | bytes 737280 | tf_op jit(solution)/shard_map/all_gather | solution.py:264
  59.0 15.8 %all_gather.34 = bf16[3072,96]{0,1:T(8,128)(2,1)} all-gather(bf16[768,96]{0,1:T(8,128)(2,1)S(1)} %copy-done.11), channel_id=1, replica_groups=mesh['batch'=4,'seq'=8] {'batch'}, dimensions={0}, use_global_device_ids=true | all-gather | bytes 737280 | tf_op jit(solution)/shard_map/all_gather | solution.py:265
  77.6 4.2 fusion.55
  102.6 4.2 all-to-all-start
  108.1 40.7 %all-to-all-done = bf16[8,3,3,64,256]{4,3,2,1,0:T(8,128)(2,1)S(1)} async-done(((bf16[8,3,3,64,256]{4,3,2,1,0:T(8,128)(2,1)}), bf16[8,3,3,64,256]{4,3,2,1,0:T(8,128)(2,1)S(1)}, u32[]{:S(2)}, u32[]{:S(2)}) %all-to-all-start) | async-done | bytes 2359328 | tf_op jit(solution)/shard_map/all_to_all | solution.py:286
  150.5 17.1 %attn_fwd.1 = (bf16[3,64,2048]{2,1,0:T(8,128)(2,1)}, f32[3,1,2048]{2,1,0:T(1,128)}) custom-call(s32[3]{0:T(128)} %and_select_fusion.2.seg_ref, bf16[3,3,64,2048]{3,2,1,0:T(8,128)(2,1)} %bitcast.193, bf16[3,3,64,2048]{3,2,1,0:T(8,128)(2,1)} %bitcast.194, bf16[3,3,64,2048]{3,2,1,0:T(8,128)(2,1)} %bitcast.195), custom_call_target="tpu_custom_call" | custom-call | flops 2013265920 | bytes 3170304 | tf_op jit(solution)/shard_map/attn_fwd/pallas_call | solution.py:86
  169.8 3.5 all-to-all-start.1
  174.1 24.2 %all-gather = f32[24,1,2048]{2,1,0:T(1,128)S(1)} all-gather(f32[3,1,2048]{2,1,0:T(1,128)S(1)} %copy-done.14), channel_id=2, replica_groups=mesh['batch'=4,'seq'=8] {'seq'}, dimensions={0}, use_global_device_ids=true | all-gather | bytes 221184 | tf_op jit(solution)/shard_map/all_gather | solution.py:291
  203.3 8.4 %fusion.57 = f32[512,3072]{1,0:T(8,128)} fusion(bf16[768,3072]{1,0:T(8,128)(2,1)} %all-gather.10.cloned.1.call-done, f32[512,768]{1,0:T(8,128)} %copy-done.3, f32[768]{0:T(1024)S(1)} %copy-done.21, f32[768]{0:T(1024)S(1)} %copy-done.15, f32[512]{0:T(512)S(1)} %add_rsqrt_fusion, f32[512]{0:T(512)S(1)} %broadcast_multiply_fusion.5), kind=kOutput, calls=%fused_computation.141 | convolution fusion | flops 2417885184 | bytes 12593152 | tf_op jit(solution)/shard_map/dot_general | solution.py:299
  211.7 10.0 %fusion.6 = bf16[512,3072]{1,0:T(8,128)(2,1)S(1)} fusion(f32[512,3072]{1,0:T(8,128)} %fusion.57, bf16[3072,768]{0,1:T(8,128)(2,1)} %all-gather.12.cloned.1.call-done, bf16[512,768]{1,0:T(8,128)(2,1)} %param.16, f32[]{:T(128)} %bitcast), kind=kOutput, calls=%fused_computation.11 | convolution fusion | flops 2448556032 | bytes 14942212 | tf_op jit(solution)/shard_map/nd,fd->nf/dot_general | solution.py:317
  225.2 13.8 %fusion.32 = (bf16[512,768]{1,0:T(8,128)(2,1)}, f32[512,768]{1,0:T(8,128)S(1)}) fusion(f32[]{:T(128)} %bitcast.26, f32[]{:T(128)} %bitcast.24, f32[]{:T(128)} %bitcast.22, f32[]{:T(128)} %bitcast.20, f32[]{:T(128)} %bitcast.18, f32[]{:T(128)} %bitcast.16, f32[]{:T(128)} %bitcast.14, f32[]{:T(128)} %bitcast.12, f32[]{:T(128)} %bitcast, ...), kind=kOutput, calls=%fused_computation.64 | convolution fusion | flops 2440691712 | bytes 21233700 | tf_op jit(solution)/shard_map/dot_general | solution.py:302
  239.0 3.6 fusion.40
  245.2 15.3 %all_to_all.20 = bf16[8,3,64,256]{3,2,1,0:T(8,128)(2,1)S(1)} all-to-all(bf16[8,3,64,256]{3,2,1,0:T(8,128)(2,1)S(1)} %bitcast.190), channel_id=1, replica_groups=mesh['batch'=4,'seq'=8] {'seq'}, dimensions={0} | all-to-all | bytes 1572864 | tf_op jit(solution)/shard_map/all_to_all | solution.py:331
  261.5 20.8 %attn_bwd.1 = bf16[3,3,64,2048]{3,2,1,0:T(8,128)(2,1)} custom-call(s32[3]{0:T(128)} %and_select_fusion.2.seg_ref, bf16[3,3,64,2048]{3,2,1,0:T(8,128)(2,1)} %bitcast.196, bf16[3,3,64,2048]{3,2,1,0:T(8,128)(2,1)} %bitcast.197, bf16[3,3,64,2048]{3,2,1,0:T(8,128)(2,1)} %bitcast.198, bf16[3,64,2048]{2,1,0:T(8,128)(2,1)} %bitcast.203, ...), custom_call_target="tpu_custom_call" | custom-call | flops 5033164800 | bytes 6316032 | tf_op jit(solution)/shard_map/attn_bwd/pallas_call | solution.py:174
  285.7 3.6 all-to-all-start.3
  292.9 25.8 %all-to-all-done.3 = bf16[8,3,3,64,256]{4,3,2,1,0:T(8,128)(2,1)S(1)} async-done(((bf16[8,3,3,64,256]{4,3,2,1,0:T(8,128)(2,1)}), bf16[8,3,3,64,256]{4,3,2,1,0:T(8,128)(2,1)S(1)}, u32[]{:S(2)}, u32[]{:S(2)}) %all-to-all-start.3) | async-done | bytes 2359328 | tf_op jit(solution)/shard_map/all_to_all | solution.py:337
  327.5 4.1 convolution_convert_fusion.2
  333.1 6.8 convolution_convert_fusion.1
  341.0 9.1 %convolution_convert_fusion = bf16[3072,768]{1,0:T(8,128)(2,1)} fusion(bf16[512,768]{1,0:T(8,128)(2,1)S(1)} %copy-done.8, f32[]{:T(128)} %bitcast, f32[512,3072]{1,0:T(8,128)} %fusion.57), kind=kOutput, calls=%fused_computation.13 | convolution fusion | flops 2433613824 | bytes 11796484 | tf_op jit(solution)/shard_map/nf,nd->fd/dot_general | solution.py:316
  352.2 58.8 %reduce-scatter.17.cloned.1.call-done = bf16[192,2304]{1,0:T(8,128)(2,1)} async-done(((bf16[768,2304]{1,0:T(8,128)(2,1)}), bf16[192,2304]{1,0:T(8,128)(2,1)}) %reduce-scatter.17.cloned.1.call-update) | async-done | bytes 884752 | tf_op jit(solution)/shard_map/reduce_scatter | solution.py:350
  413.4 85.4 %reduce-scatter.21.cloned.1.call-done = bf16[192,3072]{1,0:T(8,128)(2,1)} async-done(((bf16[768,3072]{1,0:T(8,128)(2,1)}), bf16[192,3072]{1,0:T(8,128)(2,1)}) %reduce-scatter.21.cloned.1.call-update) | async-done | bytes 1179664 | tf_op jit(solution)/shard_map/reduce_scatter | solution.py:350
  502.2 4.5 multiply_convert_fusion
  507.3 79.7 %reduce-scatter.23.cloned.1.call-done = bf16[768,768]{1,0:T(8,128)(2,1)} async-done(((bf16[3072,768]{1,0:T(8,128)(2,1)}), bf16[768,768]{1,0:T(8,128)(2,1)}) %reduce-scatter.23.cloned.1.call-update) | async-done | bytes 1179664 | tf_op jit(solution)/shard_map/reduce_scatter | solution.py:350
  590.0 6.3 fusion.22
  596.4 5.9 concatenate.30
  602.3 24.0 %psum.14 = f32[3081]{0:T(1024)S(1)} all-reduce(f32[3081]{0:T(1024)S(1)} %concatenate.30), channel_id=1, replica_groups=mesh['batch'=4,'seq'=8] {'seq'}, use_global_device_ids=true, to_apply=%region_29.30 | all-reduce | flops 3081 | bytes 24648 | tf_op jit(solution)/shard_map/psum | solution.py:364
  626.2 18.3 %psum.15 = f32[3081]{0:T(1024)S(1)} all-reduce(f32[3081]{0:T(1024)S(1)} %psum.14), channel_id=1, replica_groups=mesh['batch'=4,'seq'=8] {'batch'}, use_global_device_ids=true, to_apply=%region_30.31 | all-reduce | flops 3081 | bytes 24648 | tf_op jit(solution)/shard_map/psum | solution.py:363
  650.0 14.2 %reduce-scatter.25.cloned.1.call-done = bf16[288,192]{1,0:T(8,128)(2,1)} async-done(((bf16[2304,192]{1,0:T(8,128)(2,1)}), bf16[288,192]{1,0:T(8,128)(2,1)}) %reduce-scatter.25.cloned.1.call-update) | async-done | bytes 110608
  666.0 39.9 %reduce-scatter.29.cloned.1.call-done = bf16[384,192]{1,0:T(8,128)(2,1)} async-done(((bf16[3072,192]{1,0:T(8,128)(2,1)}), bf16[384,192]{1,0:T(8,128)(2,1)}) %reduce-scatter.29.cloned.1.call-update) | async-done | bytes 147472
  707.7 38.0 %reduce-scatter.31.cloned.1.call-done = bf16[96,768]{1,0:T(8,128)(2,1)} async-done(((bf16[768,768]{1,0:T(8,128)(2,1)}), bf16[96,768]{1,0:T(8,128)(2,1)}) %reduce-scatter.31.cloned.1.call-update) | async-done | bytes 147472
  (176 shorter events, 84.0 us)
Async XLA Ops:
  7.2 19.7 %copy-start.13 = (bf16[192,96]{1,0:T(8,128)(2,1)S(1)}, bf16[192,96]{1,0:T(8,128)(2,1)}, u32[]{:S(2)}) copy-start(bf16[192,96]{1,0:T(8,128)(2,1)} %param.18) | copy-start | bytes 110596
  7.2 34.2 %copy-start.10 = (bf16[192,384]{1,0:T(8,128)(2,1)S(1)}, bf16[192,384]{1,0:T(8,128)(2,1)}, u32[]{:S(2)}) copy-start(bf16[192,384]{1,0:T(8,128)(2,1)} %param.19) | copy-start | bytes 442372
  7.2 70.4 %all-gather.6.cloned.1.call-start = ((), (), s32[]{:S(2)}) async-start(), calls=%async_computation.12 | async-start | bytes 3981312 | tf_op jit(solution)/shard_map/all_gather | solution.py:268
  25.8 33.2 %copy-start.11 = (bf16[768,96]{0,1:T(8,128)(2,1)S(1)}, bf16[768,96]{0,1:T(8,128)(2,1)}, u32[]{:S(2)}) copy-start(bf16[768,96]{0,1:T(8,128)(2,1)} %param.20) | copy-start | bytes 442372
  26.9 172.5 %all-gather.8.cloned.1.call-start = ((), (), s32[]{:S(2)}) async-start(), calls=%async_computation.13 | async-start | bytes 1327104 | tf_op jit(solution)/shard_map/all_gather | solution.py:269
  40.5 34.4 %copy-start.22 = (s32[1,2]{1,0:T(1,128)S(1)}, s32[1,2]{1,0:T(1,128)}, u32[]{:S(2)}) copy-start(s32[1,2]{1,0:T(1,128)} %param.27) | copy-start | bytes 28
  41.3 35.6 %copy-start.2 = (bf16[512,768]{1,0:T(8,128)(2,1)S(1)}, bf16[512,768]{1,0:T(8,128)(2,1)}, u32[]{:S(2)}) copy-start(bf16[512,768]{1,0:T(8,128)(2,1)} %param.14) | copy-start | bytes 2359300
  41.4 161.9 %all-gather.10.cloned.1.call-start = ((), (), s32[]{:S(2)}) async-start(), calls=%async_computation.14 | async-start | bytes 5308416 | tf_op jit(solution)/shard_map/all_gather | solution.py:270
  59.0 152.7 %all-gather.12.cloned.1.call-start = ((), (), s32[]{:S(2)}) async-start(), calls=%async_computation.15 | async-start | bytes 5308416 | tf_op jit(solution)/shard_map/all_gather | solution.py:271
  74.9 2.7 copy-start.20
  102.6 46.2 %all-to-all-start = ((bf16[8,3,3,64,256]{4,3,2,1,0:T(8,128)(2,1)}), bf16[8,3,3,64,256]{4,3,2,1,0:T(8,128)(2,1)S(1)}, u32[]{:S(2)}, u32[]{:S(2)}) async-start(bf16[8,3,3,64,256]{4,3,2,1,0:T(8,128)(2,1)} %copy.93), calls=%async_computation | async-start | bytes 4718592 | tf_op jit(solution)/shard_map/all_to_all | solution.py:286
  167.7 5.7 copy-start.12
  167.7 6.4 copy-start.14
  169.8 28.5 %all-to-all-start.1 = ((bf16[8,3,64,256]{3,2,1,0:T(8,128)(2,1)}), bf16[8,3,64,256]{3,2,1,0:T(8,128)(2,1)S(1)}, u32[]{:S(2)}, u32[]{:S(2)}) async-start(bf16[8,3,64,256]{3,2,1,0:T(8,128)(2,1)} %bitcast.164), calls=%async_computation.1 | async-start | bytes 1572864 | tf_op jit(solution)/shard_map/all_to_all | solution.py:290
  203.3 21.5 %slice-start = ((s8[6291456]{0:T(1024)(128)(4,1)}), s8[2097152]{0:T(1024)(128)(4,1)S(1)}, s32[]{:S(2)}) async-start(s8[6291456]{0:T(1024)(128)(4,1)} %bitcast.172), calls=%async_computation.24 | async-start | bytes 4194304
  211.7 10.0 %copy-start.4 = (f32[512,768]{1,0:T(8,128)S(1)}, f32[512,768]{1,0:T(8,128)}, u32[]{:S(2)}) copy-start(f32[512,768]{1,0:T(8,128)} %copy-done.3) | copy-start | bytes 4718596
  211.7 10.0 %copy-start.17 = (bf16[768,3072]{1,0:T(8,128)(2,1)S(1)}, bf16[768,3072]{1,0:T(8,128)(2,1)}, u32[]{:S(2)}) copy-start(bf16[768,3072]{1,0:T(8,128)(2,1)} %all-gather.10.cloned.1.call-done) | copy-start | bytes 14155780
  211.7 13.1 %slice-start.1 = ((s8[6291456]{0:T(1024)(128)(4,1)}), s8[4194304]{0:T(1024)(128)(4,1)S(1)}, s32[]{:S(2)}) async-start(s8[6291456]{0:T(1024)(128)(4,1)} %bitcast.172), calls=%async_computation.25 | async-start | bytes 8388608
  221.7 3.1 copy-start.24
  221.7 3.5 copy-start.18
  225.2 13.8 %copy-start.7 = (bf16[512,768]{1,0:T(8,128)(2,1)S(1)}, bf16[512,768]{1,0:T(8,128)(2,1)}, u32[]{:S(2)}) copy-start(bf16[512,768]{1,0:T(8,128)(2,1)} %param.16) | copy-start | bytes 2359300
  239.0 4.8 copy-start.19
  285.7 33.0 %all-to-all-start.3 = ((bf16[8,3,3,64,256]{4,3,2,1,0:T(8,128)(2,1)}), bf16[8,3,3,64,256]{4,3,2,1,0:T(8,128)(2,1)S(1)}, u32[]{:S(2)}, u32[]{:S(2)}) async-start(bf16[8,3,3,64,256]{4,3,2,1,0:T(8,128)(2,1)} %bitcast.170), calls=%async_computation.3 | async-start | bytes 4718592 | tf_op jit(solution)/shard_map/all_to_all | solution.py:337
  289.3 60.8 %reduce-scatter.19.cloned.1.call-start = ((), (), s32[]{:S(2)}) async-start(), calls=%async_computation.17 | async-start | bytes 1474560 | tf_op jit(solution)/shard_map/reduce_scatter | solution.py:350
  292.9 118.1 %reduce-scatter.17.cloned.1.call-start = ((), (), s32[]{:S(2)}) async-start(), calls=%async_computation.16 | async-start | bytes 4423680 | tf_op jit(solution)/shard_map/reduce_scatter | solution.py:350
  331.7 167.1 %reduce-scatter.21.cloned.1.call-start = ((), (), s32[]{:S(2)}) async-start(), calls=%async_computation.18 | async-start | bytes 5898240 | tf_op jit(solution)/shard_map/reduce_scatter | solution.py:350
  339.9 247.1 %reduce-scatter.23.cloned.1.call-start = ((), (), s32[]{:S(2)}) async-start(), calls=%async_computation.19 | async-start | bytes 5898240 | tf_op jit(solution)/shard_map/reduce_scatter | solution.py:350
  350.1 298.4 %reduce-scatter.27.cloned.1.call-start = ((), (), s32[]{:S(2)}) async-start(), calls=%async_computation.21 | async-start | bytes 442368
  352.1 312.1 %reduce-scatter.25.cloned.1.call-start = ((), (), s32[]{:S(2)}) async-start(), calls=%async_computation.20 | async-start | bytes 1327104
  413.3 292.6 %reduce-scatter.29.cloned.1.call-start = ((), (), s32[]{:S(2)}) async-start(), calls=%async_computation.22 | async-start | bytes 1769472
  501.4 244.4 %reduce-scatter.31.cloned.1.call-start = ((), (), s32[]{:S(2)}) async-start(), calls=%async_computation.23 | async-start | bytes 1327104
  590.0 55.6 %copy-start.1 = (f32[512,768]{1,0:T(8,128)S(1)}, f32[512,768]{1,0:T(8,128)}, u32[]{:S(2)}) copy-start(f32[512,768]{1,0:T(8,128)} %copy-done) | copy-start | bytes 4718596
  (10 other events, 15.2 us)
Sparse Core Ops, SparseCore 0:
  27.0 35.0 all-gather.5
  64.5 23.9 all-gather.7
  90.4 53.8 all-gather.9
  146.0 54.0 all-gather.11
  293.0 44.1 reduce-scatter.18
  339.4 71.5 reduce-scatter.16
  413.3 85.4 reduce-scatter.20
  501.1 85.7 reduce-scatter.22
  590.0 34.3 reduce-scatter.26
  627.5 36.6 reduce-scatter.24
  667.6 38.3 reduce-scatter.28
  709.0 36.6 reduce-scatter.30

commit v7 on v5

--- a/solution.py
+++ b/solution.py
@@ -261,7 +261,6 @@
     w_qkv = lax.all_gather(
         lax.all_gather(qkv_weight, "batch", axis=0, tiled=True), "seq", axis=1, tiled=True
     )
-    later = (proj_weight, up_weight, down_weight)
     inputs32 = block_input.astype(jnp.float32)
     norm1_out, normed1, inv_std1 = norm_rows(inputs32, norm1_gain, norm1_bias)
     norm1_low = norm1_out.astype(jnp.bfloat16)
@@ -276,14 +275,13 @@
         stacked.reshape(slot_count, piece_len, 3, head_groups, per_dev, HD), (0, 3, 4, 2, 5, 1)
     ).reshape(n_seq, per_dev, 3, HD, piece_len)
     incoming = lax.all_to_all(send, "seq", split_axis=0, concat_axis=0, tiled=True)
-    later_rows = lax.all_gather(jnp.concatenate([w.reshape(-1) for w in later]), "batch", axis=0)
-    offset = 0
-    later_full = []
-    for w in later:
-        rows = later_rows[:, offset : offset + w.size].reshape(-1, w.shape[1])
-        later_full.append(lax.all_gather(rows, "seq", axis=1, tiled=True))
-        offset += w.size
-    w_proj, w_up, w_down = later_full
+    later_rows = [
+        lax.all_gather(w, "batch", axis=0, tiled=True)
+        for w in (proj_weight, up_weight, down_weight)
+    ]
+    w_proj, w_up, w_down = (
+        lax.all_gather(rows, "seq", axis=1, tiled=True) for rows in later_rows
+    )
     qkv_t = jnp.transpose(incoming, (1, 2, 3, 0, 4)).reshape(per_dev, 3, HD, SLOT)
     attn_t, lse_rows = attn_forward(qkv_t, seg_pairs)
     back = jnp.transpose(attn_t.reshape(per_dev, HD, n_seq, piece_len), (2, 0, 1, 3))

time: 581 us -> 588 us (1.012)
  blocking collectives: 103 us -> 149 us
  waiting for transfers between devices: 237 us -> 203 us
  local copies, waits for them, and re-layouts: 68.7 us -> 59.2 us
    all_gather x0 -> x3, blocking collectives: none -> 46.9 us  [local(): lax.all_gather(w, 'batch', axis=0, tiled=True)]
    all_gather x1, waiting for transfers between devices: 26.8 us -> 0.02 us  [local(): lax.all_gather(lax.all_gather(qkv_weight, 'batch', axis=0, tiled=True), '...]
    all_gather x4 -> x3, waiting for transfers between devices: 20.5 us -> 0.04 us  [local(): lax.all_gather(rows, 'seq', axis=1, tiled=True)]
    all_to_all x1, waiting for transfers between devices: 34.4 us -> 40.8 us  [local(): lax.all_to_all(send, 'seq', split_axis=0, concat_axis=0, tiled=True)]
    reshape x8 -> x0, local copies, waits for them, and re-layouts: 6.1 us -> none  [the longest x5 3.9 us: local(): rows = later_rows[:, offset:offset + w.size].reshape(-1, w.shape[1])]
    unnamed x16 -> x15, waiting for transfers between devices: 33.8 us -> 35.4 us
    unnamed x61 -> x64, local copies, waits for them, and re-layouts: 22.6 us -> 21.4 us
  transfers between devices with their start and end apart: 16 -> 15, of which waited for: 9 -> 7; matrix products, arithmetic and copies ran while one was open for 22% -> 21% of each run, Pallas kernels for 7% -> 7%
where the time goes in v7:
time: 588 us; the launch traced here: 577 us
  waiting for transfers between devices  203 us (35%)
  blocking collectives  149 us (25%)
  matrix products  71.2 us (12%)
  local copies, waits for them, and re-layouts  59.2 us (10%)
  Pallas kernels  38.1 us (6%)
  other arithmetic  29.3 us (5%)
  between operations  15.3 us (3%)
  starting transfers between devices  12.4 us (2%)
    reduce_scatter x1, waiting for transfers between devices, local(): lax.psum_scatter(down_local.astype(jnp.bfloat16), 'seq', scatter_dimensio...  49.9 us
    all_gather x3, blocking collectives, local(): lax.all_gather(w, 'batch', axis=0, tiled=True)  46.9 us
    reduce_scatter x1, waiting for transfers between devices, local(): lax.psum_scatter(qkv_local.astype(jnp.bfloat16), 'seq', scatter_dimension...  41.8 us
    all_to_all x1, waiting for transfers between devices, local(): lax.all_to_all(send, 'seq', split_axis=0, concat_axis=0, tiled=True)  40.8 us
    unnamed x15, waiting for transfers between devices  35.4 us
    all_to_all x1, waiting for transfers between devices, local(): lax.all_to_all(dback, 'seq', split_axis=0, concat_axis=0, tiled=True)  34.9 us
    all_gather x1, blocking collectives, local(): lax.all_gather(lse_rows.reshape(per_dev, SLOT), 'seq', axis=0, tiled=True)  24.1 us
    psum x1, blocking collectives, local(): lax.psum(jnp.concatenate([gain1_local, bias1_local, gain2_local, bias2_lo...  23.5 us
  transfers between devices with their start and end apart: 15, of which 7 were waited for; matrix products, arithmetic and copies ran while one was open for 21% of the time, Pallas kernels for 7%

profile of v7, /device:TPU:0, one launch (start us, length us, event | category | flops | bytes accessed | tf_op | source)
XLA Modules:
  0.0 576.9 jit_solution(6232310997926149501)
XLA Ops:
  7.2 18.6 %all_gather.27 = bf16[768,288]{1,0:T(8,128)(2,1)S(1)} all-gather(bf16[192,288]{1,0:T(8,128)(2,1)} %param.17), channel_id=1, replica_groups=mesh['batch'=4,'seq'=8] {'batch'}, dimensions={0}, use_global_device_ids=true | all-gather | bytes 552960 | tf_op jit(solution)/shard_map/all_gather | solution.py:262
  26.9 13.6 %all_gather.30 = bf16[768,96]{1,0:T(8,128)(2,1)S(1)} all-gather(bf16[192,96]{1,0:T(8,128)(2,1)S(1)} %copy-done.11), channel_id=1, replica_groups=mesh['batch'=4,'seq'=8] {'batch'}, dimensions={0}, use_global_device_ids=true | all-gather | bytes 184320 | tf_op jit(solution)/shard_map/all_gather | solution.py:279
  41.4 17.5 %all_gather.32 = bf16[768,384]{1,0:T(8,128)(2,1)} all-gather(bf16[192,384]{1,0:T(8,128)(2,1)S(1)} %copy-done.8), channel_id=1, replica_groups=mesh['batch'=4,'seq'=8] {'batch'}, dimensions={0}, use_global_device_ids=true | all-gather | bytes 737280 | tf_op jit(solution)/shard_map/all_gather | solution.py:279
  59.0 15.8 %all_gather.34 = bf16[3072,96]{0,1:T(8,128)(2,1)} all-gather(bf16[768,96]{0,1:T(8,128)(2,1)S(1)} %copy-done.9), channel_id=1, replica_groups=mesh['batch'=4,'seq'=8] {'batch'}, dimensions={0}, use_global_device_ids=true | all-gather | bytes 737280 | tf_op jit(solution)/shard_map/all_gather | solution.py:279
  77.6 4.2 fusion.55
  102.6 4.1 all-to-all-start
  107.9 40.8 %all-to-all-done = bf16[8,3,3,64,256]{4,3,2,1,0:T(8,128)(2,1)S(1)} async-done(((bf16[8,3,3,64,256]{4,3,2,1,0:T(8,128)(2,1)}), bf16[8,3,3,64,256]{4,3,2,1,0:T(8,128)(2,1)S(1)}, u32[]{:S(2)}, u32[]{:S(2)}) %all-to-all-start) | async-done | bytes 2359328 | tf_op jit(solution)/shard_map/all_to_all | solution.py:277
  150.4 17.1 %attn_fwd.1 = (bf16[3,64,2048]{2,1,0:T(8,128)(2,1)}, f32[3,1,2048]{2,1,0:T(1,128)}) custom-call(s32[3]{0:T(128)} %and_select_fusion.2.seg_ref, bf16[3,3,64,2048]{3,2,1,0:T(8,128)(2,1)} %bitcast.187, bf16[3,3,64,2048]{3,2,1,0:T(8,128)(2,1)} %bitcast.188, bf16[3,3,64,2048]{3,2,1,0:T(8,128)(2,1)} %bitcast.189), custom_call_target="tpu_custom_call" | custom-call | flops 2013265920 | bytes 3170304 | tf_op jit(solution)/shard_map/attn_fwd/pallas_call | solution.py:86
  169.7 3.5 all-to-all-start.1
  174.0 24.1 %all-gather = f32[24,1,2048]{2,1,0:T(1,128)S(1)} all-gather(f32[3,1,2048]{2,1,0:T(1,128)S(1)} %copy-done.12), channel_id=2, replica_groups=mesh['batch'=4,'seq'=8] {'seq'}, dimensions={0}, use_global_device_ids=true | all-gather | bytes 221184 | tf_op jit(solution)/shard_map/all_gather | solution.py:289
  202.1 7.0 %fusion.57 = f32[512,3072]{1,0:T(8,128)} fusion(bf16[768,3072]{1,0:T(8,128)(2,1)} %all-gather.10.cloned.1.call-done, f32[512,768]{1,0:T(8,128)S(1)} %get-tuple-element.138, f32[768]{0:T(1024)S(1)} %copy-done.17, f32[768]{0:T(1024)S(1)} %copy-done.13, f32[512]{0:T(512)S(1)} %add_rsqrt_fusion, f32[512]{0:T(512)S(1)} %broadcast_multiply_fusion.5), kind=kOutput, calls=%fused_computation.141 | convolution fusion | flops 2417885184 | bytes 12593152 | tf_op jit(solution)/shard_map/dot_general | solution.py:297
  209.1 9.5 %fusion.6 = bf16[512,3072]{1,0:T(8,128)(2,1)S(1)} fusion(f32[512,3072]{1,0:T(8,128)} %fusion.57, bf16[3072,768]{0,1:T(8,128)(2,1)} %all-gather.12.cloned.1.call-done, bf16[512,768]{1,0:T(8,128)(2,1)} %param.16, f32[]{:T(128)} %bitcast), kind=kOutput, calls=%fused_computation.11 | convolution fusion | flops 2448556032 | bytes 14942212 | tf_op jit(solution)/shard_map/nd,fd->nf/dot_general | solution.py:315
  222.2 15.2 %fusion.32 = (bf16[512,768]{1,0:T(8,128)(2,1)}, f32[512,768]{1,0:T(8,128)S(1)}) fusion(f32[]{:T(128)} %bitcast.26, f32[]{:T(128)} %bitcast.24, f32[]{:T(128)} %bitcast.22, f32[]{:T(128)} %bitcast.20, f32[]{:T(128)} %bitcast.18, f32[]{:T(128)} %bitcast.16, f32[]{:T(128)} %bitcast.14, f32[]{:T(128)} %bitcast.12, f32[]{:T(128)} %bitcast, ...), kind=kOutput, calls=%fused_computation.64 | convolution fusion | flops 2440691712 | bytes 21233700 | tf_op jit(solution)/shard_map/dot_general | solution.py:300
  237.3 5.0 fusion.40
  244.4 7.4 %convolution_convert_fusion.2 = bf16[768,3072]{1,0:T(8,128)(2,1)} fusion(bf16[512,3072]{1,0:T(8,128)(2,1)} %copy-done.21, f32[512,768]{1,0:T(8,128)} %copy-done.3, f32[768]{0:T(1024)S(1)} %copy-done.17, f32[768]{0:T(1024)S(1)} %copy-done.13, f32[512]{0:T(512)S(1)} %add_rsqrt_fusion, f32[512]{0:T(512)S(1)} %broadcast_multiply_fusion.5), kind=kOutput, calls=%fused_computation.15 | convolution fusion | flops 2420244480 | bytes 9447424 | tf_op jit(solution)/shard_map/nd,nf->df/dot_general | solution.py:317
  251.8 6.7 %copy.119 = bf16[768,3072]{0,1:T(8,128)(2,1)} copy(bf16[768,3072]{1,0:T(8,128)(2,1)} %convolution_convert_fusion.2) | data formatting | bytes 9437184
  259.7 8.6 %convolution_convert_fusion.1 = bf16[3072,768]{0,1:T(8,128)(2,1)} fusion(bf16[512,768]{1,0:T(8,128)(2,1)S(1)} %copy-done.5, f32[]{:T(128)} %bitcast, f32[512,3072]{1,0:T(8,128)} %fusion.57), kind=kOutput, calls=%fused_computation.14 | convolution fusion | flops 2433613824 | bytes 11796484 | tf_op jit(solution)/shard_map/nf,nd->fd/dot_general | solution.py:314
  271.0 16.7 %all_to_all.20 = bf16[8,3,64,256]{3,2,1,0:T(8,128)(2,1)S(1)} all-to-all(bf16[8,3,64,256]{3,2,1,0:T(8,128)(2,1)S(1)} %bitcast.183), channel_id=1, replica_groups=mesh['batch'=4,'seq'=8] {'seq'}, dimensions={0} | all-to-all | bytes 1572864 | tf_op jit(solution)/shard_map/all_to_all | solution.py:329
  288.7 20.9 %attn_bwd.1 = bf16[3,3,64,2048]{3,2,1,0:T(8,128)(2,1)} custom-call(s32[3]{0:T(128)} %and_select_fusion.2.seg_ref, bf16[3,3,64,2048]{3,2,1,0:T(8,128)(2,1)} %bitcast.190, bf16[3,3,64,2048]{3,2,1,0:T(8,128)(2,1)} %bitcast.191, bf16[3,3,64,2048]{3,2,1,0:T(8,128)(2,1)} %bitcast.192, bf16[3,64,2048]{2,1,0:T(8,128)(2,1)} %bitcast.196, ...), custom_call_target="tpu_custom_call" | custom-call | flops 5033164800 | bytes 6316032 | tf_op jit(solution)/shard_map/attn_bwd/pallas_call | solution.py:174
  309.7 3.4 copy.141
  313.0 3.6 all-to-all-start.3
  318.7 34.9 %all-to-all-done.3 = bf16[8,3,3,64,256]{4,3,2,1,0:T(8,128)(2,1)S(1)} async-done(((bf16[8,3,3,64,256]{4,3,2,1,0:T(8,128)(2,1)}), bf16[8,3,3,64,256]{4,3,2,1,0:T(8,128)(2,1)S(1)}, u32[]{:S(2)}, u32[]{:S(2)}) %all-to-all-start.3) | async-done | bytes 2359328 | tf_op jit(solution)/shard_map/all_to_all | solution.py:335
  362.5 4.0 convolution_convert_fusion
  370.9 4.5 multiply_convert_fusion
  375.5 49.9 %reduce-scatter.21.cloned.1.call-done = bf16[3072,96]{0,1:T(8,128)(2,1)} async-done(((bf16[3072,768]{0,1:T(8,128)(2,1)}), bf16[3072,96]{0,1:T(8,128)(2,1)}) %reduce-scatter.21.cloned.1.call-update) | async-done | bytes 589840 | tf_op jit(solution)/shard_map/reduce_scatter | solution.py:357
  427.0 20.8 %reduce-scatter.27.cloned.1.call-done = bf16[192,96]{1,0:T(8,128)(2,1)} async-done(((bf16[768,96]{1,0:T(8,128)(2,1)}), bf16[192,96]{1,0:T(8,128)(2,1)}) %reduce-scatter.27.cloned.1.call-update) | async-done | bytes 36880
  449.4 6.2 %fusion.22 = (f32[768]{0:T(1024)S(1)}, f32[512]{0:T(512)S(1)}, f32[512]{0:T(512)S(1)}, f32[768]{0:T(1024)S(1)}, f32[512,768]{1,0:T(8,128)}) fusion(bf16[512,768]{1,0:T(8,128)(2,1)S(1)} %copy-done.2, f32[512]{0:T(512)S(1)} %add_rsqrt_fusion.1, f32[512]{0:T(512)S(1)} %broadcast_multiply_fusion.6, f32[768]{0:T(1024)S(1)} %copy-done.14, ...), kind=kOutput, calls=%fused_computation.54 | convolution fusion | flops 1815868928 | bytes 8274944 | tf_op jit(solution)/shard_map/nf,df->nd/dot_general | solution.py:344
  455.6 41.8 %reduce-scatter.15.cloned.1.call-done = bf16[768,288]{0,1:T(8,128)(2,1)} async-done(((bf16[768,2304]{0,1:T(8,128)(2,1)}), bf16[768,288]{0,1:T(8,128)(2,1)}) %reduce-scatter.15.cloned.1.call-update) | async-done | bytes 442384 | tf_op jit(solution)/shard_map/reduce_scatter | solution.py:348
  499.6 5.7 concatenate.30
  505.3 23.5 %psum.14 = f32[3081]{0:T(1024)S(1)} all-reduce(f32[3081]{0:T(1024)S(1)} %concatenate.30), channel_id=1, replica_groups=mesh['batch'=4,'seq'=8] {'seq'}, use_global_device_ids=true, to_apply=%region_29.30 | all-reduce | flops 3081 | bytes 24648 | tf_op jit(solution)/shard_map/psum | solution.py:376
  528.7 18.8 %psum.15 = f32[3081]{0:T(1024)S(1)} all-reduce(f32[3081]{0:T(1024)S(1)} %psum.14), channel_id=1, replica_groups=mesh['batch'=4,'seq'=8] {'batch'}, use_global_device_ids=true, to_apply=%region_30.31 | all-reduce | flops 3081 | bytes 24648 | tf_op jit(solution)/shard_map/psum | solution.py:375
  554.8 13.0 %reduce-scatter.25.cloned.1.call-done = bf16[192,288]{1,0:T(8,128)(2,1)} async-done(((bf16[768,288]{1,0:T(8,128)(2,1)}), bf16[192,288]{1,0:T(8,128)(2,1)}) %reduce-scatter.25.cloned.1.call-update) | async-done | bytes 110608
  (168 shorter events, 75.1 us)
Async XLA Ops:
  7.2 19.7 %copy-start.11 = (bf16[192,96]{1,0:T(8,128)(2,1)S(1)}, bf16[192,96]{1,0:T(8,128)(2,1)}, u32[]{:S(2)}) copy-start(bf16[192,96]{1,0:T(8,128)(2,1)} %param.18) | copy-start | bytes 110596
  7.2 34.2 %copy-start.8 = (bf16[192,384]{1,0:T(8,128)(2,1)S(1)}, bf16[192,384]{1,0:T(8,128)(2,1)}, u32[]{:S(2)}) copy-start(bf16[192,384]{1,0:T(8,128)(2,1)} %param.19) | copy-start | bytes 442372
  7.2 70.4 %all-gather.6.cloned.1.call-start = ((), (), s32[]{:S(2)}) async-start(), calls=%async_computation.12 | async-start | bytes 3981312 | tf_op jit(solution)/shard_map/all_gather | solution.py:261
  25.8 33.2 %copy-start.9 = (bf16[768,96]{0,1:T(8,128)(2,1)S(1)}, bf16[768,96]{0,1:T(8,128)(2,1)}, u32[]{:S(2)}) copy-start(bf16[768,96]{0,1:T(8,128)(2,1)} %param.20) | copy-start | bytes 442372
  26.9 172.3 %all-gather.8.cloned.1.call-start = ((), (), s32[]{:S(2)}) async-start(), calls=%async_computation.13 | async-start | bytes 1327104 | tf_op jit(solution)/shard_map/all_gather | solution.py:283
  40.5 34.4 %copy-start.19 = (s32[1,2]{1,0:T(1,128)S(1)}, s32[1,2]{1,0:T(1,128)}, u32[]{:S(2)}) copy-start(s32[1,2]{1,0:T(1,128)} %param.27) | copy-start | bytes 28
  41.3 35.6 %copy-start.2 = (bf16[512,768]{1,0:T(8,128)(2,1)S(1)}, bf16[512,768]{1,0:T(8,128)(2,1)}, u32[]{:S(2)}) copy-start(bf16[512,768]{1,0:T(8,128)(2,1)} %param.14) | copy-start | bytes 2359300
  41.4 160.4 %all-gather.10.cloned.1.call-start = ((), (), s32[]{:S(2)}) async-start(), calls=%async_computation.14 | async-start | bytes 5308416 | tf_op jit(solution)/shard_map/all_gather | solution.py:283
  59.0 150.2 %all-gather.12.cloned.1.call-start = ((), (), s32[]{:S(2)}) async-start(), calls=%async_computation.15 | async-start | bytes 5308416 | tf_op jit(solution)/shard_map/all_gather | solution.py:283
  102.6 46.1 %all-to-all-start = ((bf16[8,3,3,64,256]{4,3,2,1,0:T(8,128)(2,1)}), bf16[8,3,3,64,256]{4,3,2,1,0:T(8,128)(2,1)S(1)}, u32[]{:S(2)}, u32[]{:S(2)}) async-start(bf16[8,3,3,64,256]{4,3,2,1,0:T(8,128)(2,1)} %copy.97), calls=%async_computation | async-start | bytes 4718592 | tf_op jit(solution)/shard_map/all_to_all | solution.py:277
  167.5 5.7 copy-start.10
  167.5 6.4 %copy-start.12 = (f32[3,1,2048]{2,1,0:T(1,128)S(1)}, f32[3,1,2048]{2,1,0:T(1,128)}, u32[]{:S(2)}) copy-start(f32[3,1,2048]{2,1,0:T(1,128)} %get-tuple-element.17.lse_ref) | copy-start | bytes 73732
  169.7 28.5 %all-to-all-start.1 = ((bf16[8,3,64,256]{3,2,1,0:T(8,128)(2,1)}), bf16[8,3,64,256]{3,2,1,0:T(8,128)(2,1)S(1)}, u32[]{:S(2)}, u32[]{:S(2)}) async-start(bf16[8,3,64,256]{3,2,1,0:T(8,128)(2,1)} %bitcast.160), calls=%async_computation.1 | async-start | bytes 1572864 | tf_op jit(solution)/shard_map/all_to_all | solution.py:288
  173.2 143.5 %reduce-scatter.17.cloned.1.call-start = ((), (), s32[]{:S(2)}) async-start(), calls=%async_computation.17 | async-start | bytes 1327104 | tf_op jit(solution)/shard_map/reduce_scatter | solution.py:351
  201.4 20.4 %copy-start.3 = (f32[512,768]{1,0:T(8,128)}, f32[512,768]{1,0:T(8,128)S(1)}, u32[]{:S(2)}) copy-start(f32[512,768]{1,0:T(8,128)S(1)} %get-tuple-element.138) | copy-start | bytes 4718596
  209.1 9.5 %copy-start.15 = (bf16[768,3072]{1,0:T(8,128)(2,1)S(1)}, bf16[768,3072]{1,0:T(8,128)(2,1)}, u32[]{:S(2)}) copy-start(bf16[768,3072]{1,0:T(8,128)(2,1)} %all-gather.10.cloned.1.call-done) | copy-start | bytes 14155780
  218.7 3.0 copy-start.21
  218.7 3.5 copy-start.16
  221.7 15.6 %slice-start = ((s8[6291456]{0:T(1024)(128)(4,1)}), s8[4194304]{0:T(1024)(128)(4,1)S(1)}, s32[]{:S(2)}) async-start(s8[6291456]{0:T(1024)(128)(4,1)} %bitcast.169), calls=%async_computation.24 | async-start | bytes 8388608
  222.1 15.2 %slice-start.1 = ((s8[6291456]{0:T(1024)(128)(4,1)}), s8[2097152]{0:T(1024)(128)(4,1)S(1)}, s32[]{:S(2)}) async-start(s8[6291456]{0:T(1024)(128)(4,1)} %bitcast.169), calls=%async_computation.25 | async-start | bytes 4194304
  222.2 15.2 %copy-start.4 = (bf16[512,768]{1,0:T(8,128)(2,1)S(1)}, bf16[512,768]{1,0:T(8,128)(2,1)}, u32[]{:S(2)}) copy-start(bf16[512,768]{1,0:T(8,128)(2,1)} %param.16) | copy-start | bytes 2359300
  242.3 26.0 %copy-start = (f32[512,768]{1,0:T(8,128)}, f32[512,768]{1,0:T(8,128)S(1)}, u32[]{:S(2)}) copy-start(f32[512,768]{1,0:T(8,128)S(1)} %get-tuple-element.117) | copy-start | bytes 4718596
  244.2 123.8 %reduce-scatter.29.cloned.1.call-start = ((), (), s32[]{:S(2)}) async-start(), calls=%async_computation.23 | async-start | bytes 5308416
  258.6 166.8 %reduce-scatter.21.cloned.1.call-start = ((), (), s32[]{:S(2)}) async-start(), calls=%async_computation.19 | async-start | bytes 5308416 | tf_op jit(solution)/shard_map/reduce_scatter | solution.py:357
  313.0 40.6 %all-to-all-start.3 = ((bf16[8,3,3,64,256]{4,3,2,1,0:T(8,128)(2,1)}), bf16[8,3,3,64,256]{4,3,2,1,0:T(8,128)(2,1)S(1)}, u32[]{:S(2)}, u32[]{:S(2)}) async-start(bf16[8,3,3,64,256]{4,3,2,1,0:T(8,128)(2,1)} %bitcast.166), calls=%async_computation.3 | async-start | bytes 4718592 | tf_op jit(solution)/shard_map/all_to_all | solution.py:335
  316.7 131.1 %reduce-scatter.27.cloned.1.call-start = ((), (), s32[]{:S(2)}) async-start(), calls=%async_computation.22 | async-start | bytes 245760
  318.5 179.0 %reduce-scatter.15.cloned.1.call-start = ((), (), s32[]{:S(2)}) async-start(), calls=%async_computation.16 | async-start | bytes 3981312 | tf_op jit(solution)/shard_map/reduce_scatter | solution.py:348
  366.5 3.7 copy-start.6
  366.6 184.9 %reduce-scatter.19.cloned.1.call-start = ((), (), s32[]{:S(2)}) async-start(), calls=%async_computation.18 | async-start | bytes 737280 | tf_op jit(solution)/shard_map/reduce_scatter | solution.py:368
  370.2 182.9 %reduce-scatter.23.cloned.1.call-start = ((), (), s32[]{:S(2)}) async-start(), calls=%async_computation.20 | async-start | bytes 737280 | tf_op jit(solution)/shard_map/reduce_scatter | solution.py:371
  425.4 142.4 %reduce-scatter.25.cloned.1.call-start = ((), (), s32[]{:S(2)}) async-start(), calls=%async_computation.21 | async-start | bytes 737280
  455.6 93.0 %copy-start.1 = (f32[512,768]{1,0:T(8,128)S(1)}, f32[512,768]{1,0:T(8,128)}, u32[]{:S(2)}) copy-start(f32[512,768]{1,0:T(8,128)} %copy-done) | copy-start | bytes 4718596
  (7 other events, 10.1 us)
Sparse Core Ops, SparseCore 0:
  27.0 35.0 all-gather.5
  64.5 23.9 all-gather.7
  90.4 53.7 all-gather.9
  145.9 54.0 all-gather.11
  244.3 42.4 reduce-scatter.16
  290.1 77.8 reduce-scatter.28
  371.5 53.7 reduce-scatter.20
  428.2 19.5 reduce-scatter.26
  451.3 46.1 reduce-scatter.14
  499.6 22.1 reduce-scatter.18
  524.1 20.7 reduce-scatter.22
  547.0 20.6 reduce-scatter.24

commit v8 on v6

--- a/solution.py
+++ b/solution.py
@@ -258,17 +258,8 @@
     held_pairs = lax.dynamic_slice_in_dim(order_row, my_index * per_dev, per_dev, 0)
     my_pairs = my_index * per_dev + jnp.arange(per_dev, dtype=jnp.int32)
     seg_pairs = jnp.take(seg_len, my_pairs // HEADS).astype(jnp.int32)
-    row_parts = (
-        lax.all_gather(qkv_weight, "batch", axis=0, tiled=True),
-        lax.all_gather(proj_weight, "batch", axis=0, tiled=True),
-        lax.all_gather(up_weight, "batch", axis=0, tiled=True),
-        lax.all_gather(down_weight, "batch", axis=0, tiled=True),
-    )
-    w_qkv, w_proj, w_up, w_down = (
-        lax.all_gather(row_parts[0], "seq", axis=1, tiled=True),
-        lax.all_gather(row_parts[1], "seq", axis=1, tiled=True),
-        lax.all_gather(row_parts[2], "seq", axis=1, tiled=True),
-        lax.all_gather(row_parts[3], "seq", axis=1, tiled=True),
+    w_qkv = lax.all_gather(
+        lax.all_gather(qkv_weight, "batch", axis=0, tiled=True), "seq", axis=1, tiled=True
     )
     inputs32 = block_input.astype(jnp.float32)
     norm1_out, normed1, inv_std1 = norm_rows(inputs32, norm1_gain, norm1_bias)
@@ -284,6 +275,13 @@
         stacked.reshape(slot_count, piece_len, 3, head_groups, per_dev, HD), (0, 3, 4, 2, 5, 1)
     ).reshape(n_seq, per_dev, 3, HD, piece_len)
     incoming = lax.all_to_all(send, "seq", split_axis=0, concat_axis=0, tiled=True)
+    later_rows = [
+        lax.all_gather(w, "batch", axis=0, tiled=True)
+        for w in (proj_weight, up_weight, down_weight)
+    ]
+    w_proj, w_up, w_down = (
+        lax.all_gather(rows, "seq", axis=1, tiled=True) for rows in later_rows
+    )
     qkv_t = jnp.transpose(incoming, (1, 2, 3, 0, 4)).reshape(per_dev, 3, HD, SLOT)
     attn_t, lse_rows = attn_forward(qkv_t, seg_pairs)
     back = jnp.transpose(attn_t.reshape(per_dev, HD, n_seq, piece_len), (2, 0, 1, 3))
@@ -346,20 +344,29 @@
     dnorm1 = jnp.einsum("nf,df->nd", dqkv_low, w_qkv, preferred_element_type=jnp.float32)
     dinput_norm, gain1_local, bias1_local = norm_back(dnorm1, normed1, inv_std1, norm1_gain)
     input_grad = (dmiddle + dinput_norm).astype(jnp.bfloat16)
-    def scatter_grad(partial):
-        by_rows = lax.psum_scatter(
-            partial.astype(jnp.bfloat16), "batch", scatter_dimension=0, tiled=True
+
+    def by_cols_offloaded(partial):
+        return lax.psum_scatter(
+            partial.astype(jnp.bfloat16), "seq", scatter_dimension=1, tiled=True
         )
-        return lax.psum_scatter(by_rows, "seq", scatter_dimension=1, tiled=True).astype(
+
+    def by_cols_exchanged(partial):
+        rows, cols = partial.shape
+        blocks = jnp.transpose(
+            partial.astype(jnp.bfloat16).reshape(rows, n_seq, cols // n_seq), (1, 0, 2)
+        )
+        got = lax.all_to_all(blocks, "seq", split_axis=0, concat_axis=0, tiled=True)
+        return jnp.sum(got.astype(jnp.float32), axis=0).astype(jnp.bfloat16)
+
+    def by_rows(col_sum):
+        return lax.psum_scatter(col_sum, "batch", scatter_dimension=0, tiled=True).astype(
             jnp.float32
         )
 
-    qkv_grad, proj_grad, up_grad, down_grad = (
-        scatter_grad(qkv_local),
-        scatter_grad(proj_local),
-        scatter_grad(up_local),
-        scatter_grad(down_local),
-    )
+    qkv_grad = by_rows(by_cols_offloaded(qkv_local))
+    proj_grad = by_rows(by_cols_offloaded(proj_local))
+    up_grad = by_rows(by_cols_exchanged(up_local))
+    down_grad = by_rows(by_cols_exchanged(down_local))
     small_sums = lax.psum(
         lax.psum(
             jnp.concatenate([gain1_local, bias1_local, gain2_local, bias2_local, dwa_local]),
@@ -406,6 +413,7 @@
         P("batch", None),
         P("batch", None),
     )
+
     return jax.shard_map(
         local,
         mesh=mesh,

time: 766 us -> 570 us (0.74)
  waiting for transfers between devices: 383 us -> 175 us
  other arithmetic: 26.8 us -> 36.3 us
  starting transfers between devices: 11.9 us -> 21 us
    reduce_scatter x4, waiting for transfers between devices: 224 us -> 45.8 us  [the longest x2 45.8 us: by_cols_offloaded(): lax.psum_scatter(partial.astype(jnp.bfloat16), 'seq', scatter_dimension=1...]
    unnamed x16 -> x12, waiting for transfers between devices: 92.3 us -> 0.17 us
    all_to_all x0 -> x2, waiting for transfers between devices: none -> 88.6 us  [by_cols_exchanged(): got = lax.all_to_all(blocks, 'seq', split_axis=0, concat_axis=0, tiled=True)]
    all_to_all x1, waiting for transfers between devices: 25.8 us -> 0.01 us  [local(): lax.all_to_all(dback, 'seq', split_axis=0, concat_axis=0, tiled=True)]
    all_to_all x0 -> x2, starting transfers between devices: none -> 9.23 us  [by_cols_exchanged(): got = lax.all_to_all(blocks, 'seq', split_axis=0, concat_axis=0, tiled=True)]
    unnamed x71 -> x68, local copies, waits for them, and re-layouts: 22.6 us -> 14.4 us
    reduce_sum x0 -> x2, other arithmetic: none -> 8.16 us  [by_cols_exchanged(): return jnp.sum(got.astype(jnp.float32), axis=0).astype(jnp.bfloat16)]
  transfers between devices with their start and end apart: 15 -> 15, of which waited for: 8 -> 4; matrix products, arithmetic and copies ran while one was open for 15% -> 21% of each run, Pallas kernels for 2% -> 3%
where the time goes in v8:
time: 570 us; the launch traced here: 560 us
  waiting for transfers between devices  175 us (31%)
  blocking collectives  147 us (26%)
  matrix products  69.9 us (12%)
  local copies, waits for them, and re-layouts  56.8 us (10%)
  Pallas kernels  38 us (7%)
  other arithmetic  36.3 us (6%)
  starting transfers between devices  21 us (4%)
  between operations  15.3 us (3%)
    all_to_all x2, waiting for transfers between devices, by_cols_exchanged(): got = lax.all_to_all(blocks, 'seq', split_axis=0, concat_axis=0, tiled=True)  88.6 us
    all_gather x3, blocking collectives, local(): lax.all_gather(w, 'batch', axis=0, tiled=True)  46.9 us
    reduce_scatter x2, waiting for transfers between devices, by_cols_offloaded(): lax.psum_scatter(partial.astype(jnp.bfloat16), 'seq', scatter_dimension=1...  45.8 us
    all_to_all x1, waiting for transfers between devices, local(): lax.all_to_all(send, 'seq', split_axis=0, concat_axis=0, tiled=True)  40.8 us
    all_gather x1, blocking collectives, local(): lax.all_gather(lse_rows.reshape(per_dev, SLOT), 'seq', axis=0, tiled=True)  24.2 us
    psum x1, blocking collectives, local(): lax.psum(jnp.concatenate([gain1_local, bias1_local, gain2_local, bias2_lo...  23.2 us
    pallas_call x1, Pallas kernels, attn_backward(): pl.pallas_call(functools.partial(bwd_kernel, bk=bk, bq=bq, scale=scale),...  20.8 us
    all_gather x1, blocking collectives, local(): lax.all_gather(qkv_weight, 'batch', axis=0, tiled=True)  18.6 us
  transfers between devices with their start and end apart: 15, of which 4 were waited for; matrix products, arithmetic and copies ran while one was open for 21% of the time, Pallas kernels for 3%

profile of v8, /device:TPU:0, one launch (start us, length us, event | category | flops | bytes accessed | tf_op | source)
XLA Modules:
  0.0 559.7 jit_solution(11394062702613777437)
XLA Ops:
  7.2 18.6 %all_gather.27 = bf16[768,288]{1,0:T(8,128)(2,1)S(1)} all-gather(bf16[192,288]{1,0:T(8,128)(2,1)} %param.17), channel_id=1, replica_groups=mesh['batch'=4,'seq'=8] {'batch'}, dimensions={0}, use_global_device_ids=true | all-gather | bytes 552960 | tf_op jit(solution)/shard_map/all_gather | solution.py:262
  26.9 13.6 %all_gather.30 = bf16[768,96]{1,0:T(8,128)(2,1)S(1)} all-gather(bf16[192,96]{1,0:T(8,128)(2,1)S(1)} %copy-done.13), channel_id=1, replica_groups=mesh['batch'=4,'seq'=8] {'batch'}, dimensions={0}, use_global_device_ids=true | all-gather | bytes 184320 | tf_op jit(solution)/shard_map/all_gather | solution.py:279
  41.4 17.5 %all_gather.32 = bf16[768,384]{1,0:T(8,128)(2,1)} all-gather(bf16[192,384]{1,0:T(8,128)(2,1)S(1)} %copy-done.10), channel_id=1, replica_groups=mesh['batch'=4,'seq'=8] {'batch'}, dimensions={0}, use_global_device_ids=true | all-gather | bytes 737280 | tf_op jit(solution)/shard_map/all_gather | solution.py:279
  59.0 15.8 %all_gather.34 = bf16[3072,96]{0,1:T(8,128)(2,1)} all-gather(bf16[768,96]{0,1:T(8,128)(2,1)S(1)} %copy-done.11), channel_id=1, replica_groups=mesh['batch'=4,'seq'=8] {'batch'}, dimensions={0}, use_global_device_ids=true | all-gather | bytes 737280 | tf_op jit(solution)/shard_map/all_gather | solution.py:279
  77.6 4.2 fusion.55
  104.4 4.0 all-to-all-start
  109.6 40.8 %all-to-all-done = bf16[8,3,3,64,256]{4,3,2,1,0:T(8,128)(2,1)S(1)} async-done(((bf16[8,3,3,64,256]{4,3,2,1,0:T(8,128)(2,1)}), bf16[8,3,3,64,256]{4,3,2,1,0:T(8,128)(2,1)S(1)}, u32[]{:S(2)}, u32[]{:S(2)}) %all-to-all-start) | async-done | bytes 2359328 | tf_op jit(solution)/shard_map/all_to_all | solution.py:277
  152.1 17.1 %attn_fwd.1 = (bf16[3,64,2048]{2,1,0:T(8,128)(2,1)}, f32[3,1,2048]{2,1,0:T(1,128)}) custom-call(s32[3]{0:T(128)} %and_select_fusion.2.seg_ref, bf16[3,3,64,2048]{3,2,1,0:T(8,128)(2,1)} %bitcast.197, bf16[3,3,64,2048]{3,2,1,0:T(8,128)(2,1)} %bitcast.198, bf16[3,3,64,2048]{3,2,1,0:T(8,128)(2,1)} %bitcast.199), custom_call_target="tpu_custom_call" | custom-call | flops 2013265920 | bytes 3170304 | tf_op jit(solution)/shard_map/attn_fwd/pallas_call | solution.py:86
  171.4 3.5 all-to-all-start.1
  175.6 24.2 %all-gather = f32[24,1,2048]{2,1,0:T(1,128)S(1)} all-gather(f32[3,1,2048]{2,1,0:T(1,128)S(1)} %copy-done.14), channel_id=2, replica_groups=mesh['batch'=4,'seq'=8] {'seq'}, dimensions={0}, use_global_device_ids=true | all-gather | bytes 221184 | tf_op jit(solution)/shard_map/all_gather | solution.py:289
  205.0 8.4 %fusion.57 = f32[512,3072]{1,0:T(8,128)} fusion(bf16[768,3072]{1,0:T(8,128)(2,1)} %all-gather.10.cloned.1.call-done, f32[512,768]{1,0:T(8,128)} %copy-done.3, f32[768]{0:T(1024)S(1)} %copy-done.20, f32[768]{0:T(1024)S(1)} %copy-done.15, f32[512]{0:T(512)S(1)} %add_rsqrt_fusion, f32[512]{0:T(512)S(1)} %broadcast_multiply_fusion.5), kind=kOutput, calls=%fused_computation.142 | convolution fusion | flops 2417885184 | bytes 12593152 | tf_op jit(solution)/shard_map/dot_general | solution.py:297
  213.3 10.3 %fusion.6 = bf16[512,3072]{1,0:T(8,128)(2,1)S(1)} fusion(f32[512,3072]{1,0:T(8,128)} %fusion.57, bf16[3072,768]{0,1:T(8,128)(2,1)} %all-gather.12.cloned.1.call-done, bf16[512,768]{1,0:T(8,128)(2,1)} %param.16, f32[]{:T(128)} %bitcast), kind=kOutput, calls=%fused_computation.11 | convolution fusion | flops 2448556032 | bytes 14942212 | tf_op jit(solution)/shard_map/nd,fd->nf/dot_general | solution.py:315
  227.2 13.7 %fusion.32 = (bf16[512,768]{1,0:T(8,128)(2,1)}, f32[512,768]{1,0:T(8,128)S(1)}) fusion(f32[]{:T(128)} %bitcast.26, f32[]{:T(128)} %bitcast.24, f32[]{:T(128)} %bitcast.22, f32[]{:T(128)} %bitcast.20, f32[]{:T(128)} %bitcast.18, f32[]{:T(128)} %bitcast.16, f32[]{:T(128)} %bitcast.14, f32[]{:T(128)} %bitcast.12, f32[]{:T(128)} %bitcast, ...), kind=kOutput, calls=%fused_computation.65 | convolution fusion | flops 2440691712 | bytes 21233700 | tf_op jit(solution)/shard_map/dot_general | solution.py:300
  240.9 3.6 fusion.40
  247.1 15.2 %all_to_all.30 = bf16[8,3,64,256]{3,2,1,0:T(8,128)(2,1)S(1)} all-to-all(bf16[8,3,64,256]{3,2,1,0:T(8,128)(2,1)S(1)} %bitcast.194), channel_id=1, replica_groups=mesh['batch'=4,'seq'=8] {'seq'}, dimensions={0} | all-to-all | bytes 1572864 | tf_op jit(solution)/shard_map/all_to_all | solution.py:329
  263.3 20.8 %attn_bwd.1 = bf16[3,3,64,2048]{3,2,1,0:T(8,128)(2,1)} custom-call(s32[3]{0:T(128)} %and_select_fusion.2.seg_ref, bf16[3,3,64,2048]{3,2,1,0:T(8,128)(2,1)} %bitcast.200, bf16[3,3,64,2048]{3,2,1,0:T(8,128)(2,1)} %bitcast.201, bf16[3,3,64,2048]{3,2,1,0:T(8,128)(2,1)} %bitcast.202, bf16[3,64,2048]{2,1,0:T(8,128)(2,1)} %bitcast.206, ...), custom_call_target="tpu_custom_call" | custom-call | flops 5033164800 | bytes 6316032 | tf_op jit(solution)/shard_map/attn_bwd/pallas_call | solution.py:174
  287.6 3.6 all-to-all-start.3
  294.8 5.2 convolution_convert_fusion.2
  302.7 45.8 %reduce-scatter.13.cloned.1.call-done = bf16[768,96]{0,1:T(8,128)(2,1)} async-done(((bf16[768,768]{0,1:T(8,128)(2,1)}), bf16[768,96]{0,1:T(8,128)(2,1)}) %reduce-scatter.13.cloned.1.call-update) | async-done | bytes 147472 | tf_op jit(solution)/shard_map/reduce_scatter | solution.py:349
  350.3 4.6 all-to-all-start.4
  364.1 4.0 convolution_convert_fusion
  369.2 8.7 %convolution_convert_fusion.1 = bf16[3072,768]{0,1:T(8,128)(2,1)} fusion(bf16[512,768]{1,0:T(8,128)(2,1)S(1)} %copy-done.7, f32[]{:T(128)} %bitcast, f32[512,3072]{1,0:T(8,128)} %fusion.57), kind=kOutput, calls=%fused_computation.14 | convolution fusion | flops 2433613824 | bytes 11796484 | tf_op jit(solution)/shard_map/nf,nd->fd/dot_general | solution.py:314
  377.9 41.2 %all-to-all-done.4 = bf16[8,768,384]{2,1,0:T(8,128)(2,1)} async-done(((bf16[8,768,384]{2,1,0:T(8,128)(2,1)}), bf16[8,768,384]{2,1,0:T(8,128)(2,1)}, u32[]{:S(2)}, u32[]{:S(2)}) %all-to-all-start.4) | async-done | bytes 4718624 | tf_op jit(solution)/shard_map/all_to_all | solution.py:358
  419.1 4.6 all-to-all-start.5
  423.8 4.0 reduce_sum.221
  428.5 4.5 multiply_convert_fusion
  433.1 47.5 %all-to-all-done.5 = bf16[8,3072,96]{1,2,0:T(8,128)(2,1)} async-done(((bf16[8,3072,96]{1,2,0:T(8,128)(2,1)}), bf16[8,3072,96]{1,2,0:T(8,128)(2,1)}, u32[]{:S(2)}, u32[]{:S(2)}) %all-to-all-start.5) | async-done | bytes 4718624 | tf_op jit(solution)/shard_map/all_to_all | solution.py:358
  480.6 4.1 reduce_sum.222
  487.8 5.6 fusion.22
  495.6 5.9 %concatenate.30 = f32[3081]{0:T(1024)S(1)} concatenate(f32[768]{0:T(1024)S(1)} %get-tuple-element.96, f32[768]{0:T(1024)S(1)} %get-tuple-element.101, f32[768]{0:T(1024)S(1)} %get-tuple-element.94, f32[768]{0:T(1024)S(1)} %get-tuple-element.100, f32[1]{0:T(128)} %bitcast.49, f32[1]{0:T(128)} %bitcast.51, f32[1]{0:T(128)} %bitcast.53, f32[1]{0:T(128)} %bitcast.55, f32[1]{0:T(128)} %bitcast.57, ...), dimensions={0} | concatenate | bytes 24648 | tf_op jit(solution)/shard_map/concatenate | solution.py:372
  501.5 23.2 %psum.14 = f32[3081]{0:T(1024)S(1)} all-reduce(f32[3081]{0:T(1024)S(1)} %concatenate.30), channel_id=1, replica_groups=mesh['batch'=4,'seq'=8] {'seq'}, use_global_device_ids=true, to_apply=%region_29.30 | all-reduce | flops 3081 | bytes 24648 | tf_op jit(solution)/shard_map/psum | solution.py:371
  524.7 18.6 %psum.15 = f32[3081]{0:T(1024)S(1)} all-reduce(f32[3081]{0:T(1024)S(1)} %psum.14), channel_id=1, replica_groups=mesh['batch'=4,'seq'=8] {'batch'}, use_global_device_ids=true, to_apply=%region_30.31 | all-reduce | flops 3081 | bytes 24648 | tf_op jit(solution)/shard_map/psum | solution.py:370
  (173 shorter events, 81.6 us)
Async XLA Ops:
  7.2 19.7 %copy-start.13 = (bf16[192,96]{1,0:T(8,128)(2,1)S(1)}, bf16[192,96]{1,0:T(8,128)(2,1)}, u32[]{:S(2)}) copy-start(bf16[192,96]{1,0:T(8,128)(2,1)} %param.18) | copy-start | bytes 110596
  7.2 34.2 %copy-start.10 = (bf16[192,384]{1,0:T(8,128)(2,1)S(1)}, bf16[192,384]{1,0:T(8,128)(2,1)}, u32[]{:S(2)}) copy-start(bf16[192,384]{1,0:T(8,128)(2,1)} %param.19) | copy-start | bytes 442372
  7.2 70.4 %all-gather.6.cloned.1.call-start = ((), (), s32[]{:S(2)}) async-start(), calls=%async_computation.12 | async-start | bytes 3981312 | tf_op jit(solution)/shard_map/all_gather | solution.py:261
  25.8 33.2 %copy-start.11 = (bf16[768,96]{0,1:T(8,128)(2,1)S(1)}, bf16[768,96]{0,1:T(8,128)(2,1)}, u32[]{:S(2)}) copy-start(bf16[768,96]{0,1:T(8,128)(2,1)} %param.20) | copy-start | bytes 442372
  26.9 174.0 %all-gather.8.cloned.1.call-start = ((), (), s32[]{:S(2)}) async-start(), calls=%async_computation.13 | async-start | bytes 1327104 | tf_op jit(solution)/shard_map/all_gather | solution.py:283
  40.5 34.4 %copy-start.22 = (s32[1,2]{1,0:T(1,128)S(1)}, s32[1,2]{1,0:T(1,128)}, u32[]{:S(2)}) copy-start(s32[1,2]{1,0:T(1,128)} %param.27) | copy-start | bytes 28
  41.4 35.6 %copy-start.2 = (bf16[512,768]{1,0:T(8,128)(2,1)S(1)}, bf16[512,768]{1,0:T(8,128)(2,1)}, u32[]{:S(2)}) copy-start(bf16[512,768]{1,0:T(8,128)(2,1)} %param.14) | copy-start | bytes 2359300
  41.4 163.6 %all-gather.10.cloned.1.call-start = ((), (), s32[]{:S(2)}) async-start(), calls=%async_computation.14 | async-start | bytes 5308416 | tf_op jit(solution)/shard_map/all_gather | solution.py:283
  59.0 154.4 %all-gather.12.cloned.1.call-start = ((), (), s32[]{:S(2)}) async-start(), calls=%async_computation.15 | async-start | bytes 5308416 | tf_op jit(solution)/shard_map/all_gather | solution.py:283
  104.4 45.9 %all-to-all-start = ((bf16[8,3,3,64,256]{4,3,2,1,0:T(8,128)(2,1)}), bf16[8,3,3,64,256]{4,3,2,1,0:T(8,128)(2,1)S(1)}, u32[]{:S(2)}, u32[]{:S(2)}) async-start(bf16[8,3,3,64,256]{4,3,2,1,0:T(8,128)(2,1)} %copy.98), calls=%async_computation | async-start | bytes 4718592 | tf_op jit(solution)/shard_map/all_to_all | solution.py:277
  169.2 5.7 %copy-start.12 = (f32[9]{0:T(128)S(1)}, f32[9]{0:T(128)}, u32[]{:S(2)}) copy-start(f32[9]{0:T(128)} %param.25) | copy-start | bytes 112
  169.2 6.3 %copy-start.14 = (f32[3,1,2048]{2,1,0:T(1,128)S(1)}, f32[3,1,2048]{2,1,0:T(1,128)}, u32[]{:S(2)}) copy-start(f32[3,1,2048]{2,1,0:T(1,128)} %get-tuple-element.17.lse_ref) | copy-start | bytes 73732
  171.4 28.5 %all-to-all-start.1 = ((bf16[8,3,64,256]{3,2,1,0:T(8,128)(2,1)}), bf16[8,3,64,256]{3,2,1,0:T(8,128)(2,1)S(1)}, u32[]{:S(2)}, u32[]{:S(2)}) async-start(bf16[8,3,64,256]{3,2,1,0:T(8,128)(2,1)} %bitcast.168), calls=%async_computation.1 | async-start | bytes 1572864 | tf_op jit(solution)/shard_map/all_to_all | solution.py:288
  205.0 21.8 %slice-start = ((s8[6291456]{0:T(1024)(128)(4,1)}), s8[2097152]{0:T(1024)(128)(4,1)S(1)}, s32[]{:S(2)}) async-start(s8[6291456]{0:T(1024)(128)(4,1)} %bitcast.177), calls=%async_computation.22 | async-start | bytes 4194304
  213.3 10.3 %copy-start.4 = (f32[512,768]{1,0:T(8,128)S(1)}, f32[512,768]{1,0:T(8,128)}, u32[]{:S(2)}) copy-start(f32[512,768]{1,0:T(8,128)} %copy-done.3) | copy-start | bytes 4718596
  213.3 10.3 %copy-start.17 = (bf16[768,3072]{1,0:T(8,128)(2,1)S(1)}, bf16[768,3072]{1,0:T(8,128)(2,1)}, u32[]{:S(2)}) copy-start(bf16[768,3072]{1,0:T(8,128)(2,1)} %all-gather.10.cloned.1.call-done) | copy-start | bytes 14155780
  213.3 13.5 %slice-start.1 = ((s8[6291456]{0:T(1024)(128)(4,1)}), s8[4194304]{0:T(1024)(128)(4,1)S(1)}, s32[]{:S(2)}) async-start(s8[6291456]{0:T(1024)(128)(4,1)} %bitcast.177), calls=%async_computation.23 | async-start | bytes 8388608
  223.7 3.1 copy-start.24
  223.7 3.5 copy-start.18
  227.2 13.7 %copy-start.6 = (bf16[512,768]{1,0:T(8,128)(2,1)S(1)}, bf16[512,768]{1,0:T(8,128)(2,1)}, u32[]{:S(2)}) copy-start(bf16[512,768]{1,0:T(8,128)(2,1)} %param.16) | copy-start | bytes 2359300
  240.9 4.8 copy-start.19
  287.6 62.7 %all-to-all-start.3 = ((bf16[8,3,3,64,256]{4,3,2,1,0:T(8,128)(2,1)}), bf16[8,3,3,64,256]{4,3,2,1,0:T(8,128)(2,1)S(1)}, u32[]{:S(2)}, u32[]{:S(2)}) async-start(bf16[8,3,3,64,256]{4,3,2,1,0:T(8,128)(2,1)} %bitcast.174), calls=%async_computation.3 | async-start | bytes 4718592 | tf_op jit(solution)/shard_map/all_to_all | solution.py:335
  291.2 57.3 %reduce-scatter.13.cloned.1.call-start = ((), (), s32[]{:S(2)}) async-start(), calls=%async_computation.17 | async-start | bytes 1327104 | tf_op jit(solution)/shard_map/reduce_scatter | solution.py:349
  294.8 191.4 %reduce-scatter.21.cloned.1.call-start = ((), (), s32[]{:S(2)}) async-start(), calls=%async_computation.21 | async-start | bytes 245760
  350.3 68.8 %all-to-all-start.4 = ((bf16[8,768,384]{2,1,0:T(8,128)(2,1)}), bf16[8,768,384]{2,1,0:T(8,128)(2,1)}, u32[]{:S(2)}, u32[]{:S(2)}) async-start(bf16[8,768,384]{2,1,0:T(8,128)(2,1)} %bitcast.171), calls=%async_computation.6 | async-start | bytes 9437184 | tf_op jit(solution)/shard_map/all_to_all | solution.py:358
  354.9 138.4 %reduce-scatter.11.cloned.1.call-start = ((), (), s32[]{:S(2)}) async-start(), calls=%async_computation.16 | async-start | bytes 3981312 | tf_op jit(solution)/shard_map/reduce_scatter | solution.py:349
  419.1 61.4 %all-to-all-start.5 = ((bf16[8,3072,96]{1,2,0:T(8,128)(2,1)}), bf16[8,3072,96]{1,2,0:T(8,128)(2,1)}, u32[]{:S(2)}, u32[]{:S(2)}) async-start(bf16[8,3072,96]{1,2,0:T(8,128)(2,1)} %bitcast.179), calls=%async_computation.8 | async-start | bytes 9437184 | tf_op jit(solution)/shard_map/all_to_all | solution.py:358
  423.7 123.5 %reduce-scatter.15.cloned.1.call-start = ((), (), s32[]{:S(2)}) async-start(), calls=%async_computation.18 | async-start | bytes 737280 | tf_op jit(solution)/shard_map/reduce_scatter | solution.py:362
  427.8 121.1 %reduce-scatter.17.cloned.1.call-start = ((), (), s32[]{:S(2)}) async-start(), calls=%async_computation.19 | async-start | bytes 737280 | tf_op jit(solution)/shard_map/reduce_scatter | solution.py:362
  433.1 54.7 %copy-start.9 = (bf16[512,2304]{0,1:T(8,128)(2,1)S(1)}, bf16[512,2304]{0,1:T(8,128)(2,1)}, u32[]{:S(2)}) copy-start(bf16[512,2304]{0,1:T(8,128)(2,1)} %copy-done.8) | copy-start | bytes 7077892
  484.7 65.8 %reduce-scatter.19.cloned.1.call-start = ((), (), s32[]{:S(2)}) async-start(), calls=%async_computation.20 | async-start | bytes 737280
  493.3 51.0 %copy-start.1 = (f32[512,768]{1,0:T(8,128)S(1)}, f32[512,768]{1,0:T(8,128)}, u32[]{:S(2)}) copy-start(f32[512,768]{1,0:T(8,128)} %copy-done) | copy-start | bytes 4718596
  (10 other events, 16.7 us)
Sparse Core Ops, SparseCore 0:
  27.0 35.0 all-gather.5
  64.5 23.9 all-gather.7
  90.4 55.4 all-gather.9
  147.6 54.0 all-gather.11
  294.9 53.5 reduce-scatter.12
  351.2 19.6 reduce-scatter.20
  374.4 57.8 reduce-scatter.10
  434.6 34.8 reduce-scatter.14
  484.8 21.2 reduce-scatter.16
  508.3 20.4 reduce-scatter.18

commit v9 on v8

--- a/solution.py
+++ b/solution.py
@@ -366,14 +366,15 @@
     qkv_grad = by_rows(by_cols_offloaded(qkv_local))
     proj_grad = by_rows(by_cols_offloaded(proj_local))
     up_grad = by_rows(by_cols_exchanged(up_local))
-    down_grad = by_rows(by_cols_exchanged(down_local))
-    small_sums = lax.psum(
-        lax.psum(
-            jnp.concatenate([gain1_local, bias1_local, gain2_local, bias2_local, dwa_local]),
-            "seq",
-        ),
-        "batch",
-    )
+    down_grad = by_rows(by_cols_offloaded(down_local))
+    small_sums = jnp.concatenate([gain1_local, bias1_local, gain2_local, bias2_local, dwa_local])
+    for axis in ("seq", "batch"):
+        size = lax.axis_size(axis)
+        hop = 1
+        while hop < size:
+            partner = [(i, i ^ hop) for i in range(size)]
+            small_sums = small_sums + lax.ppermute(small_sums, axis, partner)
+            hop *= 2
     gain1_grad, bias1_grad, gain2_grad, bias2_grad = (
         small_sums[k * D : (k + 1) * D] for k in range(4)
     )

time: 570 us -> 544 us (0.954)
  waiting for transfers between devices: 175 us -> 131 us
  blocking collectives: 147 us -> 164 us
  starting transfers between devices: 21 us -> 32.4 us
    all_to_all x2 -> x0, waiting for transfers between devices: 88.6 us -> none  [by_cols_exchanged(): got = lax.all_to_all(blocks, 'seq', split_axis=0, concat_axis=0, tiled=True)]
    all_to_all x0 -> x1, blocking collectives: none -> 59.3 us  [by_cols_exchanged(): got = lax.all_to_all(blocks, 'seq', split_axis=0, concat_axis=0, tiled=True)]
    psum x2 -> x0, blocking collectives: 41.8 us -> none  [the longest x1 23.2 us: local(): lax.psum(jnp.concatenate([gain1_local, bias1_local, gain2_local, bias2_lo...]
    all_to_all x1, waiting for transfers between devices: 0.01 us -> 39.6 us  [local(): lax.all_to_all(dback, 'seq', split_axis=0, concat_axis=0, tiled=True)]
    reduce_scatter x2 -> x3, waiting for transfers between devices: 45.8 us -> 7.27 us  [by_cols_offloaded(): lax.psum_scatter(partial.astype(jnp.bfloat16), 'seq', scatter_dimension=1...]
    unnamed x12 -> x13, waiting for transfers between devices: 0.17 us -> 21.3 us
    ppermute x0 -> x5, starting transfers between devices: none -> 20.1 us  [local(): small_sums = small_sums + lax.ppermute(small_sums, axis, partner)]
    reduce_scatter x2, waiting for transfers between devices: 0.01 us -> 17.9 us  [by_rows(): lax.psum_scatter(col_sum, 'batch', scatter_dimension=0, tiled=True)]
  transfers between devices with their start and end apart: 15 -> 19, of which waited for: 4 -> 8; matrix products, arithmetic and copies ran while one was open for 21% -> 21% of each run, Pallas kernels for 3% -> 7%
where the time goes in v9:
time: 544 us; the launch traced here: 534 us
  blocking collectives  164 us (30%)
  waiting for transfers between devices  131 us (24%)
  matrix products  68.9 us (13%)
  local copies, waits for them, and re-layouts  51.4 us (9%)
  Pallas kernels  38 us (7%)
  other arithmetic  33.4 us (6%)
  starting transfers between devices  32.4 us (6%)
  between operations  14.8 us (3%)
    all_to_all x1, blocking collectives, by_cols_exchanged(): got = lax.all_to_all(blocks, 'seq', split_axis=0, concat_axis=0, tiled=True)  59.3 us
    all_gather x3, blocking collectives, local(): lax.all_gather(w, 'batch', axis=0, tiled=True)  46.9 us
    all_to_all x1, waiting for transfers between devices, local(): lax.all_to_all(send, 'seq', split_axis=0, concat_axis=0, tiled=True)  40.8 us
    all_to_all x1, waiting for transfers between devices, local(): lax.all_to_all(dback, 'seq', split_axis=0, concat_axis=0, tiled=True)  39.6 us
    all_gather x1, blocking collectives, local(): lax.all_gather(lse_rows.reshape(per_dev, SLOT), 'seq', axis=0, tiled=True)  24.2 us
    unnamed x13, waiting for transfers between devices  21.3 us
    pallas_call x1, Pallas kernels, attn_backward(): pl.pallas_call(functools.partial(bwd_kernel, bk=bk, bq=bq, scale=scale),...  20.8 us
    ppermute x5, starting transfers between devices, local(): small_sums = small_sums + lax.ppermute(small_sums, axis, partner)  20.1 us
  transfers between devices with their start and end apart: 19, of which 8 were waited for; matrix products, arithmetic and copies ran while one was open for 21% of the time, Pallas kernels for 7%

profile of v9, /device:TPU:0, one launch (start us, length us, event | category | flops | bytes accessed | tf_op | source)
XLA Modules:
  0.0 533.7 jit_solution(12258635453033446115)
XLA Ops:
  7.2 18.6 %all_gather.27 = bf16[768,288]{1,0:T(8,128)(2,1)S(1)} all-gather(bf16[192,288]{1,0:T(8,128)(2,1)} %param.17), channel_id=1, replica_groups=mesh['batch'=4,'seq'=8] {'batch'}, dimensions={0}, use_global_device_ids=true | all-gather | bytes 552960 | tf_op jit(solution)/shard_map/all_gather | solution.py:262
  26.9 13.6 %all_gather.30 = bf16[768,96]{1,0:T(8,128)(2,1)S(1)} all-gather(bf16[192,96]{1,0:T(8,128)(2,1)S(1)} %copy-done.11), channel_id=1, replica_groups=mesh['batch'=4,'seq'=8] {'batch'}, dimensions={0}, use_global_device_ids=true | all-gather | bytes 184320 | tf_op jit(solution)/shard_map/all_gather | solution.py:279
  41.4 17.5 %all_gather.32 = bf16[768,384]{1,0:T(8,128)(2,1)} all-gather(bf16[192,384]{1,0:T(8,128)(2,1)S(1)} %copy-done.8), channel_id=1, replica_groups=mesh['batch'=4,'seq'=8] {'batch'}, dimensions={0}, use_global_device_ids=true | all-gather | bytes 737280 | tf_op jit(solution)/shard_map/all_gather | solution.py:279
  59.0 15.8 %all_gather.34 = bf16[3072,96]{0,1:T(8,128)(2,1)} all-gather(bf16[768,96]{0,1:T(8,128)(2,1)S(1)} %copy-done.9), channel_id=1, replica_groups=mesh['batch'=4,'seq'=8] {'batch'}, dimensions={0}, use_global_device_ids=true | all-gather | bytes 737280 | tf_op jit(solution)/shard_map/all_gather | solution.py:279
  77.6 4.2 fusion.55
  91.8 3.1 subtract_convert_fusion.3
  102.6 3.9 all-to-all-start
  107.7 40.8 %all-to-all-done = bf16[8,3,3,64,256]{4,3,2,1,0:T(8,128)(2,1)S(1)} async-done(((bf16[8,3,3,64,256]{4,3,2,1,0:T(8,128)(2,1)}), bf16[8,3,3,64,256]{4,3,2,1,0:T(8,128)(2,1)S(1)}, u32[]{:S(2)}, u32[]{:S(2)}) %all-to-all-start) | async-done | bytes 2359328 | tf_op jit(solution)/shard_map/all_to_all | solution.py:277
  150.2 17.1 %attn_fwd.1 = (bf16[3,64,2048]{2,1,0:T(8,128)(2,1)}, f32[3,1,2048]{2,1,0:T(1,128)}) custom-call(s32[3]{0:T(128)} %and_select_fusion.2.seg_ref, bf16[3,3,64,2048]{3,2,1,0:T(8,128)(2,1)} %bitcast.193, bf16[3,3,64,2048]{3,2,1,0:T(8,128)(2,1)} %bitcast.194, bf16[3,3,64,2048]{3,2,1,0:T(8,128)(2,1)} %bitcast.195), custom_call_target="tpu_custom_call" | custom-call | flops 2013265920 | bytes 3170304 | tf_op jit(solution)/shard_map/attn_fwd/pallas_call | solution.py:86
  169.5 3.5 all-to-all-start.1
  173.7 24.2 %all-gather = f32[24,1,2048]{2,1,0:T(1,128)S(1)} all-gather(f32[3,1,2048]{2,1,0:T(1,128)S(1)} %copy-done.12), channel_id=2, replica_groups=mesh['batch'=4,'seq'=8] {'seq'}, dimensions={0}, use_global_device_ids=true | all-gather | bytes 221184 | tf_op jit(solution)/shard_map/all_gather | solution.py:289
  202.0 7.0 %fusion.57 = f32[512,3072]{1,0:T(8,128)} fusion(bf16[768,3072]{1,0:T(8,128)(2,1)} %all-gather.10.cloned.1.call-done, f32[512,768]{1,0:T(8,128)S(1)} %get-tuple-element.138, f32[768]{0:T(1024)S(1)} %copy-done.18, f32[768]{0:T(1024)S(1)} %copy-done.13, f32[512]{0:T(512)S(1)} %add_rsqrt_fusion, f32[512]{0:T(512)S(1)} %broadcast_multiply_fusion.5), kind=kOutput, calls=%fused_computation.142 | convolution fusion | flops 2417885184 | bytes 12593152 | tf_op jit(solution)/shard_map/dot_general | solution.py:297
  209.0 9.5 %fusion.6 = bf16[512,3072]{1,0:T(8,128)(2,1)S(1)} fusion(f32[512,3072]{1,0:T(8,128)} %fusion.57, bf16[3072,768]{0,1:T(8,128)(2,1)} %all-gather.12.cloned.1.call-done, bf16[512,768]{1,0:T(8,128)(2,1)} %param.16, f32[]{:T(128)} %bitcast), kind=kOutput, calls=%fused_computation.11 | convolution fusion | flops 2448556032 | bytes 14942212 | tf_op jit(solution)/shard_map/nd,fd->nf/dot_general | solution.py:315
  222.0 15.1 %fusion.32 = (bf16[512,768]{1,0:T(8,128)(2,1)}, f32[512,768]{1,0:T(8,128)S(1)}) fusion(f32[]{:T(128)} %bitcast.26, f32[]{:T(128)} %bitcast.24, f32[]{:T(128)} %bitcast.22, f32[]{:T(128)} %bitcast.20, f32[]{:T(128)} %bitcast.18, f32[]{:T(128)} %bitcast.16, f32[]{:T(128)} %bitcast.14, f32[]{:T(128)} %bitcast.12, f32[]{:T(128)} %bitcast, ...), kind=kOutput, calls=%fused_computation.65 | convolution fusion | flops 2440691712 | bytes 21233700 | tf_op jit(solution)/shard_map/dot_general | solution.py:300
  237.1 5.0 fusion.40
  244.3 8.8 %convolution_convert_fusion.1 = bf16[3072,768]{0,1:T(8,128)(2,1)} fusion(bf16[512,768]{1,0:T(8,128)(2,1)} %param.16, f32[]{:T(128)} %bitcast, f32[512,3072]{1,0:T(8,128)} %fusion.57), kind=kOutput, calls=%fused_computation.14 | convolution fusion | flops 2433613824 | bytes 11796484 | tf_op jit(solution)/shard_map/nf,nd->fd/dot_general | solution.py:314
  255.7 15.2 %all_to_all.25 = bf16[8,3,64,256]{3,2,1,0:T(8,128)(2,1)S(1)} all-to-all(bf16[8,3,64,256]{3,2,1,0:T(8,128)(2,1)S(1)} %bitcast.189), channel_id=1, replica_groups=mesh['batch'=4,'seq'=8] {'seq'}, dimensions={0} | all-to-all | bytes 1572864 | tf_op jit(solution)/shard_map/all_to_all | solution.py:329
  271.9 20.8 %attn_bwd.1 = bf16[3,3,64,2048]{3,2,1,0:T(8,128)(2,1)} custom-call(s32[3]{0:T(128)} %and_select_fusion.2.seg_ref, bf16[3,3,64,2048]{3,2,1,0:T(8,128)(2,1)} %bitcast.196, bf16[3,3,64,2048]{3,2,1,0:T(8,128)(2,1)} %bitcast.197, bf16[3,3,64,2048]{3,2,1,0:T(8,128)(2,1)} %bitcast.198, bf16[3,64,2048]{2,1,0:T(8,128)(2,1)} %bitcast.202, ...), custom_call_target="tpu_custom_call" | custom-call | flops 5033164800 | bytes 6316032 | tf_op jit(solution)/shard_map/attn_bwd/pallas_call | solution.py:174
  292.7 3.4 copy.144
  296.1 3.6 all-to-all-start.3
  302.1 39.6 %all-to-all-done.3 = bf16[8,3,3,64,256]{4,3,2,1,0:T(8,128)(2,1)S(1)} async-done(((bf16[8,3,3,64,256]{4,3,2,1,0:T(8,128)(2,1)}), bf16[8,3,3,64,256]{4,3,2,1,0:T(8,128)(2,1)S(1)}, u32[]{:S(2)}, u32[]{:S(2)}) %all-to-all-start.3) | async-done | bytes 2359328 | tf_op jit(solution)/shard_map/all_to_all | solution.py:335
  350.6 4.0 convolution_convert_fusion
  356.1 5.0 convolution_convert_fusion.2
  361.6 59.3 %all_to_all.26 = bf16[8,768,384]{2,1,0:T(8,128)(2,1)} all-to-all(bf16[8,768,384]{2,1,0:T(8,128)(2,1)S(1)} %bitcast.168), channel_id=1, replica_groups=mesh['batch'=4,'seq'=8] {'seq'}, dimensions={0} | all-to-all | bytes 9437184 | tf_op jit(solution)/shard_map/all_to_all | solution.py:358
  420.9 4.1 reduce_sum.209
  425.7 4.5 multiply_convert_fusion
  430.3 6.2 %fusion.22 = (f32[768]{0:T(1024)S(1)}, f32[512]{0:T(512)S(1)}, f32[512]{0:T(512)S(1)}, f32[768]{0:T(1024)S(1)}, f32[512,768]{1,0:T(8,128)}) fusion(bf16[512,768]{1,0:T(8,128)(2,1)S(1)} %copy-done.2, f32[512]{0:T(512)S(1)} %add_rsqrt_fusion.1, f32[512]{0:T(512)S(1)} %broadcast_multiply_fusion.6, f32[768]{0:T(1024)S(1)} %copy-done.14, ...), kind=kOutput, calls=%fused_computation.55 | convolution fusion | flops 1815868928 | bytes 8274944 | tf_op jit(solution)/shard_map/nf,df->nd/dot_general | solution.py:344
  436.6 6.0 %concatenate.30 = f32[3081]{0:T(1024)S(1)} concatenate(f32[768]{0:T(1024)S(1)} %get-tuple-element.96, f32[768]{0:T(1024)S(1)} %get-tuple-element.101, f32[768]{0:T(1024)S(1)} %get-tuple-element.94, f32[768]{0:T(1024)S(1)} %get-tuple-element.100, f32[1]{0:T(128)} %bitcast.47, f32[1]{0:T(128)} %bitcast.49, f32[1]{0:T(128)} %bitcast.51, f32[1]{0:T(128)} %bitcast.53, f32[1]{0:T(128)} %bitcast.55, ...), dimensions={0} | concatenate | bytes 24648 | tf_op jit(solution)/shard_map/concatenate | solution.py:370
  448.0 7.2 %reduce-scatter.12.cloned.1.call-done = bf16[768,288]{0,1:T(8,128)(2,1)} async-done(((bf16[768,2304]{0,1:T(8,128)(2,1)}), bf16[768,288]{0,1:T(8,128)(2,1)}) %reduce-scatter.12.cloned.1.call-update) | async-done | bytes 442384 | tf_op jit(solution)/shard_map/reduce_scatter | solution.py:349
  457.4 16.6 %collective-permute-start.3 = (f32[3081]{0:T(1024)S(1)}, f32[3081]{0:T(1024)S(1)}, u32[]{:S(2)}, u32[]{:S(2)}) collective-permute-start(f32[3081]{0:T(1024)S(1)} %add.241), channel_id=1, source_target_pairs={{0,8},{8,0},{16,24},{24,16},{1,9},{9,1},{17,25},{25,17},{2,10},{10... | collective-permute-start | bytes 36980 | tf_op jit(solution)/shard_map/ppermute | solution.py:376
  484.4 17.9 %reduce-scatter.20.cloned.1.call-done = bf16[768,96]{0,1:T(8,128)(2,1)} async-done(((bf16[3072,96]{0,1:T(8,128)(2,1)}), bf16[768,96]{0,1:T(8,128)(2,1)}) %reduce-scatter.20.cloned.1.call-update) | async-done | bytes 147472 | tf_op jit(solution)/shard_map/reduce_scatter | solution.py:362
  503.9 21.1 %reduce-scatter.22.cloned.1.call-done = bf16[192,288]{1,0:T(8,128)(2,1)} async-done(((bf16[768,288]{1,0:T(8,128)(2,1)}), bf16[192,288]{1,0:T(8,128)(2,1)}) %reduce-scatter.22.cloned.1.call-update) | async-done | bytes 110608
  (179 shorter events, 76.3 us)
Async XLA Ops:
  7.2 19.7 %copy-start.11 = (bf16[192,96]{1,0:T(8,128)(2,1)S(1)}, bf16[192,96]{1,0:T(8,128)(2,1)}, u32[]{:S(2)}) copy-start(bf16[192,96]{1,0:T(8,128)(2,1)} %param.18) | copy-start | bytes 110596
  7.2 34.2 %copy-start.8 = (bf16[192,384]{1,0:T(8,128)(2,1)S(1)}, bf16[192,384]{1,0:T(8,128)(2,1)}, u32[]{:S(2)}) copy-start(bf16[192,384]{1,0:T(8,128)(2,1)} %param.19) | copy-start | bytes 442372
  7.2 70.4 %all-gather.6.cloned.1.call-start = ((), (), s32[]{:S(2)}) async-start(), calls=%async_computation.12 | async-start | bytes 3981312 | tf_op jit(solution)/shard_map/all_gather | solution.py:261
  25.8 33.2 %copy-start.9 = (bf16[768,96]{0,1:T(8,128)(2,1)S(1)}, bf16[768,96]{0,1:T(8,128)(2,1)}, u32[]{:S(2)}) copy-start(bf16[768,96]{0,1:T(8,128)(2,1)} %param.20) | copy-start | bytes 442372
  26.9 172.1 %all-gather.8.cloned.1.call-start = ((), (), s32[]{:S(2)}) async-start(), calls=%async_computation.13 | async-start | bytes 1327104 | tf_op jit(solution)/shard_map/all_gather | solution.py:283
  40.5 34.4 %copy-start.19 = (s32[1,2]{1,0:T(1,128)S(1)}, s32[1,2]{1,0:T(1,128)}, u32[]{:S(2)}) copy-start(s32[1,2]{1,0:T(1,128)} %param.27) | copy-start | bytes 28
  41.3 35.6 %copy-start.2 = (bf16[512,768]{1,0:T(8,128)(2,1)S(1)}, bf16[512,768]{1,0:T(8,128)(2,1)}, u32[]{:S(2)}) copy-start(bf16[512,768]{1,0:T(8,128)(2,1)} %param.14) | copy-start | bytes 2359300
  41.4 160.2 %all-gather.10.cloned.1.call-start = ((), (), s32[]{:S(2)}) async-start(), calls=%async_computation.14 | async-start | bytes 5308416 | tf_op jit(solution)/shard_map/all_gather | solution.py:283
  59.0 150.0 %all-gather.12.cloned.1.call-start = ((), (), s32[]{:S(2)}) async-start(), calls=%async_computation.15 | async-start | bytes 5308416 | tf_op jit(solution)/shard_map/all_gather | solution.py:283
  102.6 45.9 %all-to-all-start = ((bf16[8,3,3,64,256]{4,3,2,1,0:T(8,128)(2,1)}), bf16[8,3,3,64,256]{4,3,2,1,0:T(8,128)(2,1)S(1)}, u32[]{:S(2)}, u32[]{:S(2)}) async-start(bf16[8,3,3,64,256]{4,3,2,1,0:T(8,128)(2,1)} %copy.98), calls=%async_computation | async-start | bytes 4718592 | tf_op jit(solution)/shard_map/all_to_all | solution.py:277
  167.4 6.4 %copy-start.12 = (f32[3,1,2048]{2,1,0:T(1,128)S(1)}, f32[3,1,2048]{2,1,0:T(1,128)}, u32[]{:S(2)}) copy-start(f32[3,1,2048]{2,1,0:T(1,128)} %get-tuple-element.17.lse_ref) | copy-start | bytes 73732
  169.5 28.5 %all-to-all-start.1 = ((bf16[8,3,64,256]{3,2,1,0:T(8,128)(2,1)}), bf16[8,3,64,256]{3,2,1,0:T(8,128)(2,1)S(1)}, u32[]{:S(2)}, u32[]{:S(2)}) async-start(bf16[8,3,64,256]{3,2,1,0:T(8,128)(2,1)} %bitcast.165), calls=%async_computation.1 | async-start | bytes 1572864 | tf_op jit(solution)/shard_map/all_to_all | solution.py:288
  173.1 126.8 %reduce-scatter.14.cloned.1.call-start = ((), (), s32[]{:S(2)}) async-start(), calls=%async_computation.17 | async-start | bytes 1327104 | tf_op jit(solution)/shard_map/reduce_scatter | solution.py:349
  201.2 20.4 %copy-start.3 = (f32[512,768]{1,0:T(8,128)}, f32[512,768]{1,0:T(8,128)S(1)}, u32[]{:S(2)}) copy-start(f32[512,768]{1,0:T(8,128)S(1)} %get-tuple-element.138) | copy-start | bytes 4718596
  209.0 9.5 %copy-start.15 = (bf16[768,3072]{1,0:T(8,128)(2,1)S(1)}, bf16[768,3072]{1,0:T(8,128)(2,1)}, u32[]{:S(2)}) copy-start(bf16[768,3072]{1,0:T(8,128)(2,1)} %all-gather.10.cloned.1.call-done) | copy-start | bytes 14155780
  221.5 15.5 %slice-start = ((s8[6291456]{0:T(1024)(128)(4,1)}), s8[4194304]{0:T(1024)(128)(4,1)S(1)}, s32[]{:S(2)}) async-start(s8[6291456]{0:T(1024)(128)(4,1)} %bitcast.174), calls=%async_computation.23 | async-start | bytes 8388608
  222.0 15.1 %slice-start.1 = ((s8[6291456]{0:T(1024)(128)(4,1)}), s8[2097152]{0:T(1024)(128)(4,1)S(1)}, s32[]{:S(2)}) async-start(s8[6291456]{0:T(1024)(128)(4,1)} %bitcast.174), calls=%async_computation.24 | async-start | bytes 4194304
  222.0 15.1 %copy-start.5 = (bf16[512,768]{1,0:T(8,128)(2,1)S(1)}, bf16[512,768]{1,0:T(8,128)(2,1)}, u32[]{:S(2)}) copy-start(bf16[512,768]{1,0:T(8,128)(2,1)} %param.16) | copy-start | bytes 2359300
  242.1 10.9 %copy-start = (f32[512,768]{1,0:T(8,128)}, f32[512,768]{1,0:T(8,128)S(1)}, u32[]{:S(2)}) copy-start(f32[512,768]{1,0:T(8,128)S(1)} %get-tuple-element.117) | copy-start | bytes 4718596
  244.0 186.3 %reduce-scatter.18.cloned.1.call-start = ((), (), s32[]{:S(2)}) async-start(), calls=%async_computation.19 | async-start | bytes 5308416 | tf_op jit(solution)/shard_map/reduce_scatter | solution.py:349
  296.1 45.6 %all-to-all-start.3 = ((bf16[8,3,3,64,256]{4,3,2,1,0:T(8,128)(2,1)}), bf16[8,3,3,64,256]{4,3,2,1,0:T(8,128)(2,1)S(1)}, u32[]{:S(2)}, u32[]{:S(2)}) async-start(bf16[8,3,3,64,256]{4,3,2,1,0:T(8,128)(2,1)} %bitcast.171), calls=%async_computation.3 | async-start | bytes 4718592 | tf_op jit(solution)/shard_map/all_to_all | solution.py:335
  299.7 144.8 %reduce-scatter.24.cloned.1.call-start = ((), (), s32[]{:S(2)}) async-start(), calls=%async_computation.22 | async-start | bytes 245760
  301.6 153.6 %reduce-scatter.12.cloned.1.call-start = ((), (), s32[]{:S(2)}) async-start(), calls=%async_computation.16 | async-start | bytes 3981312 | tf_op jit(solution)/shard_map/reduce_scatter | solution.py:349
  354.6 128.1 %reduce-scatter.16.cloned.1.call-start = ((), (), s32[]{:S(2)}) async-start(), calls=%async_computation.18 | async-start | bytes 737280 | tf_op jit(solution)/shard_map/reduce_scatter | solution.py:362
  425.0 77.3 %reduce-scatter.20.cloned.1.call-start = ((), (), s32[]{:S(2)}) async-start(), calls=%async_computation.20 | async-start | bytes 737280 | tf_op jit(solution)/shard_map/reduce_scatter | solution.py:362
  430.3 94.8 %reduce-scatter.22.cloned.1.call-start = ((), (), s32[]{:S(2)}) async-start(), calls=%async_computation.21 | async-start | bytes 737280
  436.6 42.2 %copy-start.1 = (f32[512,768]{1,0:T(8,128)S(1)}, f32[512,768]{1,0:T(8,128)}, u32[]{:S(2)}) copy-start(f32[512,768]{1,0:T(8,128)} %copy-done) | copy-start | bytes 4718596
  442.6 1.2 collective-permute-start
  443.8 3.7 collective-permute-start.1
  447.6 9.9 %collective-permute-start.2 = (f32[3081]{0:T(1024)S(1)}, f32[3081]{0:T(1024)S(1)}, u32[]{:S(2)}, u32[]{:S(2)}) collective-permute-start(f32[3081]{0:T(1024)S(1)} %add.240), channel_id=1, source_target_pairs={{0,4},{1,5},{2,6},{3,7},{4,0},{5,1},{6,2},{7,3},{8,12},{9,13},{10,... | collective-permute-start | bytes 36980 | tf_op jit(solution)/shard_map/ppermute | solution.py:376
  457.4 18.4 %collective-permute-start.3 = (f32[3081]{0:T(1024)S(1)}, f32[3081]{0:T(1024)S(1)}, u32[]{:S(2)}, u32[]{:S(2)}) collective-permute-start(f32[3081]{0:T(1024)S(1)} %add.241), channel_id=1, source_target_pairs={{0,8},{8,0},{16,24},{24,16},{1,9},{9,1},{17,25},{25,17},{2,10},{10... | collective-permute-start | bytes 36980 | tf_op jit(solution)/shard_map/ppermute | solution.py:376
  475.8 5.8 %collective-permute-start.4 = (f32[3081]{0:T(1024)S(1)}, f32[3081]{0:T(1024)S(1)}, u32[]{:S(2)}, u32[]{:S(2)}) collective-permute-start(f32[3081]{0:T(1024)S(1)} %add.242), channel_id=1, source_target_pairs={{0,16},{8,24},{16,0},{24,8},{1,17},{9,25},{17,1},{25,9},{2,18},{10... | collective-permute-start | bytes 36980 | tf_op jit(solution)/shard_map/ppermute | solution.py:376
  (11 other events, 27.1 us)
Sparse Core Ops, SparseCore 0:
  27.0 35.0 all-gather.5
  64.5 23.9 all-gather.7
  90.4 53.5 all-gather.9
  145.7 54.0 all-gather.11
  244.1 43.9 reduce-scatter.13
  291.4 72.9 reduce-scatter.17
  367.2 24.9 reduce-scatter.23
  395.7 59.5 reduce-scatter.11
  457.6 21.8 reduce-scatter.15
  481.6 20.6 reduce-scatter.19
  504.6 20.4 reduce-scatter.21
